TPU v7x, 32 devices: a whole 2x2x4 slice. The times are simulated.
32 devices in a mesh: range: 4 (over z), line: 4 (over y, x), freq: 2 (over core).
Axes of the slice: x: 2, y: 2, z: 4, core: 2. Of those that a mesh axis runs over, the one named last changes fastest.
Arguments:
- checkpoint: bfloat16 [4, 4, 1024, 2048], P('range', 'freq', None, 'line'), parts along dimension 1, may hold values from -6 to 6
- adjoint_start: bfloat16 [4, 4, 1024, 2048], P('range', 'freq', None, 'line'), parts along dimension 1, may hold values from -6 to 6
- misfit: bfloat16 [4, 4, 1024, 2048], P('range', 'freq', None, 'line'), parts along dimension 1, may hold values from -3 to 3
- pade_factors: bfloat16 [6, 4, 256, 256], P(None, 'freq'), parts along dimension 1, may hold values from -0.6 to 1.4
- azimuth_inverse: bfloat16 [4, 4, 256, 256], P('range', 'freq'), parts along dimension 1, may hold values from -0.6 to 1.4
- bottom: int32 [4, 1024], P('range'), may hold values from 512 to 2047
- base_speed: float32 [2048], P('line'), may hold values from 0.92 to 1.08
- speed_step: float32 [4, 2048], P('range', 'line'), may hold values from -0.012 to 0.012
Outputs:
- field_end: bfloat16 [4, 4, 1024, 2048], P('range', 'freq', None, 'line'), parts along dimension 1
- adjoint_begin: bfloat16 [4, 4, 1024, 2048], P('range', 'freq', None, 'line'), parts along dimension 1
- grad_increment: float32 [8, 2048], P(('freq', 'range'), 'line'), parts along dimension 0
There are 2 independent parts, one for each index of `freq`. A program takes and returns all parts, laid end to end along the dimension named above; an argument that names none is the same for every part. Nothing has to cross between parts.
All inputs are finite; a program needn't handle non-finite values.
Results may differ from a plain program's by a relative error of at most 0.0093.
Values may be sent and summed in bfloat16 or wider, within the bound.
No kernel may reach another device: no remote copies, remote signals or barrier semaphores. Data moves between devices by JAX's collectives and lax.ppermute only.
A program may use at most 64 MiB of HBM per device.

v0:
```python
import jax
import jax.numpy as jnp
from jax import lax
from jax.sharding import PartitionSpec as P
from jax.experimental import pallas as pl
from jax.experimental.pallas import tpu as pltpu

phase_scale = 4.0
bed_phase = -1.8
coupling = 0.3


def passed_along(value, axis, by):
    count = lax.axis_size(axis)
    pairs = [(i, i + by) for i in range(count) if 0 <= i + by < count]
    return lax.ppermute(value, axis, pairs)


def pair_terms(diag_one, diag_two, cross_one, cross_two, adjoint):
    if adjoint:
        return (diag_one + diag_two, cross_one - cross_two)
    return (diag_one - diag_two, cross_one + cross_two)


def depth_apply(current, pade_ops, adjoint):
    factor_count = pade_ops.shape[0]
    sequence = range(factor_count - 1, -1, -1) if adjoint else range(factor_count)
    for factor in sequence:
        contract = 1 if adjoint else 2
        product = lax.dot_general(
            current,
            pade_ops[factor],
            (((3,), (contract,)), ((), ())),
            preferred_element_type=jnp.float32,
        )
        real_part, imag_part = pair_terms(
            product[0, :, :, 0],
            product[1, :, :, 1],
            product[1, :, :, 0],
            product[0, :, :, 1],
            adjoint,
        )
        current = jnp.stack([real_part, imag_part]).astype(jnp.bfloat16)
    return current


def azimuth_apply(field_in, inverse, adjoint):
    block_width = inverse.shape[1]
    blocked = field_in.reshape(2, field_in.shape[1] // block_width, block_width, field_in.shape[2])
    contract = 1 if adjoint else 2
    product = lax.dot_general(
        inverse, blocked, (((contract,), (2,)), ((), ())), preferred_element_type=jnp.float32
    )
    real_part, imag_part = pair_terms(
        product[0, :, 0], product[1, :, 1], product[0, :, 1], product[1, :, 0], adjoint
    )
    joined = jnp.stack([real_part, imag_part])
    return joined.transpose(0, 2, 1, 3).reshape(field_in.shape)


def numerator_map(field_in):
    return field_in + coupling * (
        jnp.roll(field_in, 1, axis=1) + jnp.roll(field_in, -1, axis=1) - 2.0 * field_in
    )


def screen_phase(profile, bottom_row, depth_start):
    depths = depth_start + jnp.arange(profile.shape[0], dtype=jnp.int32)
    in_water = depths[None, :] < bottom_row[:, None]
    water_phase = phase_scale * (1.0 / (profile * profile) - 1.0)
    return (jnp.where(in_water, water_phase[None, :], bed_phase), in_water)


def depth_segment(field_in, pade_factors, adjoint):
    block_size = pade_factors.shape[3]
    if field_in.shape[2] % block_size == 0:
        worked = depth_apply(
            field_in.reshape(2, field_in.shape[1], field_in.shape[2] // block_size, block_size),
            pade_factors,
            adjoint,
        )
        return worked.reshape(field_in.shape)
    turned = lax.all_to_all(field_in, "line", split_axis=1, concat_axis=2, tiled=True)
    full_depth = turned.shape[2]
    worked = depth_apply(
        turned.reshape(2, turned.shape[1], full_depth // block_size, block_size),
        pade_factors,
        adjoint,
    )
    return lax.all_to_all(
        worked.reshape(turned.shape), "line", split_axis=2, concat_axis=1, tiled=True
    )


def general_local(
    checkpoint, adjoint_start, misfit, pade_factors, azimuth_inverse, bottom, base_speed, speed_step
):
    depth_rows = checkpoint.shape[3]
    depth_start = lax.axis_index("line") * depth_rows
    every_step = lax.all_gather(speed_step, "range", axis=0, tiled=True)
    running = jnp.cumsum(every_step, axis=0)
    profile = base_speed + lax.dynamic_index_in_dim(
        running, lax.axis_index("range"), 0, keepdims=False
    )
    phase_angle, in_water = screen_phase(profile, bottom[0], depth_start)
    cosine = jnp.cos(phase_angle)
    sine_term = jnp.sin(phase_angle)
    source = checkpoint[0].astype(jnp.float32)
    screened = jnp.stack(
        [cosine * source[0] - sine_term * source[1], sine_term * source[0] + cosine * source[1]]
    ).astype(jnp.bfloat16)
    depth_out = depth_segment(screened, pade_factors, False)
    numerator = numerator_map(depth_out.astype(jnp.float32)).astype(jnp.bfloat16)
    inverse = azimuth_inverse[0]
    field_end = azimuth_apply(numerator, inverse, False).astype(jnp.bfloat16)
    arrival = passed_along(adjoint_start, "range", -1)
    lam_end = (arrival[0].astype(jnp.float32) + misfit[0].astype(jnp.float32)).astype(jnp.bfloat16)
    backward = numerator_map(azimuth_apply(lam_end, inverse, True)).astype(jnp.bfloat16)
    backward = depth_segment(backward, pade_factors, True)
    cotangent = backward.astype(jnp.float32)
    adjoint_begin = jnp.stack(
        [
            cosine * cotangent[0] + sine_term * cotangent[1],
            cosine * cotangent[1] - sine_term * cotangent[0],
        ]
    ).astype(jnp.bfloat16)
    screened_f = screened.astype(jnp.float32)
    weight = jnp.where(in_water, cotangent[1] * screened_f[0] - cotangent[0] * screened_f[1], 0.0)
    grad_here = (
        jnp.sum(weight, axis=0) * (-8.0 / (profile * profile * profile)) / checkpoint.shape[2]
    )[None, :]
    all_grads = lax.all_gather(grad_here, "range", axis=0, tiled=True)
    suffix = jnp.flip(jnp.cumsum(jnp.flip(all_grads, 0), axis=0), 0)
    grad_increment = lax.dynamic_slice_in_dim(suffix, lax.axis_index("range"), 1, 0)
    return (field_end[None], adjoint_begin[None], grad_increment)


def dot_nt(left, right):
    return lax.dot_general(
        left, right, (((1,), (1,)), ((), ())), preferred_element_type=jnp.float32
    )


def dot_nn(left, right):
    return jnp.dot(left, right, preferred_element_type=jnp.float32)


def numerator_rows(field_in):
    rows = field_in.shape[0]
    return field_in + coupling * (
        pltpu.roll(field_in, 1, 0) + pltpu.roll(field_in, rows - 1, 0) - 2.0 * field_in
    )


def phase_tile(trig_ref, limit_ref, block_index, shape):
    columns = lax.broadcasted_iota(jnp.int32, shape, 1) + block_index * shape[1]
    in_water = columns < limit_ref[...]
    trig = trig_ref[...]
    cosine = jnp.where(in_water, trig[0:1], trig[2:3])
    sine_term = jnp.where(in_water, trig[1:2], trig[3:4])
    return cosine, sine_term, in_water


def screen_tile(source_ref, cosine, sine_term):
    source_r = source_ref[0].astype(jnp.float32)
    source_i = source_ref[1].astype(jnp.float32)
    screened_r = (cosine * source_r - sine_term * source_i).astype(jnp.bfloat16)
    screened_i = (sine_term * source_r + cosine * source_i).astype(jnp.bfloat16)
    return screened_r, screened_i


def forward_kernel(source_ref, trig_ref, limit_ref, pade_ref, inverse_ref, out_ref):
    block_index = pl.program_id(0)
    rows, width = source_ref.shape[1], source_ref.shape[2]
    cosine, sine_term, _ = phase_tile(trig_ref, limit_ref, block_index, (rows, width))
    cur_r, cur_i = screen_tile(source_ref, cosine, sine_term)
    for factor in range(pade_ref.shape[0]):
        pade_r = pade_ref[factor, 0]
        pade_i = pade_ref[factor, 1]
        real_part = dot_nt(cur_r, pade_r) - dot_nt(cur_i, pade_i)
        imag_part = dot_nt(cur_i, pade_r) + dot_nt(cur_r, pade_i)
        cur_r = real_part.astype(jnp.bfloat16)
        cur_i = imag_part.astype(jnp.bfloat16)
    num_r = numerator_rows(cur_r.astype(jnp.float32)).astype(jnp.bfloat16)
    num_i = numerator_rows(cur_i.astype(jnp.float32)).astype(jnp.bfloat16)
    inv_r = inverse_ref[0]
    inv_i = inverse_ref[1]
    block_width = inv_r.shape[0]
    for start in range(0, rows, block_width):
        part_r = num_r[start : start + block_width]
        part_i = num_i[start : start + block_width]
        out_ref[0, start : start + block_width, :] = (
            dot_nn(inv_r, part_r) - dot_nn(inv_i, part_i)
        ).astype(jnp.bfloat16)
        out_ref[1, start : start + block_width, :] = (
            dot_nn(inv_r, part_i) + dot_nn(inv_i, part_r)
        ).astype(jnp.bfloat16)


def make_backward_kernel(block_index):
    def backward_kernel(
        arrival_ref, misfit_ref, source_ref, trig_ref, limit_ref, pade_ref, inverse_t_ref,
        out_ref, grad_ref,
    ):
        rows, width = source_ref.shape[1], source_ref.shape[2]
        lam_r = (
            arrival_ref[0].astype(jnp.float32) + misfit_ref[0].astype(jnp.float32)
        ).astype(jnp.bfloat16)
        lam_i = (
            arrival_ref[1].astype(jnp.float32) + misfit_ref[1].astype(jnp.float32)
        ).astype(jnp.bfloat16)
        inv_r = inverse_t_ref[0]
        inv_i = inverse_t_ref[1]
        block_width = inv_r.shape[0]
        pieces_r = []
        pieces_i = []
        for start in range(0, rows, block_width):
            part_r = lam_r[start : start + block_width]
            part_i = lam_i[start : start + block_width]
            pieces_r.append(dot_nn(inv_r, part_r) + dot_nn(inv_i, part_i))
            pieces_i.append(dot_nn(inv_r, part_i) - dot_nn(inv_i, part_r))
        cur_r = numerator_rows(jnp.concatenate(pieces_r, axis=0)).astype(jnp.bfloat16)
        cur_i = numerator_rows(jnp.concatenate(pieces_i, axis=0)).astype(jnp.bfloat16)
        for factor in range(pade_ref.shape[0] - 1, -1, -1):
            pade_r = pade_ref[factor, 0]
            pade_i = pade_ref[factor, 1]
            real_part = dot_nn(cur_r, pade_r) + dot_nn(cur_i, pade_i)
            imag_part = dot_nn(cur_i, pade_r) - dot_nn(cur_r, pade_i)
            cur_r = real_part.astype(jnp.bfloat16)
            cur_i = imag_part.astype(jnp.bfloat16)
        cot_r = cur_r.astype(jnp.float32)
        cot_i = cur_i.astype(jnp.float32)
        cosine, sine_term, in_water = phase_tile(trig_ref, limit_ref, block_index, (rows, width))
        out_ref[0] = (cosine * cot_r + sine_term * cot_i).astype(jnp.bfloat16)
        out_ref[1] = (cosine * cot_i - sine_term * cot_r).astype(jnp.bfloat16)
        screened_r, screened_i = screen_tile(source_ref, cosine, sine_term)
        weight = jnp.where(
            in_water,
            cot_i * screened_r.astype(jnp.float32) - cot_r * screened_i.astype(jnp.float32),
            0.0,
        )
        grad_ref[...] = jnp.sum(weight, axis=0, keepdims=True)

    return backward_kernel


def lam_rows(arrival, misfit_part):
    return (arrival.astype(jnp.float32) + misfit_part.astype(jnp.float32)).astype(jnp.bfloat16)


def azimuth_adjoint(inv_r, inv_i, part_r, part_i):
    return (
        dot_nn(inv_r, part_r) + dot_nn(inv_i, part_i),
        dot_nn(inv_r, part_i) - dot_nn(inv_i, part_r),
    )


def depth_adjoint(cur_r, cur_i, pade_ref):
    for factor in range(pade_ref.shape[0] - 1, -1, -1):
        pade_r = pade_ref[factor, 0]
        pade_i = pade_ref[factor, 1]
        real_part = dot_nn(cur_r, pade_r) + dot_nn(cur_i, pade_i)
        imag_part = dot_nn(cur_i, pade_r) - dot_nn(cur_r, pade_i)
        cur_r = real_part.astype(jnp.bfloat16)
        cur_i = imag_part.astype(jnp.bfloat16)
    return cur_r.astype(jnp.float32), cur_i.astype(jnp.float32)


def finish_rows(cot_r, cot_i, trig_ref, limit_rows, source_r, source_i, block_index):
    shape = cot_r.shape
    columns = lax.broadcasted_iota(jnp.int32, shape, 1) + block_index * shape[1]
    in_water = columns < limit_rows
    trig = trig_ref[...]
    cosine = jnp.where(in_water, trig[0:1], trig[2:3])
    sine_term = jnp.where(in_water, trig[1:2], trig[3:4])
    out_r = cosine * cot_r + sine_term * cot_i
    out_i = cosine * cot_i - sine_term * cot_r
    screened_r = (cosine * source_r - sine_term * source_i).astype(jnp.bfloat16)
    screened_i = (sine_term * source_r + cosine * source_i).astype(jnp.bfloat16)
    weight = jnp.where(
        in_water,
        cot_i * screened_r.astype(jnp.float32) - cot_r * screened_i.astype(jnp.float32),
        0.0,
    )
    return out_r, out_i, jnp.sum(weight, axis=0, keepdims=True)


HALO = 8


def make_first_half_kernel(block_index):
    def kernel(
        arrival_ref, misfit_ref, source_ref, trig_ref, limit_ref, pade_ref, inverse_t_ref,
        begin_in, begin_out, grad_ref, stage_ref, copy_sem,
    ):
        half, width = arrival_ref.shape[1], arrival_ref.shape[2]
        lam_r = lam_rows(arrival_ref[0], misfit_ref[0])
        lam_i = lam_rows(arrival_ref[1], misfit_ref[1])
        inv_r = inverse_t_ref[0]
        inv_i = inverse_t_ref[1]
        block_width = inv_r.shape[0]
        pieces_r = []
        pieces_i = []
        for start in range(0, half, block_width):
            piece_r, piece_i = azimuth_adjoint(
                inv_r, inv_i, lam_r[start : start + block_width], lam_i[start : start + block_width]
            )
            pieces_r.append(piece_r)
            pieces_i.append(piece_i)
        num_r = numerator_rows(jnp.concatenate(pieces_r, axis=0))[HALO : half - HALO]
        num_i = numerator_rows(jnp.concatenate(pieces_i, axis=0))[HALO : half - HALO]
        cot_r, cot_i = depth_adjoint(
            num_r.astype(jnp.bfloat16), num_i.astype(jnp.bfloat16), pade_ref
        )
        source_r = source_ref[0].astype(jnp.float32)[HALO : half - HALO]
        source_i = source_ref[1].astype(jnp.float32)[HALO : half - HALO]
        out_r, out_i, grad_row = finish_rows(
            cot_r, cot_i, trig_ref, limit_ref[HALO : half - HALO], source_r, source_i, block_index
        )
        stage_ref[0] = out_r.astype(jnp.bfloat16)
        stage_ref[1] = out_i.astype(jnp.bfloat16)
        copy = pltpu.make_async_copy(
            stage_ref,
            begin_out.at[0, :, pl.ds(HALO, half - 2 * HALO), pl.ds(block_index * width, width)],
            copy_sem.at[0],
        )
        copy.start()
        grad_ref[...] = grad_row
        copy.wait()

    return kernel


def make_second_half_kernel(block_index):
    def kernel(
        first_ref, arrival_ref, misfit_ref, source_ref, trig_ref, limit_ref, pade_ref,
        inverse_t_ref, begin_in, begin_out, grad_ref, main_ref, wrap_ref, copy_sem,
    ):
        half, width = arrival_ref.shape[1], arrival_ref.shape[2]
        inv_r = inverse_t_ref[0]
        inv_i = inverse_t_ref[1]
        block_width = inv_r.shape[0]
        edge = 2 * HALO
        lam_r = lam_rows(arrival_ref[0], misfit_ref[0, half:])
        lam_i = lam_rows(arrival_ref[1], misfit_ref[1, half:])
        top_r = lam_rows(first_ref[0, half - block_width :], misfit_ref[0, half - block_width : half])
        top_i = lam_rows(first_ref[1, half - block_width :], misfit_ref[1, half - block_width : half])
        low_r = lam_rows(first_ref[0, :block_width], misfit_ref[0, :block_width])
        low_i = lam_rows(first_ref[1, :block_width], misfit_ref[1, :block_width])
        before_r, before_i = azimuth_adjoint(
            inverse_t_ref[0, block_width - edge :], inverse_t_ref[1, block_width - edge :],
            top_r, top_i,
        )
        after_r, after_i = azimuth_adjoint(
            inverse_t_ref[0, :edge], inverse_t_ref[1, :edge], low_r, low_i
        )
        pieces_r = [before_r]
        pieces_i = [before_i]
        for start in range(0, half, block_width):
            piece_r, piece_i = azimuth_adjoint(
                inv_r, inv_i, lam_r[start : start + block_width], lam_i[start : start + block_width]
            )
            pieces_r.append(piece_r)
            pieces_i.append(piece_i)
        pieces_r.append(after_r)
        pieces_i.append(after_i)
        span = half + 2 * HALO
        num_r = numerator_rows(jnp.concatenate(pieces_r, axis=0))[HALO : HALO + span]
        num_i = numerator_rows(jnp.concatenate(pieces_i, axis=0))[HALO : HALO + span]
        cot_r, cot_i = depth_adjoint(
            num_r.astype(jnp.bfloat16), num_i.astype(jnp.bfloat16), pade_ref
        )
        full_r = source_ref[0].astype(jnp.float32)
        full_i = source_ref[1].astype(jnp.float32)
        source_r = jnp.concatenate([full_r[half - HALO :], full_r[:HALO]], axis=0)
        source_i = jnp.concatenate([full_i[half - HALO :], full_i[:HALO]], axis=0)
        limit_rows = jnp.concatenate([limit_ref[half - HALO :], limit_ref[:HALO]], axis=0)
        out_r, out_i, grad_row = finish_rows(
            cot_r, cot_i, trig_ref, limit_rows, source_r, source_i, block_index
        )
        main_ref[0] = out_r[: half + HALO].astype(jnp.bfloat16)
        main_ref[1] = out_i[: half + HALO].astype(jnp.bfloat16)
        wrap_ref[0] = out_r[half + HALO :].astype(jnp.bfloat16)
        wrap_ref[1] = out_i[half + HALO :].astype(jnp.bfloat16)
        columns = pl.ds(block_index * width, width)
        main_copy = pltpu.make_async_copy(
            main_ref, begin_out.at[0, :, pl.ds(half - HALO, half + HALO), columns], copy_sem.at[0]
        )
        wrap_copy = pltpu.make_async_copy(
            wrap_ref, begin_out.at[0, :, pl.ds(0, HALO), columns], copy_sem.at[1]
        )
        main_copy.start()
        wrap_copy.start()
        grad_ref[...] = grad_row
        main_copy.wait()
        wrap_copy.wait()

    return kernel


def range_scan(value, direction):
    count = lax.axis_size("range")
    total = value
    for reach in range(1, count):
        total = total + passed_along(value, "range", direction * reach)
    return total


def fused_local(
    checkpoint, adjoint_start, misfit, pade_factors, azimuth_inverse, bottom, base_speed, speed_step
):
    depth_rows = checkpoint.shape[3]
    rows = checkpoint.shape[2]
    block_size = pade_factors.shape[3]
    block_count = depth_rows // block_size
    depth_start = lax.axis_index("line") * depth_rows
    half = rows // 2
    last = block_count - 1
    arrivals = [
        passed_along(
            adjoint_start[:, :, :, index * block_size : (index + 1) * block_size], "range", -1
        )
        for index in range(last)
    ]
    last_columns = adjoint_start[:, :, :, last * block_size :]
    first_half = passed_along(last_columns[:, :, :half], "range", -1)
    second_half = passed_along(last_columns[:, :, half:], "range", -1)
    halves = [first_half, second_half]
    profile = base_speed + range_scan(speed_step, 1)[0]
    water_phase = phase_scale * (1.0 / (profile * profile) - 1.0)
    bed_row = jnp.full_like(water_phase, bed_phase)
    trig = jnp.stack(
        [jnp.cos(water_phase), jnp.sin(water_phase), jnp.cos(bed_row), jnp.sin(bed_row)]
    )
    limit = (bottom[0] - depth_start)[:, None]
    inverse = azimuth_inverse[0]
    inverse_t = jnp.swapaxes(inverse, 1, 2)
    field_spec = pl.BlockSpec((None, 2, rows, block_size), lambda b: (0, 0, 0, b))
    trig_spec = pl.BlockSpec((4, block_size), lambda b: (0, b))
    limit_spec = pl.BlockSpec((rows, 1), lambda b: (0, 0))
    pade_spec = pl.BlockSpec(pade_factors.shape, lambda b: (0, 0, 0, 0))
    inverse_spec = pl.BlockSpec(inverse.shape, lambda b: (0, 0, 0))
    field_end = pl.pallas_call(
        forward_kernel,
        grid=(block_count,),
        in_specs=[field_spec, trig_spec, limit_spec, pade_spec, inverse_spec],
        out_specs=field_spec,
        out_shape=jax.ShapeDtypeStruct(checkpoint.shape, jnp.bfloat16),
    )(checkpoint, trig, limit, pade_factors, inverse)
    field_end, arrivals[0] = lax.optimization_barrier((field_end, arrivals[0]))
    adjoint_begin = None
    grads = []
    for index in range(last):
        fixed = lambda b, index=index: (0, 0, 0, index)
        chunk_spec = pl.BlockSpec((None, 2, rows, block_size), lambda b: (0, 0, 0, 0))
        block_spec = pl.BlockSpec((None, 2, rows, block_size), fixed)
        in_specs = [
            chunk_spec,
            block_spec,
            block_spec,
            pl.BlockSpec((4, block_size), lambda b, index=index: (0, index)),
            limit_spec,
            pade_spec,
            inverse_spec,
        ]
        operands = [arrivals[index], misfit, checkpoint, trig, limit, pade_factors, inverse_t]
        aliases = {}
        kernel = make_backward_kernel(index)
        if adjoint_begin is not None:
            in_specs.append(pl.BlockSpec(memory_space=pl.ANY))
            operands.append(adjoint_begin)
            aliases = {len(operands) - 1: 0}
            kernel = lambda *refs, kernel=kernel: kernel(*refs[:7], *refs[8:])
        adjoint_begin, grad_part = pl.pallas_call(
            kernel,
            grid=(1,),
            in_specs=in_specs,
            out_specs=[
                block_spec,
                pl.BlockSpec((1, block_size), lambda b: (0, 0)),
            ],
            out_shape=[
                jax.ShapeDtypeStruct(checkpoint.shape, jnp.bfloat16),
                jax.ShapeDtypeStruct((1, block_size), jnp.float32),
            ],
            input_output_aliases=aliases,
        )(*operands)
        grads.append(grad_part)
    any_spec = pl.BlockSpec(memory_space=pl.ANY)
    fixed_last = lambda b: (0, 0, 0, last)
    half_spec = pl.BlockSpec((None, 2, half, block_size), lambda b: (0, 0, 0, 0))
    trig_last = pl.BlockSpec((4, block_size), lambda b: (0, last))
    grad_spec = pl.BlockSpec((1, block_size), lambda b: (0, 0))
    begin_shape = jax.ShapeDtypeStruct(checkpoint.shape, jnp.bfloat16)
    grad_shape = jax.ShapeDtypeStruct((1, block_size), jnp.float32)
    adjoint_begin, grad_first = pl.pallas_call(
        make_first_half_kernel(last),
        grid=(1,),
        in_specs=[
            half_spec,
            pl.BlockSpec((None, 2, half, block_size), fixed_last),
            pl.BlockSpec((None, 2, half, block_size), fixed_last),
            trig_last,
            limit_spec,
            pade_spec,
            inverse_spec,
            any_spec,
        ],
        out_specs=[any_spec, grad_spec],
        out_shape=[begin_shape, grad_shape],
        scratch_shapes=[
            pltpu.VMEM((2, half - 2 * HALO, block_size), jnp.bfloat16),
            pltpu.SemaphoreType.DMA((1,)),
        ],
        input_output_aliases={7: 0},
    )(halves[0], misfit, checkpoint, trig, limit, pade_factors, inverse_t, adjoint_begin)
    full_last = pl.BlockSpec((None, 2, rows, block_size), fixed_last)
    adjoint_begin, grad_second = pl.pallas_call(
        make_second_half_kernel(last),
        grid=(1,),
        in_specs=[
            half_spec,
            half_spec,
            full_last,
            full_last,
            trig_last,
            limit_spec,
            pade_spec,
            inverse_spec,
            any_spec,
        ],
        out_specs=[any_spec, grad_spec],
        out_shape=[begin_shape, grad_shape],
        scratch_shapes=[
            pltpu.VMEM((2, half + HALO, block_size), jnp.bfloat16),
            pltpu.VMEM((2, HALO, block_size), jnp.bfloat16),
            pltpu.SemaphoreType.DMA((2,)),
        ],
        input_output_aliases={8: 0},
    )(
        halves[0], halves[1], misfit, checkpoint, trig, limit, pade_factors, inverse_t,
        adjoint_begin,
    )
    grads.append(grad_first + grad_second)
    grad_sum = jnp.concatenate(grads, axis=1)
    grad_here = grad_sum * (-8.0 / (profile * profile * profile)) / rows
    grad_increment = range_scan(grad_here, -1)
    return (field_end, adjoint_begin, grad_increment)


def local(
    checkpoint, adjoint_start, misfit, pade_factors, azimuth_inverse, bottom, base_speed, speed_step
):
    if (
        checkpoint.shape[3] % pade_factors.shape[3] == 0
        and checkpoint.shape[3] >= 2 * pade_factors.shape[3]
        and checkpoint.shape[2] % (2 * azimuth_inverse.shape[2]) == 0
    ):
        return fused_local(
            checkpoint, adjoint_start, misfit, pade_factors, azimuth_inverse, bottom,
            base_speed, speed_step,
        )
    return general_local(
        checkpoint, adjoint_start, misfit, pade_factors, azimuth_inverse, bottom,
        base_speed, speed_step,
    )


def solution(mesh):
    in_specs = (
        P("range", "freq", None, "line"),
        P("range", "freq", None, "line"),
        P("range", "freq", None, "line"),
        P(None, "freq", None, None),
        P("range", "freq", None, None),
        P("range", None),
        P("line"),
        P("range", "line"),
    )
    out_specs = (
        P("range", "freq", None, "line"),
        P("range", "freq", None, "line"),
        P(("freq", "range"), "line"),
    )
    return jax.shard_map(local, mesh=mesh, in_specs=in_specs, out_specs=out_specs, check_vma=False)
```

profile of v0, /device:TPU:0, one launch (start us, length us, event | category | flops | bytes accessed | tf_op | source)
XLA Modules:
  0.0 84.6 jit_solution(2514319893821710119)
XLA Ops:
  0.6 0.0 copy-start
  0.6 0.0 copy-start.6
  0.7 0.0 copy-start.2
  0.7 5.1 %collective-permute-start = (f32[1,512]{1,0:T(1,128)}, f32[1,512]{1,0:T(1,128)S(1)}, u32[]{:S(2)}, u32[]{:S(2)}) collective-permute-start(f32[1,512]{1,0:T(1,128)} %param.15), channel_id=1, source_target_pairs={{0,8},{8,16},{16,24},{1,9},{9,17},{17,25},{2,10},{10,18},{18,26},{... | collective-permute-start | bytes 6152 | tf_op jit(solution)/shard_map/ppermute | solution.py:16
  5.8 3.3 %collective-permute-start.2 = (f32[1,512]{1,0:T(1,128)}, f32[1,512]{1,0:T(1,128)S(1)}, u32[]{:S(2)}, u32[]{:S(2)}) collective-permute-start(f32[1,512]{1,0:T(1,128)} %param.15), channel_id=1, source_target_pairs={{0,24},{1,25},{2,26},{3,27},{4,28},{5,29},{6,30},{7,31}} | collective-permute-start | bytes 6152 | tf_op jit(solution)/shard_map/ppermute | solution.py:16
  9.1 1.8 %collective-permute-start.1 = (f32[1,512]{1,0:T(1,128)}, f32[1,512]{1,0:T(1,128)S(1)}, u32[]{:S(2)}, u32[]{:S(2)}) collective-permute-start(f32[1,512]{1,0:T(1,128)} %param.15), channel_id=1, source_target_pairs={{0,16},{8,24},{1,17},{9,25},{2,18},{10,26},{3,19},{11,27},{4,20},{... | collective-permute-start | bytes 6152 | tf_op jit(solution)/shard_map/ppermute | solution.py:16
  10.9 1.3 %slice.12 = bf16[1,2,1024,256]{3,2,1,0:T(8,128)(2,1)S(1)} slice(bf16[1,2,1024,512]{3,2,1,0:T(8,128)(2,1)} %param.9), slice={[0:1], [0:2], [0:1024], [0:256]} | slice | bytes 2097152 | tf_op jit(solution)/shard_map/slice | solution.py:421
  12.2 0.0 copy-start.7
  12.2 0.0 copy-start.5
  12.3 1.3 %collective-permute-start.3 = (bf16[1,2,1024,256]{3,2,1,0:T(8,128)(2,1)S(1)}, bf16[1,2,1024,256]{3,2,1,0:T(8,128)(2,1)S(1)}, u32[]{:S(2)}, u32[]{:S(2)}) collective-permute-start(bf16[1,2,1024,256]{3,2,1,0:T(8,128)(2,1)S(1)} %slice.12), channel_id=1, source_target_pairs={{8,0},{16,8},{24,16},{9,1},{17,9},{25,17},{10,2},{18,10},{26,18},{... | collective-permute-start | bytes 3145736 | tf_op jit(solution)/shard_map/ppermute | solution.py:16
  13.6 0.0 copy-done
  13.6 1.0 %fusion.5 = (bf16[1,2,512,256]{3,2,1,0:T(8,128)(2,1)}, bf16[1,2,512,256]{3,2,1,0:T(8,128)(2,1)}) fusion(bf16[1,2,1024,512]{3,2,1,0:T(8,128)(2,1)S(1)} %copy-done), kind=kLoop, calls=%fused_computation.11 | loop fusion | bytes 2097152 | tf_op jit(solution)/shard_map/slice | solution.py:427
  14.6 1.3 %collective-permute-start.5 = (bf16[1,2,512,256]{3,2,1,0:T(8,128)(2,1)}, bf16[1,2,512,256]{3,2,1,0:T(8,128)(2,1)S(1)}, u32[]{:S(2)}, u32[]{:S(2)}) collective-permute-start(bf16[1,2,512,256]{3,2,1,0:T(8,128)(2,1)} %get-tuple-element.21), channel_id=1, source_target_pairs={{8,0},{16,8},{24,16},{9,1},{17,9},{25,17},{10,2},{18,10},{26,18},{... | collective-permute-start | bytes 1572872 | tf_op jit(solution)/shard_map/ppermute | solution.py:16
  15.9 0.0 copy-done.6
  15.9 0.1 pad.4.clone
  16.0 0.1 pad.5.clone
  16.1 0.0 copy-done.2
  16.1 0.9 %copy.15 = bf16[1,2,256,256]{2,3,1,0:T(8,128)(2,1)} copy(bf16[1,2,256,256]{3,2,1,0:T(8,128)(2,1)S(1)} %copy-done.2) | data formatting | bytes 524288 | tf_op args[4]
  16.9 1.0 %copy.16.limit_ref = s32[1024,1]{1,0:T(8,128)} copy(s32[1024,1]{0,1:T(1,128)S(1)} %subtract_bitcast_fusion) | data formatting | bytes 8192 | tf_op jit(solution)/shard_map/sub | solution.py:435
  18.0 0.0 collective-permute-done
  18.0 1.3 %collective-permute-start.4 = (bf16[1,2,512,256]{3,2,1,0:T(8,128)(2,1)}, bf16[1,2,512,256]{3,2,1,0:T(8,128)(2,1)S(1)}, u32[]{:S(2)}, u32[]{:S(2)}) collective-permute-start(bf16[1,2,512,256]{3,2,1,0:T(8,128)(2,1)} %get-tuple-element.22), channel_id=1, source_target_pairs={{8,0},{16,8},{24,16},{9,1},{17,9},{25,17},{10,2},{18,10},{26,18},{... | collective-permute-start | bytes 1572872 | tf_op jit(solution)/shard_map/ppermute | solution.py:16
  19.3 0.0 collective-permute-done.2
  19.3 0.0 collective-permute-done.1
  19.3 0.0 copy-done.7
  19.3 0.0 copy-done.5
  19.4 0.7 maximum_maximum_fusion.trig_ref
  20.1 13.1 %shard_map.103 = bf16[1,2,1024,512]{3,2,1,0:T(8,128)(2,1)} custom-call(bf16[1,2,1024,512]{3,2,1,0:T(8,128)(2,1)} %source_ref.7, f32[4,512]{1,0:T(4,128)} %maximum_maximum_fusion.trig_ref, s32[1024,1]{1,0:T(8,128)} %copy.16.limit_ref, bf16[6,2,256,256]{3,2,1,0:T(8,128)(2,1)} %pade_ref.7, bf16[2,256,256]{2,1,0:T(8,128)(2,1)} %bitcast.17), custom_call_target="tpu_custom_call" | custom-call | tf_op jit(solution)/shard_map/pallas_call | solution.py:443
  33.2 7.0 %collective-permute-done.3.arrival_ref = bf16[1,2,1024,256]{3,2,1,0:T(8,128)(2,1)S(1)} collective-permute-done((bf16[1,2,1024,256]{3,2,1,0:T(8,128)(2,1)S(1)}, bf16[1,2,1024,256]{3,2,1,0:T(8,128)(2,1)S(1)}, u32[]{:S(2)}, u32[]{:S(2)}) %collective-permute-start.3) | collective-permute-done | bytes 1048608 | tf_op jit(solution)/shard_map/ppermute | solution.py:16
  40.2 0.0 copy-start.3
  40.2 1.0 %copy-done.3 = bf16[1,2,1024,256]{3,2,1,0:T(8,128)(2,1)} copy-done((bf16[1,2,1024,256]{3,2,1,0:T(8,128)(2,1)}, bf16[1,2,1024,256]{3,2,1,0:T(8,128)(2,1)S(1)}, u32[]{:S(2)}) %copy-start.3) | copy-done | bytes 1048600
  41.2 8.6 %shard_map.104 = (bf16[1,2,1024,512]{3,2,1,0:T(8,128)(2,1)}, f32[1,256]{1,0:T(1,128)}) custom-call(bf16[1,2,1024,256]{3,2,1,0:T(8,128)(2,1)} %copy-done.3, bf16[1,2,1024,512]{3,2,1,0:T(8,128)(2,1)} %misfit_ref.5, bf16[1,2,1024,512]{3,2,1,0:T(8,128)(2,1)} %source_ref.7, f32[4,512]{1,0:T(4,128)} %maximum_maximum_fusion.trig_ref, s32[1024,1]{1,0:T(8,128)} %copy.16.limit_ref, ...), custom_call_target="tpu_custom_call" | custom-call | tf_op jit(solution)/shard_map/pallas_call | solution.py:474
  49.8 11.2 %collective-permute-done.4.arrival_ref.first_ref = bf16[1,2,512,256]{3,2,1,0:T(8,128)(2,1)S(1)} collective-permute-done((bf16[1,2,512,256]{3,2,1,0:T(8,128)(2,1)}, bf16[1,2,512,256]{3,2,1,0:T(8,128)(2,1)S(1)}, u32[]{:S(2)}, u32[]{:S(2)}) %collective-permute-start.4) | collective-permute-done | bytes 524320 | tf_op jit(solution)/shard_map/ppermute | solution.py:16
  61.0 0.8 copy-done.1
  61.8 6.0 %shard_map.105 = (bf16[1,2,1024,512]{3,2,1,0:T(8,128)(2,1)}, f32[1,256]{1,0:T(1,128)}) custom-call(bf16[1,2,512,256]{3,2,1,0:T(8,128)(2,1)} %copy-done.1, bf16[1,2,1024,512]{3,2,1,0:T(8,128)(2,1)} %misfit_ref.5, bf16[1,2,1024,512]{3,2,1,0:T(8,128)(2,1)} %source_ref.7, f32[4,512]{1,0:T(4,128)} %maximum_maximum_fusion.trig_ref, ...), custom_call_target="tpu_custom_call", output_to_operand_aliasing={{0}: (7, {})} | custom-call | tf_op jit(solution)/shard_map/pallas_call | solution.py:496
  67.7 0.0 collective-permute-done.5.arrival_ref
  67.7 0.0 copy-start.4
  67.8 0.8 copy-done.4
  68.5 6.7 %shard_map.106 = (bf16[1,2,1024,512]{3,2,1,0:T(8,128)(2,1)}, f32[1,256]{1,0:T(1,128)}) custom-call(bf16[1,2,512,256]{3,2,1,0:T(8,128)(2,1)} %copy-done.1, bf16[1,2,512,256]{3,2,1,0:T(8,128)(2,1)} %copy-done.4, bf16[1,2,1024,512]{3,2,1,0:T(8,128)(2,1)} %misfit_ref.5, bf16[1,2,1024,512]{3,2,1,0:T(8,128)(2,1)} %source_ref.7, ...), custom_call_target="tpu_custom_call", output_to_operand_aliasing={{0}: (8, {})} | custom-call | tf_op jit(solution)/shard_map/pallas_call | solution.py:518
  75.3 0.0 copy-done.8
  75.3 0.7 add.29
  76.0 0.0 copy-done.9
  76.0 1.3 %collective-permute-start.8 = (f32[1,512]{1,0:T(1,128)S(1)}, f32[1,512]{1,0:T(1,128)S(1)}, u32[]{:S(2)}, u32[]{:S(2)}) collective-permute-start(f32[1,512]{1,0:T(1,128)S(1)} %bitcast.20), channel_id=1, source_target_pairs={{24,0},{25,1},{26,2},{27,3},{28,4},{29,5},{30,6},{31,7}} | collective-permute-start | bytes 6152 | tf_op jit(solution)/shard_map/ppermute | solution.py:16
  77.3 1.3 %collective-permute-start.7 = (f32[1,512]{1,0:T(1,128)S(1)}, f32[1,512]{1,0:T(1,128)S(1)}, u32[]{:S(2)}, u32[]{:S(2)}) collective-permute-start(f32[1,512]{1,0:T(1,128)S(1)} %bitcast.21), channel_id=1, source_target_pairs={{16,0},{24,8},{17,1},{25,9},{18,2},{26,10},{19,3},{27,11},{20,4},{... | collective-permute-start | bytes 6152 | tf_op jit(solution)/shard_map/ppermute | solution.py:16
  78.6 1.3 %collective-permute-start.6 = (f32[1,512]{1,0:T(1,128)S(1)}, f32[1,512]{1,0:T(1,128)S(1)}, u32[]{:S(2)}, u32[]{:S(2)}) collective-permute-start(f32[1,512]{1,0:T(1,128)S(1)} %bitcast.22), channel_id=1, source_target_pairs={{8,0},{16,8},{24,16},{9,1},{17,9},{25,17},{10,2},{18,10},{26,18},{... | collective-permute-start | bytes 6152 | tf_op jit(solution)/shard_map/ppermute | solution.py:16
  79.9 3.4 %collective-permute-done.8 = f32[1,512]{1,0:T(1,128)S(1)} collective-permute-done((f32[1,512]{1,0:T(1,128)S(1)}, f32[1,512]{1,0:T(1,128)S(1)}, u32[]{:S(2)}, u32[]{:S(2)}) %collective-permute-start.8) | collective-permute-done | bytes 2080 | tf_op jit(solution)/shard_map/ppermute | solution.py:16
  83.3 0.4 collective-permute-done.7
  83.7 0.4 collective-permute-done.6
  84.1 0.6 add_add_fusion
  (8 shorter events, 0.1 us)
Async XLA Ops:
  0.6 12.9 %copy-start = (bf16[1,2,1024,512]{3,2,1,0:T(8,128)(2,1)S(1)}, bf16[1,2,1024,512]{3,2,1,0:T(8,128)(2,1)}, u32[]{:S(2)}) copy-start(bf16[1,2,1024,512]{3,2,1,0:T(8,128)(2,1)} %param.9) | copy-start | bytes 6291460
  0.6 15.3 %copy-start.6 = (s32[1,1024]{1,0:T(1,128)S(1)}, s32[1,1024]{1,0:T(1,128)}, u32[]{:S(2)}) copy-start(s32[1,1024]{1,0:T(1,128)} %param.13) | copy-start | bytes 12292
  0.7 15.4 %copy-start.2 = (bf16[1,2,256,256]{3,2,1,0:T(8,128)(2,1)S(1)}, bf16[1,2,256,256]{3,2,1,0:T(8,128)(2,1)}, u32[]{:S(2)}) copy-start(bf16[1,2,256,256]{3,2,1,0:T(8,128)(2,1)} %param.12) | copy-start | bytes 786436
  0.7 17.3 %collective-permute-start = (f32[1,512]{1,0:T(1,128)}, f32[1,512]{1,0:T(1,128)S(1)}, u32[]{:S(2)}, u32[]{:S(2)}) collective-permute-start(f32[1,512]{1,0:T(1,128)} %param.15), channel_id=1, source_target_pairs={{0,8},{8,16},{16,24},{1,9},{9,17},{17,25},{2,10},{10,18},{18,26},{... | collective-permute-start | bytes 6152 | tf_op jit(solution)/shard_map/ppermute | solution.py:16
  5.8 13.5 %collective-permute-start.2 = (f32[1,512]{1,0:T(1,128)}, f32[1,512]{1,0:T(1,128)S(1)}, u32[]{:S(2)}, u32[]{:S(2)}) collective-permute-start(f32[1,512]{1,0:T(1,128)} %param.15), channel_id=1, source_target_pairs={{0,24},{1,25},{2,26},{3,27},{4,28},{5,29},{6,30},{7,31}} | collective-permute-start | bytes 6152 | tf_op jit(solution)/shard_map/ppermute | solution.py:16
  9.1 10.2 %collective-permute-start.1 = (f32[1,512]{1,0:T(1,128)}, f32[1,512]{1,0:T(1,128)S(1)}, u32[]{:S(2)}, u32[]{:S(2)}) collective-permute-start(f32[1,512]{1,0:T(1,128)} %param.15), channel_id=1, source_target_pairs={{0,16},{8,24},{1,17},{9,25},{2,18},{10,26},{3,19},{11,27},{4,20},{... | collective-permute-start | bytes 6152 | tf_op jit(solution)/shard_map/ppermute | solution.py:16
  12.2 7.0 %copy-start.7 = (f32[1,512]{1,0:T(1,128)S(1)}, f32[1,512]{1,0:T(1,128)}, u32[]{:S(2)}) copy-start(f32[1,512]{1,0:T(1,128)} %param.15) | copy-start | bytes 6148
  12.2 7.1 %copy-start.5 = (f32[512]{0:T(512)S(1)}, f32[512]{0:T(512)}, u32[]{:S(2)}) copy-start(f32[512]{0:T(512)} %param.14) | copy-start | bytes 6148
  12.3 27.9 %collective-permute-start.3 = (bf16[1,2,1024,256]{3,2,1,0:T(8,128)(2,1)S(1)}, bf16[1,2,1024,256]{3,2,1,0:T(8,128)(2,1)S(1)}, u32[]{:S(2)}, u32[]{:S(2)}) collective-permute-start(bf16[1,2,1024,256]{3,2,1,0:T(8,128)(2,1)S(1)} %slice.12), channel_id=1, source_target_pairs={{8,0},{16,8},{24,16},{9,1},{17,9},{25,17},{10,2},{18,10},{26,18},{... | collective-permute-start | bytes 3145736 | tf_op jit(solution)/shard_map/ppermute | solution.py:16
  14.6 53.1 %collective-permute-start.5 = (bf16[1,2,512,256]{3,2,1,0:T(8,128)(2,1)}, bf16[1,2,512,256]{3,2,1,0:T(8,128)(2,1)S(1)}, u32[]{:S(2)}, u32[]{:S(2)}) collective-permute-start(bf16[1,2,512,256]{3,2,1,0:T(8,128)(2,1)} %get-tuple-element.21), channel_id=1, source_target_pairs={{8,0},{16,8},{24,16},{9,1},{17,9},{25,17},{10,2},{18,10},{26,18},{... | collective-permute-start | bytes 1572872 | tf_op jit(solution)/shard_map/ppermute | solution.py:16
  18.0 43.0 %collective-permute-start.4 = (bf16[1,2,512,256]{3,2,1,0:T(8,128)(2,1)}, bf16[1,2,512,256]{3,2,1,0:T(8,128)(2,1)S(1)}, u32[]{:S(2)}, u32[]{:S(2)}) collective-permute-start(bf16[1,2,512,256]{3,2,1,0:T(8,128)(2,1)} %get-tuple-element.22), channel_id=1, source_target_pairs={{8,0},{16,8},{24,16},{9,1},{17,9},{25,17},{10,2},{18,10},{26,18},{... | collective-permute-start | bytes 1572872 | tf_op jit(solution)/shard_map/ppermute | solution.py:16
  40.2 1.0 %copy-start.3 = (bf16[1,2,1024,256]{3,2,1,0:T(8,128)(2,1)}, bf16[1,2,1024,256]{3,2,1,0:T(8,128)(2,1)S(1)}, u32[]{:S(2)}) copy-start(bf16[1,2,1024,256]{3,2,1,0:T(8,128)(2,1)S(1)} %collective-permute-done.3.arrival_ref) | copy-start | bytes 3145732
  61.0 0.8 copy-start.1
  67.7 0.8 copy-start.4
  68.5 6.7 %copy-start.8 = (f32[1,256]{1,0:T(1,128)S(1)}, f32[1,256]{1,0:T(1,128)}, u32[]{:S(2)}) copy-start(f32[1,256]{1,0:T(1,128)} %get-tuple-element.17) | copy-start | bytes 3076
  68.5 7.4 %copy-start.9 = (f32[1,256]{1,0:T(1,128)S(1)}, f32[1,256]{1,0:T(1,128)}, u32[]{:S(2)}) copy-start(f32[1,256]{1,0:T(1,128)} %get-tuple-element.16) | copy-start | bytes 3076
  76.0 7.3 %collective-permute-start.8 = (f32[1,512]{1,0:T(1,128)S(1)}, f32[1,512]{1,0:T(1,128)S(1)}, u32[]{:S(2)}, u32[]{:S(2)}) collective-permute-start(f32[1,512]{1,0:T(1,128)S(1)} %bitcast.20), channel_id=1, source_target_pairs={{24,0},{25,1},{26,2},{27,3},{28,4},{29,5},{30,6},{31,7}} | collective-permute-start | bytes 6152 | tf_op jit(solution)/shard_map/ppermute | solution.py:16
  77.3 6.4 %collective-permute-start.7 = (f32[1,512]{1,0:T(1,128)S(1)}, f32[1,512]{1,0:T(1,128)S(1)}, u32[]{:S(2)}, u32[]{:S(2)}) collective-permute-start(f32[1,512]{1,0:T(1,128)S(1)} %bitcast.21), channel_id=1, source_target_pairs={{16,0},{24,8},{17,1},{25,9},{18,2},{26,10},{19,3},{27,11},{20,4},{... | collective-permute-start | bytes 6152 | tf_op jit(solution)/shard_map/ppermute | solution.py:16
  78.6 5.5 %collective-permute-start.6 = (f32[1,512]{1,0:T(1,128)S(1)}, f32[1,512]{1,0:T(1,128)S(1)}, u32[]{:S(2)}, u32[]{:S(2)}) collective-permute-start(f32[1,512]{1,0:T(1,128)S(1)} %bitcast.22), channel_id=1, source_target_pairs={{8,0},{16,8},{24,16},{9,1},{17,9},{25,17},{10,2},{18,10},{26,18},{... | collective-permute-start | bytes 6152 | tf_op jit(solution)/shard_map/ppermute | solution.py:16
where the time goes:
time: 85 us; the launch traced here: 84.6 us
  Pallas kernels  34.4 us (40%)
  waiting for transfers between devices  22.3 us (26%)
  starting transfers between devices  18 us (21%)
  local copies, waits for them, and re-layouts  7.02 us (8%)
  other arithmetic  2.01 us (2%)
  between operations  0.88 us (1%)
    ppermute x9, waiting for transfers between devices, passed_along(): return lax.ppermute(value, axis, pairs)  22.3 us
    ppermute x9, starting transfers between devices, passed_along(): return lax.ppermute(value, axis, pairs)  18 us
    pallas_call x1, Pallas kernels, fused_local(): pl.pallas_call(forward_kernel, grid=(block_count,), in_specs=[field_spec,...  13.1 us
    pallas_call x1, Pallas kernels, fused_local(): pl.pallas_call(kernel, grid=(1,), in_specs=in_specs, out_specs=[block_spe...  8.61 us
    pallas_call x1, Pallas kernels, fused_local(): pl.pallas_call(make_second_half_kernel(last), grid=(1,), in_specs=[half_s...  6.72 us
    pallas_call x1, Pallas kernels, fused_local(): pl.pallas_call(make_first_half_kernel(last), grid=(1,), in_specs=[half_sp...  5.96 us
    unnamed x21, local copies, waits for them, and re-layouts  3.47 us
  transfers between devices with their start and end apart: 9, of which 5 were waited for; matrix products, arithmetic and copies ran while one was open for 6% of the time, Pallas kernels for 33%

commit v1 on v0

--- a/solution.py
+++ b/solution.py
@@ -334,9 +334,11 @@
 def make_second_half_kernel(block_index):
     def kernel(
         first_ref, arrival_ref, misfit_ref, source_ref, trig_ref, limit_ref, pade_ref,
-        inverse_t_ref, begin_in, begin_out, grad_ref, main_ref, wrap_ref, copy_sem,
+        inverse_t_ref, begin_in, whole_grad_ref, first_grad_ref, scale_ref,
+        begin_out, grad_ref, main_ref, wrap_ref, copy_sem,
     ):
         half, width = arrival_ref.shape[1], arrival_ref.shape[2]
+        rows = 2 * half
         inv_r = inverse_t_ref[0]
         inv_i = inverse_t_ref[1]
         block_width = inv_r.shape[0]
@@ -391,7 +393,13 @@
         )
         main_copy.start()
         wrap_copy.start()
-        grad_ref[...] = grad_row
+        scale = scale_ref[...]
+        grad_ref[:, : block_index * width] = (
+            whole_grad_ref[...] * scale[:, : block_index * width] / rows
+        )
+        grad_ref[:, block_index * width :] = (
+            (first_grad_ref[...] + grad_row) * scale[:, block_index * width :] / rows
+        )
         main_copy.wait()
         wrap_copy.wait()
 
@@ -515,7 +523,9 @@
         input_output_aliases={7: 0},
     )(halves[0], misfit, checkpoint, trig, limit, pade_factors, inverse_t, adjoint_begin)
     full_last = pl.BlockSpec((None, 2, rows, block_size), fixed_last)
-    adjoint_begin, grad_second = pl.pallas_call(
+    scale = (-8.0 / (profile * profile * profile))[None, :]
+    whole_row = pl.BlockSpec((1, depth_rows), lambda b: (0, 0))
+    adjoint_begin, grad_here = pl.pallas_call(
         make_second_half_kernel(last),
         grid=(1,),
         in_specs=[
@@ -528,9 +538,12 @@
             pade_spec,
             inverse_spec,
             any_spec,
+            pl.BlockSpec((1, last * block_size), lambda b: (0, 0)),
+            grad_spec,
+            whole_row,
         ],
-        out_specs=[any_spec, grad_spec],
-        out_shape=[begin_shape, grad_shape],
+        out_specs=[any_spec, whole_row],
+        out_shape=[begin_shape, jax.ShapeDtypeStruct((1, depth_rows), jnp.float32)],
         scratch_shapes=[
             pltpu.VMEM((2, half + HALO, block_size), jnp.bfloat16),
             pltpu.VMEM((2, HALO, block_size), jnp.bfloat16),
@@ -539,11 +552,8 @@
         input_output_aliases={8: 0},
     )(
         halves[0], halves[1], misfit, checkpoint, trig, limit, pade_factors, inverse_t,
-        adjoint_begin,
-    )
-    grads.append(grad_first + grad_second)
-    grad_sum = jnp.concatenate(grads, axis=1)
-    grad_here = grad_sum * (-8.0 / (profile * profile * profile)) / rows
+        adjoint_begin, grads[0], grad_first, scale,
+    )
     grad_increment = range_scan(grad_here, -1)
     return (field_end, adjoint_begin, grad_increment)
 

time: 85 us -> 85.3 us (level)
    unnamed x21 -> x17, local copies, waits for them, and re-layouts: 3.47 us -> 3.45 us
  transfers between devices with their start and end apart: 9 -> 9, of which waited for: 5 -> 5; matrix products, arithmetic and copies ran while one was open for 6% -> 7% of each run, Pallas kernels for 33% -> 33%
where the time goes in v1:
time: 85.3 us; the launch traced here: 84.9 us
  Pallas kernels  34.5 us (40%)
  waiting for transfers between devices  22 us (26%)
  starting transfers between devices  18 us (21%)
  local copies, waits for them, and re-layouts  7.01 us (8%)
  other arithmetic  2.52 us (3%)
  between operations  0.86 us (1%)
    ppermute x9, waiting for transfers between devices, passed_along(): return lax.ppermute(value, axis, pairs)  22 us
    ppermute x9, starting transfers between devices, passed_along(): return lax.ppermute(value, axis, pairs)  18 us
    pallas_call x1, Pallas kernels, fused_local(): pl.pallas_call(forward_kernel, grid=(block_count,), in_specs=[field_spec,...  13.1 us
    pallas_call x1, Pallas kernels, fused_local(): pl.pallas_call(kernel, grid=(1,), in_specs=in_specs, out_specs=[block_spe...  8.61 us
    pallas_call x1, Pallas kernels, fused_local(): pl.pallas_call(make_second_half_kernel(last), grid=(1,), in_specs=[half_s...  6.78 us
    pallas_call x1, Pallas kernels, fused_local(): pl.pallas_call(make_first_half_kernel(last), grid=(1,), in_specs=[half_sp...  5.97 us
    unnamed x17, local copies, waits for them, and re-layouts  3.45 us
  transfers between devices with their start and end apart: 9, of which 5 were waited for; matrix products, arithmetic and copies ran while one was open for 7% of the time, Pallas kernels for 33%

profile of v1, /device:TPU:0, one launch (start us, length us, event | category | flops | bytes accessed | tf_op | source)
XLA Modules:
  0.0 84.9 jit_solution(5512059976594246467)
XLA Ops:
  0.6 0.0 copy-start
  0.6 0.0 copy-start.5
  0.7 0.0 copy-start.2
  0.7 5.1 %collective-permute-start = (f32[1,512]{1,0:T(1,128)}, f32[1,512]{1,0:T(1,128)S(1)}, u32[]{:S(2)}, u32[]{:S(2)}) collective-permute-start(f32[1,512]{1,0:T(1,128)} %param.15), channel_id=1, source_target_pairs={{0,8},{8,16},{16,24},{1,9},{9,17},{17,25},{2,10},{10,18},{18,26},{... | collective-permute-start | bytes 6152 | tf_op jit(solution)/shard_map/ppermute | solution.py:16
  5.8 3.3 %collective-permute-start.2 = (f32[1,512]{1,0:T(1,128)}, f32[1,512]{1,0:T(1,128)S(1)}, u32[]{:S(2)}, u32[]{:S(2)}) collective-permute-start(f32[1,512]{1,0:T(1,128)} %param.15), channel_id=1, source_target_pairs={{0,24},{1,25},{2,26},{3,27},{4,28},{5,29},{6,30},{7,31}} | collective-permute-start | bytes 6152 | tf_op jit(solution)/shard_map/ppermute | solution.py:16
  9.1 1.8 %collective-permute-start.1 = (f32[1,512]{1,0:T(1,128)}, f32[1,512]{1,0:T(1,128)S(1)}, u32[]{:S(2)}, u32[]{:S(2)}) collective-permute-start(f32[1,512]{1,0:T(1,128)} %param.15), channel_id=1, source_target_pairs={{0,16},{8,24},{1,17},{9,25},{2,18},{10,26},{3,19},{11,27},{4,20},{... | collective-permute-start | bytes 6152 | tf_op jit(solution)/shard_map/ppermute | solution.py:16
  10.9 1.3 %slice.12 = bf16[1,2,1024,256]{3,2,1,0:T(8,128)(2,1)S(1)} slice(bf16[1,2,1024,512]{3,2,1,0:T(8,128)(2,1)} %param.9), slice={[0:1], [0:2], [0:1024], [0:256]} | slice | bytes 2097152 | tf_op jit(solution)/shard_map/slice | solution.py:429
  12.2 0.0 copy-start.6
  12.2 0.0 copy-start.7
  12.3 1.3 %collective-permute-start.3 = (bf16[1,2,1024,256]{3,2,1,0:T(8,128)(2,1)S(1)}, bf16[1,2,1024,256]{3,2,1,0:T(8,128)(2,1)S(1)}, u32[]{:S(2)}, u32[]{:S(2)}) collective-permute-start(bf16[1,2,1024,256]{3,2,1,0:T(8,128)(2,1)S(1)} %slice.12), channel_id=1, source_target_pairs={{8,0},{16,8},{24,16},{9,1},{17,9},{25,17},{10,2},{18,10},{26,18},{... | collective-permute-start | bytes 3145736 | tf_op jit(solution)/shard_map/ppermute | solution.py:16
  13.6 0.0 copy-done
  13.6 1.0 %fusion.5 = (bf16[1,2,512,256]{3,2,1,0:T(8,128)(2,1)}, bf16[1,2,512,256]{3,2,1,0:T(8,128)(2,1)}) fusion(bf16[1,2,1024,512]{3,2,1,0:T(8,128)(2,1)S(1)} %copy-done), kind=kLoop, calls=%fused_computation.10 | loop fusion | bytes 2097152 | tf_op jit(solution)/shard_map/slice | solution.py:435
  14.6 1.3 %collective-permute-start.5 = (bf16[1,2,512,256]{3,2,1,0:T(8,128)(2,1)}, bf16[1,2,512,256]{3,2,1,0:T(8,128)(2,1)S(1)}, u32[]{:S(2)}, u32[]{:S(2)}) collective-permute-start(bf16[1,2,512,256]{3,2,1,0:T(8,128)(2,1)} %get-tuple-element.21), channel_id=1, source_target_pairs={{8,0},{16,8},{24,16},{9,1},{17,9},{25,17},{10,2},{18,10},{26,18},{... | collective-permute-start | bytes 1572872 | tf_op jit(solution)/shard_map/ppermute | solution.py:16
  15.9 0.0 copy-done.5
  15.9 0.1 pad.2.clone
  16.0 0.1 pad.3.clone
  16.1 0.0 copy-done.2
  16.1 0.8 copy.15
  16.9 1.0 %copy.16.limit_ref = s32[1024,1]{1,0:T(8,128)} copy(s32[1024,1]{0,1:T(1,128)S(1)} %subtract_bitcast_fusion) | data formatting | bytes 8192 | tf_op jit(solution)/shard_map/sub | solution.py:443
  18.0 0.0 collective-permute-done
  18.0 1.3 %collective-permute-start.4 = (bf16[1,2,512,256]{3,2,1,0:T(8,128)(2,1)}, bf16[1,2,512,256]{3,2,1,0:T(8,128)(2,1)S(1)}, u32[]{:S(2)}, u32[]{:S(2)}) collective-permute-start(bf16[1,2,512,256]{3,2,1,0:T(8,128)(2,1)} %get-tuple-element.22), channel_id=1, source_target_pairs={{8,0},{16,8},{24,16},{9,1},{17,9},{25,17},{10,2},{18,10},{26,18},{... | collective-permute-start | bytes 1572872 | tf_op jit(solution)/shard_map/ppermute | solution.py:16
  19.3 0.0 collective-permute-done.2
  19.3 0.0 collective-permute-done.1
  19.3 0.0 copy-done.6
  19.3 0.0 copy-done.7
  19.3 0.6 fusion.3
  19.9 0.7 maximum_maximum_fusion.trig_ref
  20.6 13.1 %shard_map.103 = bf16[1,2,1024,512]{3,2,1,0:T(8,128)(2,1)} custom-call(bf16[1,2,1024,512]{3,2,1,0:T(8,128)(2,1)} %source_ref.7, f32[4,512]{1,0:T(4,128)} %maximum_maximum_fusion.trig_ref, s32[1024,1]{1,0:T(8,128)} %copy.16.limit_ref, bf16[6,2,256,256]{3,2,1,0:T(8,128)(2,1)} %pade_ref.7, bf16[2,256,256]{2,1,0:T(8,128)(2,1)} %bitcast.15), custom_call_target="tpu_custom_call" | custom-call | tf_op jit(solution)/shard_map/pallas_call | solution.py:451
  33.7 6.5 %collective-permute-done.3.arrival_ref = bf16[1,2,1024,256]{3,2,1,0:T(8,128)(2,1)S(1)} collective-permute-done((bf16[1,2,1024,256]{3,2,1,0:T(8,128)(2,1)S(1)}, bf16[1,2,1024,256]{3,2,1,0:T(8,128)(2,1)S(1)}, u32[]{:S(2)}, u32[]{:S(2)}) %collective-permute-start.3) | collective-permute-done | bytes 1048608 | tf_op jit(solution)/shard_map/ppermute | solution.py:16
  40.2 0.0 copy-start.3
  40.2 1.0 %copy-done.3 = bf16[1,2,1024,256]{3,2,1,0:T(8,128)(2,1)} copy-done((bf16[1,2,1024,256]{3,2,1,0:T(8,128)(2,1)}, bf16[1,2,1024,256]{3,2,1,0:T(8,128)(2,1)S(1)}, u32[]{:S(2)}) %copy-start.3) | copy-done | bytes 1048600
  41.2 8.6 %shard_map.104 = (bf16[1,2,1024,512]{3,2,1,0:T(8,128)(2,1)}, f32[1,256]{1,0:T(1,128)}) custom-call(bf16[1,2,1024,256]{3,2,1,0:T(8,128)(2,1)} %copy-done.3, bf16[1,2,1024,512]{3,2,1,0:T(8,128)(2,1)} %misfit_ref.5, bf16[1,2,1024,512]{3,2,1,0:T(8,128)(2,1)} %source_ref.7, f32[4,512]{1,0:T(4,128)} %maximum_maximum_fusion.trig_ref, s32[1024,1]{1,0:T(8,128)} %copy.16.limit_ref, ...), custom_call_target="tpu_custom_call" | custom-call | tf_op jit(solution)/shard_map/pallas_call | solution.py:482
  49.8 11.2 %collective-permute-done.4.arrival_ref.first_ref = bf16[1,2,512,256]{3,2,1,0:T(8,128)(2,1)S(1)} collective-permute-done((bf16[1,2,512,256]{3,2,1,0:T(8,128)(2,1)}, bf16[1,2,512,256]{3,2,1,0:T(8,128)(2,1)S(1)}, u32[]{:S(2)}, u32[]{:S(2)}) %collective-permute-start.4) | collective-permute-done | bytes 524320 | tf_op jit(solution)/shard_map/ppermute | solution.py:16
  61.0 0.0 copy-start.1
  61.0 0.8 copy-done.1
  61.8 6.0 %shard_map.105 = (bf16[1,2,1024,512]{3,2,1,0:T(8,128)(2,1)}, f32[1,256]{1,0:T(1,128)}) custom-call(bf16[1,2,512,256]{3,2,1,0:T(8,128)(2,1)} %copy-done.1, bf16[1,2,1024,512]{3,2,1,0:T(8,128)(2,1)} %misfit_ref.5, bf16[1,2,1024,512]{3,2,1,0:T(8,128)(2,1)} %source_ref.7, f32[4,512]{1,0:T(4,128)} %maximum_maximum_fusion.trig_ref, ...), custom_call_target="tpu_custom_call", output_to_operand_aliasing={{0}: (7, {})} | custom-call | tf_op jit(solution)/shard_map/pallas_call | solution.py:504
  67.7 0.0 collective-permute-done.5.arrival_ref
  67.8 0.0 copy-start.4
  67.8 0.8 copy-done.4
  68.5 6.8 %shard_map.106 = (bf16[1,2,1024,512]{3,2,1,0:T(8,128)(2,1)}, f32[1,512]{1,0:T(1,128)}) custom-call(bf16[1,2,512,256]{3,2,1,0:T(8,128)(2,1)} %copy-done.1, bf16[1,2,512,256]{3,2,1,0:T(8,128)(2,1)} %copy-done.4, bf16[1,2,1024,512]{3,2,1,0:T(8,128)(2,1)} %misfit_ref.5, bf16[1,2,1024,512]{3,2,1,0:T(8,128)(2,1)} %source_ref.7, ...), custom_call_target="tpu_custom_call", output_to_operand_aliasing={{0}: (8, {})} | custom-call | tf_op jit(solution)/shard_map/pallas_call | solution.py:528
  75.3 1.3 %collective-permute-start.8 = (f32[1,512]{1,0:T(1,128)}, f32[1,512]{1,0:T(1,128)S(1)}, u32[]{:S(2)}, u32[]{:S(2)}) collective-permute-start(f32[1,512]{1,0:T(1,128)} %get-tuple-element.18), channel_id=1, source_target_pairs={{24,0},{25,1},{26,2},{27,3},{28,4},{29,5},{30,6},{31,7}} | collective-permute-start | bytes 6152 | tf_op jit(solution)/shard_map/ppermute | solution.py:16
  76.6 1.3 %collective-permute-start.7 = (f32[1,512]{1,0:T(1,128)}, f32[1,512]{1,0:T(1,128)S(1)}, u32[]{:S(2)}, u32[]{:S(2)}) collective-permute-start(f32[1,512]{1,0:T(1,128)} %get-tuple-element.18), channel_id=1, source_target_pairs={{16,0},{24,8},{17,1},{25,9},{18,2},{26,10},{19,3},{27,11},{20,4},{... | collective-permute-start | bytes 6152 | tf_op jit(solution)/shard_map/ppermute | solution.py:16
  77.9 1.3 %collective-permute-start.6 = (f32[1,512]{1,0:T(1,128)}, f32[1,512]{1,0:T(1,128)S(1)}, u32[]{:S(2)}, u32[]{:S(2)}) collective-permute-start(f32[1,512]{1,0:T(1,128)} %get-tuple-element.18), channel_id=1, source_target_pairs={{8,0},{16,8},{24,16},{9,1},{17,9},{25,17},{10,2},{18,10},{26,18},{... | collective-permute-start | bytes 6152 | tf_op jit(solution)/shard_map/ppermute | solution.py:16
  79.2 3.6 %collective-permute-done.8 = f32[1,512]{1,0:T(1,128)S(1)} collective-permute-done((f32[1,512]{1,0:T(1,128)}, f32[1,512]{1,0:T(1,128)S(1)}, u32[]{:S(2)}, u32[]{:S(2)}) %collective-permute-start.8) | collective-permute-done | bytes 2080 | tf_op jit(solution)/shard_map/ppermute | solution.py:16
  82.8 0.4 collective-permute-done.7
  83.2 0.4 collective-permute-done.6
  83.6 1.2 %add_add_fusion = f32[1,512]{1,0:T(1,128)} fusion(f32[1,512]{1,0:T(1,128)S(1)} %collective-permute-done.8, f32[1,512]{1,0:T(1,128)S(1)} %collective-permute-done.7, f32[1,512]{1,0:T(1,128)} %get-tuple-element.18, f32[1,512]{1,0:T(1,128)S(1)} %collective-permute-done.6), kind=kLoop, calls=%fused_computation.7 | loop fusion | flops 1536 | bytes 10240 | tf_op jit(solution)/shard_map/add | solution.py:413
  (3 shorter events, 0.1 us)
Async XLA Ops:
  0.6 12.9 %copy-start = (bf16[1,2,1024,512]{3,2,1,0:T(8,128)(2,1)S(1)}, bf16[1,2,1024,512]{3,2,1,0:T(8,128)(2,1)}, u32[]{:S(2)}) copy-start(bf16[1,2,1024,512]{3,2,1,0:T(8,128)(2,1)} %param.9) | copy-start | bytes 6291460
  0.6 15.3 %copy-start.5 = (s32[1,1024]{1,0:T(1,128)S(1)}, s32[1,1024]{1,0:T(1,128)}, u32[]{:S(2)}) copy-start(s32[1,1024]{1,0:T(1,128)} %param.13) | copy-start | bytes 12292
  0.7 15.4 %copy-start.2 = (bf16[1,2,256,256]{3,2,1,0:T(8,128)(2,1)S(1)}, bf16[1,2,256,256]{3,2,1,0:T(8,128)(2,1)}, u32[]{:S(2)}) copy-start(bf16[1,2,256,256]{3,2,1,0:T(8,128)(2,1)} %param.12) | copy-start | bytes 786436
  0.7 17.3 %collective-permute-start = (f32[1,512]{1,0:T(1,128)}, f32[1,512]{1,0:T(1,128)S(1)}, u32[]{:S(2)}, u32[]{:S(2)}) collective-permute-start(f32[1,512]{1,0:T(1,128)} %param.15), channel_id=1, source_target_pairs={{0,8},{8,16},{16,24},{1,9},{9,17},{17,25},{2,10},{10,18},{18,26},{... | collective-permute-start | bytes 6152 | tf_op jit(solution)/shard_map/ppermute | solution.py:16
  5.8 13.5 %collective-permute-start.2 = (f32[1,512]{1,0:T(1,128)}, f32[1,512]{1,0:T(1,128)S(1)}, u32[]{:S(2)}, u32[]{:S(2)}) collective-permute-start(f32[1,512]{1,0:T(1,128)} %param.15), channel_id=1, source_target_pairs={{0,24},{1,25},{2,26},{3,27},{4,28},{5,29},{6,30},{7,31}} | collective-permute-start | bytes 6152 | tf_op jit(solution)/shard_map/ppermute | solution.py:16
  9.1 10.2 %collective-permute-start.1 = (f32[1,512]{1,0:T(1,128)}, f32[1,512]{1,0:T(1,128)S(1)}, u32[]{:S(2)}, u32[]{:S(2)}) collective-permute-start(f32[1,512]{1,0:T(1,128)} %param.15), channel_id=1, source_target_pairs={{0,16},{8,24},{1,17},{9,25},{2,18},{10,26},{3,19},{11,27},{4,20},{... | collective-permute-start | bytes 6152 | tf_op jit(solution)/shard_map/ppermute | solution.py:16
  12.2 7.0 %copy-start.6 = (f32[1,512]{1,0:T(1,128)S(1)}, f32[1,512]{1,0:T(1,128)}, u32[]{:S(2)}) copy-start(f32[1,512]{1,0:T(1,128)} %param.15) | copy-start | bytes 6148
  12.2 7.1 %copy-start.7 = (f32[512]{0:T(512)S(1)}, f32[512]{0:T(512)}, u32[]{:S(2)}) copy-start(f32[512]{0:T(512)} %param.14) | copy-start | bytes 6148
  12.3 27.9 %collective-permute-start.3 = (bf16[1,2,1024,256]{3,2,1,0:T(8,128)(2,1)S(1)}, bf16[1,2,1024,256]{3,2,1,0:T(8,128)(2,1)S(1)}, u32[]{:S(2)}, u32[]{:S(2)}) collective-permute-start(bf16[1,2,1024,256]{3,2,1,0:T(8,128)(2,1)S(1)} %slice.12), channel_id=1, source_target_pairs={{8,0},{16,8},{24,16},{9,1},{17,9},{25,17},{10,2},{18,10},{26,18},{... | collective-permute-start | bytes 3145736 | tf_op jit(solution)/shard_map/ppermute | solution.py:16
  14.6 53.1 %collective-permute-start.5 = (bf16[1,2,512,256]{3,2,1,0:T(8,128)(2,1)}, bf16[1,2,512,256]{3,2,1,0:T(8,128)(2,1)S(1)}, u32[]{:S(2)}, u32[]{:S(2)}) collective-permute-start(bf16[1,2,512,256]{3,2,1,0:T(8,128)(2,1)} %get-tuple-element.21), channel_id=1, source_target_pairs={{8,0},{16,8},{24,16},{9,1},{17,9},{25,17},{10,2},{18,10},{26,18},{... | collective-permute-start | bytes 1572872 | tf_op jit(solution)/shard_map/ppermute | solution.py:16
  18.0 43.0 %collective-permute-start.4 = (bf16[1,2,512,256]{3,2,1,0:T(8,128)(2,1)}, bf16[1,2,512,256]{3,2,1,0:T(8,128)(2,1)S(1)}, u32[]{:S(2)}, u32[]{:S(2)}) collective-permute-start(bf16[1,2,512,256]{3,2,1,0:T(8,128)(2,1)} %get-tuple-element.22), channel_id=1, source_target_pairs={{8,0},{16,8},{24,16},{9,1},{17,9},{25,17},{10,2},{18,10},{26,18},{... | collective-permute-start | bytes 1572872 | tf_op jit(solution)/shard_map/ppermute | solution.py:16
  40.2 1.0 %copy-start.3 = (bf16[1,2,1024,256]{3,2,1,0:T(8,128)(2,1)}, bf16[1,2,1024,256]{3,2,1,0:T(8,128)(2,1)S(1)}, u32[]{:S(2)}) copy-start(bf16[1,2,1024,256]{3,2,1,0:T(8,128)(2,1)S(1)} %collective-permute-done.3.arrival_ref) | copy-start | bytes 3145732
  61.0 0.8 copy-start.1
  67.8 0.8 copy-start.4
  75.3 7.5 %collective-permute-start.8 = (f32[1,512]{1,0:T(1,128)}, f32[1,512]{1,0:T(1,128)S(1)}, u32[]{:S(2)}, u32[]{:S(2)}) collective-permute-start(f32[1,512]{1,0:T(1,128)} %get-tuple-element.18), channel_id=1, source_target_pairs={{24,0},{25,1},{26,2},{27,3},{28,4},{29,5},{30,6},{31,7}} | collective-permute-start | bytes 6152 | tf_op jit(solution)/shard_map/ppermute | solution.py:16
  76.6 6.6 %collective-permute-start.7 = (f32[1,512]{1,0:T(1,128)}, f32[1,512]{1,0:T(1,128)S(1)}, u32[]{:S(2)}, u32[]{:S(2)}) collective-permute-start(f32[1,512]{1,0:T(1,128)} %get-tuple-element.18), channel_id=1, source_target_pairs={{16,0},{24,8},{17,1},{25,9},{18,2},{26,10},{19,3},{27,11},{20,4},{... | collective-permute-start | bytes 6152 | tf_op jit(solution)/shard_map/ppermute | solution.py:16
  77.9 5.7 %collective-permute-start.6 = (f32[1,512]{1,0:T(1,128)}, f32[1,512]{1,0:T(1,128)S(1)}, u32[]{:S(2)}, u32[]{:S(2)}) collective-permute-start(f32[1,512]{1,0:T(1,128)} %get-tuple-element.18), channel_id=1, source_target_pairs={{8,0},{16,8},{24,16},{9,1},{17,9},{25,17},{10,2},{18,10},{26,18},{... | collective-permute-start | bytes 6152 | tf_op jit(solution)/shard_map/ppermute | solution.py:16

commit v2 on v0

--- a/solution.py
+++ b/solution.py
@@ -294,8 +294,8 @@
         begin_in, begin_out, grad_ref, stage_ref, copy_sem,
     ):
         half, width = arrival_ref.shape[1], arrival_ref.shape[2]
-        lam_r = lam_rows(arrival_ref[0], misfit_ref[0])
-        lam_i = lam_rows(arrival_ref[1], misfit_ref[1])
+        lam_r = lam_rows(arrival_ref[0], misfit_ref[0, :half])
+        lam_i = lam_rows(arrival_ref[1], misfit_ref[1, :half])
         inv_r = inverse_t_ref[0]
         inv_i = inverse_t_ref[1]
         block_width = inv_r.shape[0]
@@ -312,8 +312,8 @@
         cot_r, cot_i = depth_adjoint(
             num_r.astype(jnp.bfloat16), num_i.astype(jnp.bfloat16), pade_ref
         )
-        source_r = source_ref[0].astype(jnp.float32)[HALO : half - HALO]
-        source_i = source_ref[1].astype(jnp.float32)[HALO : half - HALO]
+        source_r = source_ref[0, :half].astype(jnp.float32)[HALO : half - HALO]
+        source_i = source_ref[1, :half].astype(jnp.float32)[HALO : half - HALO]
         out_r, out_i, grad_row = finish_rows(
             cot_r, cot_i, trig_ref, limit_ref[HALO : half - HALO], source_r, source_i, block_index
         )
@@ -336,7 +336,8 @@
         first_ref, arrival_ref, misfit_ref, source_ref, trig_ref, limit_ref, pade_ref,
         inverse_t_ref, begin_in, begin_out, grad_ref, main_ref, wrap_ref, copy_sem,
     ):
-        half, width = arrival_ref.shape[1], arrival_ref.shape[2]
+        half, width = first_ref.shape[1], arrival_ref.shape[2]
+        tail = arrival_ref.shape[1]
         inv_r = inverse_t_ref[0]
         inv_i = inverse_t_ref[1]
         block_width = inv_r.shape[0]
@@ -356,7 +357,7 @@
         )
         pieces_r = [before_r]
         pieces_i = [before_i]
-        for start in range(0, half, block_width):
+        for start in range(0, tail, block_width):
             piece_r, piece_i = azimuth_adjoint(
                 inv_r, inv_i, lam_r[start : start + block_width], lam_i[start : start + block_width]
             )
@@ -364,7 +365,7 @@
             pieces_i.append(piece_i)
         pieces_r.append(after_r)
         pieces_i.append(after_i)
-        span = half + 2 * HALO
+        span = tail + 2 * HALO
         num_r = numerator_rows(jnp.concatenate(pieces_r, axis=0))[HALO : HALO + span]
         num_i = numerator_rows(jnp.concatenate(pieces_i, axis=0))[HALO : HALO + span]
         cot_r, cot_i = depth_adjoint(
@@ -378,13 +379,13 @@
         out_r, out_i, grad_row = finish_rows(
             cot_r, cot_i, trig_ref, limit_rows, source_r, source_i, block_index
         )
-        main_ref[0] = out_r[: half + HALO].astype(jnp.bfloat16)
-        main_ref[1] = out_i[: half + HALO].astype(jnp.bfloat16)
-        wrap_ref[0] = out_r[half + HALO :].astype(jnp.bfloat16)
-        wrap_ref[1] = out_i[half + HALO :].astype(jnp.bfloat16)
+        main_ref[0] = out_r[: tail + HALO].astype(jnp.bfloat16)
+        main_ref[1] = out_i[: tail + HALO].astype(jnp.bfloat16)
+        wrap_ref[0] = out_r[tail + HALO :].astype(jnp.bfloat16)
+        wrap_ref[1] = out_i[tail + HALO :].astype(jnp.bfloat16)
         columns = pl.ds(block_index * width, width)
         main_copy = pltpu.make_async_copy(
-            main_ref, begin_out.at[0, :, pl.ds(half - HALO, half + HALO), columns], copy_sem.at[0]
+            main_ref, begin_out.at[0, :, pl.ds(half - HALO, tail + HALO), columns], copy_sem.at[0]
         )
         wrap_copy = pltpu.make_async_copy(
             wrap_ref, begin_out.at[0, :, pl.ds(0, HALO), columns], copy_sem.at[1]
@@ -414,7 +415,8 @@
     block_size = pade_factors.shape[3]
     block_count = depth_rows // block_size
     depth_start = lax.axis_index("line") * depth_rows
-    half = rows // 2
+    half = rows - azimuth_inverse.shape[2]
+    tail = rows - half
     last = block_count - 1
     arrivals = [
         passed_along(
@@ -489,6 +491,7 @@
     any_spec = pl.BlockSpec(memory_space=pl.ANY)
     fixed_last = lambda b: (0, 0, 0, last)
     half_spec = pl.BlockSpec((None, 2, half, block_size), lambda b: (0, 0, 0, 0))
+    tail_spec = pl.BlockSpec((None, 2, tail, block_size), lambda b: (0, 0, 0, 0))
     trig_last = pl.BlockSpec((4, block_size), lambda b: (0, last))
     grad_spec = pl.BlockSpec((1, block_size), lambda b: (0, 0))
     begin_shape = jax.ShapeDtypeStruct(checkpoint.shape, jnp.bfloat16)
@@ -498,8 +501,8 @@
         grid=(1,),
         in_specs=[
             half_spec,
-            pl.BlockSpec((None, 2, half, block_size), fixed_last),
-            pl.BlockSpec((None, 2, half, block_size), fixed_last),
+            pl.BlockSpec((None, 2, rows, block_size), fixed_last),
+            pl.BlockSpec((None, 2, rows, block_size), fixed_last),
             trig_last,
             limit_spec,
             pade_spec,
@@ -520,7 +523,7 @@
         grid=(1,),
         in_specs=[
             half_spec,
-            half_spec,
+            tail_spec,
             full_last,
             full_last,
             trig_last,
@@ -532,7 +535,7 @@
         out_specs=[any_spec, grad_spec],
         out_shape=[begin_shape, grad_shape],
         scratch_shapes=[
-            pltpu.VMEM((2, half + HALO, block_size), jnp.bfloat16),
+            pltpu.VMEM((2, tail + HALO, block_size), jnp.bfloat16),
             pltpu.VMEM((2, HALO, block_size), jnp.bfloat16),
             pltpu.SemaphoreType.DMA((2,)),
         ],

time: 85 us -> 74.1 us (0.87)
  waiting for transfers between devices: 22.3 us -> 8.54 us
  starting transfers between devices: 18 us -> 20 us
  Pallas kernels: 34.4 us -> 35.3 us
    ppermute x9, waiting for transfers between devices: 22.3 us -> 8.54 us  [passed_along(): return lax.ppermute(value, axis, pairs)]
    ppermute x9, starting transfers between devices: 18 us -> 20 us  [passed_along(): return lax.ppermute(value, axis, pairs)]
    pallas_call x1, Pallas kernels: 5.96 us -> 7.73 us  [fused_local(): pl.pallas_call(make_first_half_kernel(last), grid=(1,), in_specs=[half_sp...]
    slice x1, local copies, waits for them, and re-layouts: 1.29 us -> 2.41 us  [fused_local(): adjoint_start[:, :, :, index * block_size:(index + 1) * block_size]]
    unnamed x21 -> x19, local copies, waits for them, and re-layouts: 3.47 us -> 2.43 us
    slice x1, local copies, waits for them, and re-layouts: 1.04 us -> 0.02 us  [fused_local(): second_half = passed_along(last_columns[:, :, half:], 'range', -1)]
    slice x0 -> x1, local copies, waits for them, and re-layouts: none -> 0.96 us  [fused_local(): first_half = passed_along(last_columns[:, :, :half], 'range', -1)]
    pallas_call x1, Pallas kernels: 6.72 us -> 5.86 us  [fused_local(): pl.pallas_call(make_second_half_kernel(last), grid=(1,), in_specs=[half_s...]
  transfers between devices with their start and end apart: 9 -> 9, of which waited for: 5 -> 4; matrix products, arithmetic and copies ran while one was open for 6% -> 5% of each run, Pallas kernels for 33% -> 40%
where the time goes in v2:
time: 74.1 us; the launch traced here: 73.8 us
  Pallas kernels  35.3 us (48%)
  starting transfers between devices  20 us (27%)
  waiting for transfers between devices  8.54 us (12%)
  local copies, waits for them, and re-layouts  7.04 us (10%)
  other arithmetic  2 us (3%)
  between operations  0.86 us (1%)
    ppermute x9, starting transfers between devices, passed_along(): return lax.ppermute(value, axis, pairs)  20 us
    pallas_call x1, Pallas kernels, fused_local(): pl.pallas_call(forward_kernel, grid=(block_count,), in_specs=[field_spec,...  13.1 us
    pallas_call x1, Pallas kernels, fused_local(): pl.pallas_call(kernel, grid=(1,), in_specs=in_specs, out_specs=[block_spe...  8.62 us
    ppermute x9, waiting for transfers between devices, passed_along(): return lax.ppermute(value, axis, pairs)  8.54 us
    pallas_call x1, Pallas kernels, fused_local(): pl.pallas_call(make_first_half_kernel(last), grid=(1,), in_specs=[half_sp...  7.73 us
    pallas_call x1, Pallas kernels, fused_local(): pl.pallas_call(make_second_half_kernel(last), grid=(1,), in_specs=[half_s...  5.86 us
    unnamed x19, local copies, waits for them, and re-layouts  2.43 us
    slice x1, local copies, waits for them, and re-layouts, fused_local(): adjoint_start[:, :, :, index * block_size:(index + 1) * block_size]  2.41 us
  transfers between devices with their start and end apart: 9, of which 4 were waited for; matrix products, arithmetic and copies ran while one was open for 5% of the time, Pallas kernels for 40%

profile of v2, /device:TPU:0, one launch (start us, length us, event | category | flops | bytes accessed | tf_op | source)
XLA Modules:
  0.0 73.8 jit_solution(14401696721707323486)
XLA Ops:
  0.6 0.0 copy-start.1
  0.6 0.0 copy-start.5
  0.7 0.0 copy-start.2
  0.7 2.4 %slice.12 = bf16[1,2,1024,256]{3,2,1,0:T(8,128)(2,1)} slice(bf16[1,2,1024,512]{3,2,1,0:T(8,128)(2,1)} %param.9), slice={[0:1], [0:2], [0:1024], [0:256]} | slice | bytes 2097152 | tf_op jit(solution)/shard_map/slice | solution.py:423
  3.1 0.0 copy-start.4
  3.1 1.4 %collective-permute-start.3 = (bf16[1,2,1024,256]{3,2,1,0:T(8,128)(2,1)}, bf16[1,2,1024,256]{3,2,1,0:T(8,128)(2,1)}, u32[]{:S(2)}, u32[]{:S(2)}) collective-permute-start(bf16[1,2,1024,256]{3,2,1,0:T(8,128)(2,1)} %slice.12), channel_id=1, source_target_pairs={{8,0},{16,8},{24,16},{9,1},{17,9},{25,17},{10,2},{18,10},{26,18},{... | collective-permute-start | bytes 3145736 | tf_op jit(solution)/shard_map/ppermute | solution.py:16
  4.5 5.6 %collective-permute-start = (f32[1,512]{1,0:T(1,128)}, f32[1,512]{1,0:T(1,128)S(1)}, u32[]{:S(2)}, u32[]{:S(2)}) collective-permute-start(f32[1,512]{1,0:T(1,128)} %param.15), channel_id=1, source_target_pairs={{0,8},{8,16},{16,24},{1,9},{9,17},{17,25},{2,10},{10,18},{18,26},{... | collective-permute-start | bytes 6152 | tf_op jit(solution)/shard_map/ppermute | solution.py:16
  10.1 4.7 %collective-permute-start.2 = (f32[1,512]{1,0:T(1,128)}, f32[1,512]{1,0:T(1,128)S(1)}, u32[]{:S(2)}, u32[]{:S(2)}) collective-permute-start(f32[1,512]{1,0:T(1,128)} %param.15), channel_id=1, source_target_pairs={{0,24},{1,25},{2,26},{3,27},{4,28},{5,29},{6,30},{7,31}} | collective-permute-start | bytes 6152 | tf_op jit(solution)/shard_map/ppermute | solution.py:16
  14.8 1.8 %collective-permute-start.1 = (f32[1,512]{1,0:T(1,128)}, f32[1,512]{1,0:T(1,128)S(1)}, u32[]{:S(2)}, u32[]{:S(2)}) collective-permute-start(f32[1,512]{1,0:T(1,128)} %param.15), channel_id=1, source_target_pairs={{0,16},{8,24},{1,17},{9,25},{2,18},{10,26},{3,19},{11,27},{4,20},{... | collective-permute-start | bytes 6152 | tf_op jit(solution)/shard_map/ppermute | solution.py:16
  16.7 0.0 copy-done.1
  16.7 1.0 %slice.13 = bf16[1,2,768,256]{3,2,1,0:T(8,128)(2,1)} slice(bf16[1,2,1024,512]{3,2,1,0:T(8,128)(2,1)S(1)} %copy-done.1), slice={[0:1], [0:2], [0:768], [256:512]} | slice | bytes 1572864 | tf_op jit(solution)/shard_map/slice | solution.py:428
  17.7 1.3 %collective-permute-start.4 = (bf16[1,2,768,256]{3,2,1,0:T(8,128)(2,1)}, bf16[1,2,768,256]{3,2,1,0:T(8,128)(2,1)S(1)}, u32[]{:S(2)}, u32[]{:S(2)}) collective-permute-start(bf16[1,2,768,256]{3,2,1,0:T(8,128)(2,1)} %slice.13), channel_id=1, source_target_pairs={{8,0},{16,8},{24,16},{9,1},{17,9},{25,17},{10,2},{18,10},{26,18},{... | collective-permute-start | bytes 2359304 | tf_op jit(solution)/shard_map/ppermute | solution.py:16
  18.9 0.0 copy-done.5
  19.0 0.1 pad.4.clone
  19.1 0.1 pad.5.clone
  19.1 0.0 copy-done.2
  19.1 0.8 %copy.15 = bf16[1,2,256,256]{2,3,1,0:T(8,128)(2,1)} copy(bf16[1,2,256,256]{3,2,1,0:T(8,128)(2,1)S(1)} %copy-done.2) | data formatting | bytes 524288 | tf_op args[4]
  20.0 1.0 %copy.16.limit_ref = s32[1024,1]{1,0:T(8,128)} copy(s32[1024,1]{0,1:T(1,128)S(1)} %subtract_bitcast_fusion) | data formatting | bytes 8192 | tf_op jit(solution)/shard_map/sub | solution.py:437
  21.0 0.0 collective-permute-done
  21.0 1.3 %collective-permute-start.5 = (bf16[1,2,256,256]{3,2,1,0:T(8,128)(2,1)S(1)}, bf16[1,2,256,256]{3,2,1,0:T(8,128)(2,1)S(1)}, u32[]{:S(2)}, u32[]{:S(2)}) collective-permute-start(bf16[1,2,256,256]{3,2,1,0:T(8,128)(2,1)S(1)} %slice.14), channel_id=1, source_target_pairs={{8,0},{16,8},{24,16},{9,1},{17,9},{25,17},{10,2},{18,10},{26,18},{... | collective-permute-start | bytes 786440 | tf_op jit(solution)/shard_map/ppermute | solution.py:16
  22.3 0.0 collective-permute-done.2
  22.3 0.0 collective-permute-done.1
  22.3 0.0 copy-done.6
  22.4 0.0 copy-done.4
  22.5 0.7 maximum_maximum_fusion.trig_ref
  23.1 13.1 %shard_map.103 = bf16[1,2,1024,512]{3,2,1,0:T(8,128)(2,1)} custom-call(bf16[1,2,1024,512]{3,2,1,0:T(8,128)(2,1)} %source_ref.7, f32[4,512]{1,0:T(4,128)} %maximum_maximum_fusion.trig_ref, s32[1024,1]{1,0:T(8,128)} %copy.16.limit_ref, bf16[6,2,256,256]{3,2,1,0:T(8,128)(2,1)} %pade_ref.7, bf16[2,256,256]{2,1,0:T(8,128)(2,1)} %bitcast.17), custom_call_target="tpu_custom_call" | custom-call | tf_op jit(solution)/shard_map/pallas_call | solution.py:445
  36.2 0.0 collective-permute-done.3.arrival_ref
  36.3 8.6 %shard_map.104 = (bf16[1,2,1024,512]{3,2,1,0:T(8,128)(2,1)}, f32[1,256]{1,0:T(1,128)}) custom-call(bf16[1,2,1024,256]{3,2,1,0:T(8,128)(2,1)} %collective-permute-done.3.arrival_ref, bf16[1,2,1024,512]{3,2,1,0:T(8,128)(2,1)} %misfit_ref.5, bf16[1,2,1024,512]{3,2,1,0:T(8,128)(2,1)} %source_ref.7, f32[4,512]{1,0:T(4,128)} %maximum_maximum_fusion.trig_ref, ...), custom_call_target="tpu_custom_call" | custom-call | tf_op jit(solution)/shard_map/pallas_call | solution.py:476
  44.9 4.3 %collective-permute-done.4.arrival_ref.first_ref = bf16[1,2,768,256]{3,2,1,0:T(8,128)(2,1)S(1)} collective-permute-done((bf16[1,2,768,256]{3,2,1,0:T(8,128)(2,1)}, bf16[1,2,768,256]{3,2,1,0:T(8,128)(2,1)S(1)}, u32[]{:S(2)}, u32[]{:S(2)}) %collective-permute-start.4) | collective-permute-done | bytes 786464 | tf_op jit(solution)/shard_map/ppermute | solution.py:16
  49.2 0.0 copy-start
  49.2 0.9 %copy-done = bf16[1,2,768,256]{3,2,1,0:T(8,128)(2,1)} copy-done((bf16[1,2,768,256]{3,2,1,0:T(8,128)(2,1)}, bf16[1,2,768,256]{3,2,1,0:T(8,128)(2,1)S(1)}, u32[]{:S(2)}) %copy-start) | copy-done | bytes 786456
  50.1 7.7 %shard_map.105 = (bf16[1,2,1024,512]{3,2,1,0:T(8,128)(2,1)}, f32[1,256]{1,0:T(1,128)}) custom-call(bf16[1,2,768,256]{3,2,1,0:T(8,128)(2,1)} %copy-done, bf16[1,2,1024,512]{3,2,1,0:T(8,128)(2,1)} %misfit_ref.5, bf16[1,2,1024,512]{3,2,1,0:T(8,128)(2,1)} %source_ref.7, f32[4,512]{1,0:T(4,128)} %maximum_maximum_fusion.trig_ref, ...), custom_call_target="tpu_custom_call", output_to_operand_aliasing={{0}: (7, {})} | custom-call | tf_op jit(solution)/shard_map/pallas_call | solution.py:499
  57.8 0.0 collective-permute-done.5.arrival_ref
  57.9 0.0 copy-start.3
  57.9 0.7 copy-done.3
  58.5 0.0 copy-start.7
  58.5 0.0 copy-start.8
  58.6 5.9 %shard_map.106 = (bf16[1,2,1024,512]{3,2,1,0:T(8,128)(2,1)}, f32[1,256]{1,0:T(1,128)}) custom-call(bf16[1,2,768,256]{3,2,1,0:T(8,128)(2,1)} %copy-done, bf16[1,2,256,256]{3,2,1,0:T(8,128)(2,1)} %copy-done.3, bf16[1,2,1024,512]{3,2,1,0:T(8,128)(2,1)} %misfit_ref.5, bf16[1,2,1024,512]{3,2,1,0:T(8,128)(2,1)} %source_ref.7, ...), custom_call_target="tpu_custom_call", output_to_operand_aliasing={{0}: (8, {})} | custom-call | tf_op jit(solution)/shard_map/pallas_call | solution.py:521
  64.4 0.0 copy-done.7
  64.4 0.7 add.29
  65.1 0.0 copy-done.8
  65.1 1.3 %collective-permute-start.8 = (f32[1,512]{1,0:T(1,128)S(1)}, f32[1,512]{1,0:T(1,128)S(1)}, u32[]{:S(2)}, u32[]{:S(2)}) collective-permute-start(f32[1,512]{1,0:T(1,128)S(1)} %bitcast.20), channel_id=1, source_target_pairs={{24,0},{25,1},{26,2},{27,3},{28,4},{29,5},{30,6},{31,7}} | collective-permute-start | bytes 6152 | tf_op jit(solution)/shard_map/ppermute | solution.py:16
  66.4 1.3 %collective-permute-start.7 = (f32[1,512]{1,0:T(1,128)S(1)}, f32[1,512]{1,0:T(1,128)S(1)}, u32[]{:S(2)}, u32[]{:S(2)}) collective-permute-start(f32[1,512]{1,0:T(1,128)S(1)} %bitcast.21), channel_id=1, source_target_pairs={{16,0},{24,8},{17,1},{25,9},{18,2},{26,10},{19,3},{27,11},{20,4},{... | collective-permute-start | bytes 6152 | tf_op jit(solution)/shard_map/ppermute | solution.py:16
  67.7 1.3 %collective-permute-start.6 = (f32[1,512]{1,0:T(1,128)S(1)}, f32[1,512]{1,0:T(1,128)S(1)}, u32[]{:S(2)}, u32[]{:S(2)}) collective-permute-start(f32[1,512]{1,0:T(1,128)S(1)} %bitcast.22), channel_id=1, source_target_pairs={{8,0},{16,8},{24,16},{9,1},{17,9},{25,17},{10,2},{18,10},{26,18},{... | collective-permute-start | bytes 6152 | tf_op jit(solution)/shard_map/ppermute | solution.py:16
  69.0 3.4 %collective-permute-done.8 = f32[1,512]{1,0:T(1,128)S(1)} collective-permute-done((f32[1,512]{1,0:T(1,128)S(1)}, f32[1,512]{1,0:T(1,128)S(1)}, u32[]{:S(2)}, u32[]{:S(2)}) %collective-permute-start.8) | collective-permute-done | bytes 2080 | tf_op jit(solution)/shard_map/ppermute | solution.py:16
  72.4 0.4 collective-permute-done.7
  72.8 0.4 collective-permute-done.6
  73.2 0.6 add_add_fusion
  (7 shorter events, 0.1 us)
Async XLA Ops:
  0.6 16.1 %copy-start.1 = (bf16[1,2,1024,512]{3,2,1,0:T(8,128)(2,1)S(1)}, bf16[1,2,1024,512]{3,2,1,0:T(8,128)(2,1)}, u32[]{:S(2)}) copy-start(bf16[1,2,1024,512]{3,2,1,0:T(8,128)(2,1)} %param.9) | copy-start | bytes 6291460
  0.6 18.3 %copy-start.5 = (s32[1,1024]{1,0:T(1,128)S(1)}, s32[1,1024]{1,0:T(1,128)}, u32[]{:S(2)}) copy-start(s32[1,1024]{1,0:T(1,128)} %param.13) | copy-start | bytes 12292
  0.7 18.5 %copy-start.2 = (bf16[1,2,256,256]{3,2,1,0:T(8,128)(2,1)S(1)}, bf16[1,2,256,256]{3,2,1,0:T(8,128)(2,1)}, u32[]{:S(2)}) copy-start(bf16[1,2,256,256]{3,2,1,0:T(8,128)(2,1)} %param.12) | copy-start | bytes 786436
  3.1 19.3 %copy-start.6 = (f32[1,512]{1,0:T(1,128)S(1)}, f32[1,512]{1,0:T(1,128)}, u32[]{:S(2)}) copy-start(f32[1,512]{1,0:T(1,128)} %param.15) | copy-start | bytes 6148
  3.1 19.3 %copy-start.4 = (f32[512]{0:T(512)S(1)}, f32[512]{0:T(512)}, u32[]{:S(2)}) copy-start(f32[512]{0:T(512)} %param.14) | copy-start | bytes 6148
  3.1 33.2 %collective-permute-start.3 = (bf16[1,2,1024,256]{3,2,1,0:T(8,128)(2,1)}, bf16[1,2,1024,256]{3,2,1,0:T(8,128)(2,1)}, u32[]{:S(2)}, u32[]{:S(2)}) collective-permute-start(bf16[1,2,1024,256]{3,2,1,0:T(8,128)(2,1)} %slice.12), channel_id=1, source_target_pairs={{8,0},{16,8},{24,16},{9,1},{17,9},{25,17},{10,2},{18,10},{26,18},{... | collective-permute-start | bytes 3145736 | tf_op jit(solution)/shard_map/ppermute | solution.py:16
  4.5 16.5 %collective-permute-start = (f32[1,512]{1,0:T(1,128)}, f32[1,512]{1,0:T(1,128)S(1)}, u32[]{:S(2)}, u32[]{:S(2)}) collective-permute-start(f32[1,512]{1,0:T(1,128)} %param.15), channel_id=1, source_target_pairs={{0,8},{8,16},{16,24},{1,9},{9,17},{17,25},{2,10},{10,18},{18,26},{... | collective-permute-start | bytes 6152 | tf_op jit(solution)/shard_map/ppermute | solution.py:16
  10.1 12.2 %collective-permute-start.2 = (f32[1,512]{1,0:T(1,128)}, f32[1,512]{1,0:T(1,128)S(1)}, u32[]{:S(2)}, u32[]{:S(2)}) collective-permute-start(f32[1,512]{1,0:T(1,128)} %param.15), channel_id=1, source_target_pairs={{0,24},{1,25},{2,26},{3,27},{4,28},{5,29},{6,30},{7,31}} | collective-permute-start | bytes 6152 | tf_op jit(solution)/shard_map/ppermute | solution.py:16
  14.8 7.5 %collective-permute-start.1 = (f32[1,512]{1,0:T(1,128)}, f32[1,512]{1,0:T(1,128)S(1)}, u32[]{:S(2)}, u32[]{:S(2)}) collective-permute-start(f32[1,512]{1,0:T(1,128)} %param.15), channel_id=1, source_target_pairs={{0,16},{8,24},{1,17},{9,25},{2,18},{10,26},{3,19},{11,27},{4,20},{... | collective-permute-start | bytes 6152 | tf_op jit(solution)/shard_map/ppermute | solution.py:16
  17.7 31.6 %collective-permute-start.4 = (bf16[1,2,768,256]{3,2,1,0:T(8,128)(2,1)}, bf16[1,2,768,256]{3,2,1,0:T(8,128)(2,1)S(1)}, u32[]{:S(2)}, u32[]{:S(2)}) collective-permute-start(bf16[1,2,768,256]{3,2,1,0:T(8,128)(2,1)} %slice.13), channel_id=1, source_target_pairs={{8,0},{16,8},{24,16},{9,1},{17,9},{25,17},{10,2},{18,10},{26,18},{... | collective-permute-start | bytes 2359304 | tf_op jit(solution)/shard_map/ppermute | solution.py:16
  21.0 36.8 %collective-permute-start.5 = (bf16[1,2,256,256]{3,2,1,0:T(8,128)(2,1)S(1)}, bf16[1,2,256,256]{3,2,1,0:T(8,128)(2,1)S(1)}, u32[]{:S(2)}, u32[]{:S(2)}) collective-permute-start(bf16[1,2,256,256]{3,2,1,0:T(8,128)(2,1)S(1)} %slice.14), channel_id=1, source_target_pairs={{8,0},{16,8},{24,16},{9,1},{17,9},{25,17},{10,2},{18,10},{26,18},{... | collective-permute-start | bytes 786440 | tf_op jit(solution)/shard_map/ppermute | solution.py:16
  49.2 0.9 %copy-start = (bf16[1,2,768,256]{3,2,1,0:T(8,128)(2,1)}, bf16[1,2,768,256]{3,2,1,0:T(8,128)(2,1)S(1)}, u32[]{:S(2)}) copy-start(bf16[1,2,768,256]{3,2,1,0:T(8,128)(2,1)S(1)} %collective-permute-done.4.arrival_ref.first_ref) | copy-start | bytes 2359300
  57.9 0.7 copy-start.3
  58.5 5.9 %copy-start.7 = (f32[1,256]{1,0:T(1,128)S(1)}, f32[1,256]{1,0:T(1,128)}, u32[]{:S(2)}) copy-start(f32[1,256]{1,0:T(1,128)} %get-tuple-element.17) | copy-start | bytes 3076
  58.5 6.5 %copy-start.8 = (f32[1,256]{1,0:T(1,128)S(1)}, f32[1,256]{1,0:T(1,128)}, u32[]{:S(2)}) copy-start(f32[1,256]{1,0:T(1,128)} %get-tuple-element.16) | copy-start | bytes 3076
  65.1 7.3 %collective-permute-start.8 = (f32[1,512]{1,0:T(1,128)S(1)}, f32[1,512]{1,0:T(1,128)S(1)}, u32[]{:S(2)}, u32[]{:S(2)}) collective-permute-start(f32[1,512]{1,0:T(1,128)S(1)} %bitcast.20), channel_id=1, source_target_pairs={{24,0},{25,1},{26,2},{27,3},{28,4},{29,5},{30,6},{31,7}} | collective-permute-start | bytes 6152 | tf_op jit(solution)/shard_map/ppermute | solution.py:16
  66.4 6.4 %collective-permute-start.7 = (f32[1,512]{1,0:T(1,128)S(1)}, f32[1,512]{1,0:T(1,128)S(1)}, u32[]{:S(2)}, u32[]{:S(2)}) collective-permute-start(f32[1,512]{1,0:T(1,128)S(1)} %bitcast.21), channel_id=1, source_target_pairs={{16,0},{24,8},{17,1},{25,9},{18,2},{26,10},{19,3},{27,11},{20,4},{... | collective-permute-start | bytes 6152 | tf_op jit(solution)/shard_map/ppermute | solution.py:16
  67.7 5.5 %collective-permute-start.6 = (f32[1,512]{1,0:T(1,128)S(1)}, f32[1,512]{1,0:T(1,128)S(1)}, u32[]{:S(2)}, u32[]{:S(2)}) collective-permute-start(f32[1,512]{1,0:T(1,128)S(1)} %bitcast.22), channel_id=1, source_target_pairs={{8,0},{16,8},{24,16},{9,1},{17,9},{25,17},{10,2},{18,10},{26,18},{... | collective-permute-start | bytes 6152 | tf_op jit(solution)/shard_map/ppermute | solution.py:16

commit v3 on v0

--- a/solution.py
+++ b/solution.py
@@ -291,7 +291,7 @@
 def make_first_half_kernel(block_index):
     def kernel(
         arrival_ref, misfit_ref, source_ref, trig_ref, limit_ref, pade_ref, inverse_t_ref,
-        begin_in, begin_out, grad_ref, stage_ref, copy_sem,
+        begin_in, begin_out, grad_ref, halo_ref, stage_ref, copy_sem,
     ):
         half, width = arrival_ref.shape[1], arrival_ref.shape[2]
         lam_r = lam_rows(arrival_ref[0], misfit_ref[0])
@@ -307,8 +307,15 @@
             )
             pieces_r.append(piece_r)
             pieces_i.append(piece_i)
-        num_r = numerator_rows(jnp.concatenate(pieces_r, axis=0))[HALO : half - HALO]
-        num_i = numerator_rows(jnp.concatenate(pieces_i, axis=0))[HALO : half - HALO]
+        whole_r = jnp.concatenate(pieces_r, axis=0)
+        whole_i = jnp.concatenate(pieces_i, axis=0)
+        edge = 2 * HALO
+        halo_ref[0] = whole_r[half - edge :]
+        halo_ref[1] = whole_i[half - edge :]
+        halo_ref[2] = whole_r[:edge]
+        halo_ref[3] = whole_i[:edge]
+        num_r = numerator_rows(whole_r)[HALO : half - HALO]
+        num_i = numerator_rows(whole_i)[HALO : half - HALO]
         cot_r, cot_i = depth_adjoint(
             num_r.astype(jnp.bfloat16), num_i.astype(jnp.bfloat16), pade_ref
         )
@@ -333,61 +340,73 @@
 
 def make_second_half_kernel(block_index):
     def kernel(
-        first_ref, arrival_ref, misfit_ref, source_ref, trig_ref, limit_ref, pade_ref,
-        inverse_t_ref, begin_in, begin_out, grad_ref, main_ref, wrap_ref, copy_sem,
+        halo_ref, arrival_ref, misfit_ref, source_hbm, trig_ref, limit_hbm, pade_hbm,
+        inverse_t_ref, begin_in, begin_out, grad_ref, pade_ref, source_main, source_wrap,
+        limit_main, limit_wrap, main_ref, wrap_ref, copy_sem,
     ):
-        half, width = arrival_ref.shape[1], arrival_ref.shape[2]
+        tail, width = arrival_ref.shape[1], arrival_ref.shape[2]
+        half = source_hbm.shape[2] - tail
+        columns = pl.ds(block_index * width, width)
+        loads = [
+            pltpu.make_async_copy(pade_hbm, pade_ref, copy_sem.at[0]),
+            pltpu.make_async_copy(
+                source_hbm.at[0, :, pl.ds(half - HALO, tail + HALO), columns],
+                source_main,
+                copy_sem.at[1],
+            ),
+            pltpu.make_async_copy(
+                source_hbm.at[0, :, pl.ds(0, HALO), columns], source_wrap, copy_sem.at[2]
+            ),
+            pltpu.make_async_copy(
+                limit_hbm.at[pl.ds(half - HALO, tail + HALO)], limit_main, copy_sem.at[3]
+            ),
+            pltpu.make_async_copy(limit_hbm.at[pl.ds(0, HALO)], limit_wrap, copy_sem.at[4]),
+        ]
+        for load in loads:
+            load.start()
         inv_r = inverse_t_ref[0]
         inv_i = inverse_t_ref[1]
         block_width = inv_r.shape[0]
-        edge = 2 * HALO
-        lam_r = lam_rows(arrival_ref[0], misfit_ref[0, half:])
-        lam_i = lam_rows(arrival_ref[1], misfit_ref[1, half:])
-        top_r = lam_rows(first_ref[0, half - block_width :], misfit_ref[0, half - block_width : half])
-        top_i = lam_rows(first_ref[1, half - block_width :], misfit_ref[1, half - block_width : half])
-        low_r = lam_rows(first_ref[0, :block_width], misfit_ref[0, :block_width])
-        low_i = lam_rows(first_ref[1, :block_width], misfit_ref[1, :block_width])
-        before_r, before_i = azimuth_adjoint(
-            inverse_t_ref[0, block_width - edge :], inverse_t_ref[1, block_width - edge :],
-            top_r, top_i,
-        )
-        after_r, after_i = azimuth_adjoint(
-            inverse_t_ref[0, :edge], inverse_t_ref[1, :edge], low_r, low_i
-        )
-        pieces_r = [before_r]
-        pieces_i = [before_i]
-        for start in range(0, half, block_width):
+        lam_r = lam_rows(arrival_ref[0], misfit_ref[0])
+        lam_i = lam_rows(arrival_ref[1], misfit_ref[1])
+        pieces_r = [halo_ref[0]]
+        pieces_i = [halo_ref[1]]
+        for start in range(0, tail, block_width):
             piece_r, piece_i = azimuth_adjoint(
                 inv_r, inv_i, lam_r[start : start + block_width], lam_i[start : start + block_width]
             )
             pieces_r.append(piece_r)
             pieces_i.append(piece_i)
-        pieces_r.append(after_r)
-        pieces_i.append(after_i)
-        span = half + 2 * HALO
+        pieces_r.append(halo_ref[2])
+        pieces_i.append(halo_ref[3])
+        span = tail + 2 * HALO
         num_r = numerator_rows(jnp.concatenate(pieces_r, axis=0))[HALO : HALO + span]
         num_i = numerator_rows(jnp.concatenate(pieces_i, axis=0))[HALO : HALO + span]
+        loads[0].wait()
         cot_r, cot_i = depth_adjoint(
             num_r.astype(jnp.bfloat16), num_i.astype(jnp.bfloat16), pade_ref
         )
-        full_r = source_ref[0].astype(jnp.float32)
-        full_i = source_ref[1].astype(jnp.float32)
-        source_r = jnp.concatenate([full_r[half - HALO :], full_r[:HALO]], axis=0)
-        source_i = jnp.concatenate([full_i[half - HALO :], full_i[:HALO]], axis=0)
-        limit_rows = jnp.concatenate([limit_ref[half - HALO :], limit_ref[:HALO]], axis=0)
+        for load in loads[1:]:
+            load.wait()
+        source_r = jnp.concatenate(
+            [source_main[0].astype(jnp.float32), source_wrap[0].astype(jnp.float32)], axis=0
+        )
+        source_i = jnp.concatenate(
+            [source_main[1].astype(jnp.float32), source_wrap[1].astype(jnp.float32)], axis=0
+        )
+        limit_rows = jnp.concatenate([limit_main[...], limit_wrap[...]], axis=0)
         out_r, out_i, grad_row = finish_rows(
             cot_r, cot_i, trig_ref, limit_rows, source_r, source_i, block_index
         )
-        main_ref[0] = out_r[: half + HALO].astype(jnp.bfloat16)
-        main_ref[1] = out_i[: half + HALO].astype(jnp.bfloat16)
-        wrap_ref[0] = out_r[half + HALO :].astype(jnp.bfloat16)
-        wrap_ref[1] = out_i[half + HALO :].astype(jnp.bfloat16)
-        columns = pl.ds(block_index * width, width)
+        main_ref[0] = out_r[: tail + HALO].astype(jnp.bfloat16)
+        main_ref[1] = out_i[: tail + HALO].astype(jnp.bfloat16)
+        wrap_ref[0] = out_r[tail + HALO :].astype(jnp.bfloat16)
+        wrap_ref[1] = out_i[tail + HALO :].astype(jnp.bfloat16)
         main_copy = pltpu.make_async_copy(
-            main_ref, begin_out.at[0, :, pl.ds(half - HALO, half + HALO), columns], copy_sem.at[0]
+            main_ref, begin_out.at[0, :, pl.ds(half - HALO, tail + HALO), columns], copy_sem.at[5]
         )
         wrap_copy = pltpu.make_async_copy(
-            wrap_ref, begin_out.at[0, :, pl.ds(0, HALO), columns], copy_sem.at[1]
+            wrap_ref, begin_out.at[0, :, pl.ds(0, HALO), columns], copy_sem.at[6]
         )
         main_copy.start()
         wrap_copy.start()
@@ -493,7 +512,8 @@
     grad_spec = pl.BlockSpec((1, block_size), lambda b: (0, 0))
     begin_shape = jax.ShapeDtypeStruct(checkpoint.shape, jnp.bfloat16)
     grad_shape = jax.ShapeDtypeStruct((1, block_size), jnp.float32)
-    adjoint_begin, grad_first = pl.pallas_call(
+    edge = 2 * HALO
+    adjoint_begin, grad_first, halo = pl.pallas_call(
         make_first_half_kernel(last),
         grid=(1,),
         in_specs=[
@@ -506,39 +526,46 @@
             inverse_spec,
             any_spec,
         ],
-        out_specs=[any_spec, grad_spec],
-        out_shape=[begin_shape, grad_shape],
+        out_specs=[any_spec, grad_spec, pl.BlockSpec((4, edge, block_size), lambda b: (0, 0, 0))],
+        out_shape=[
+            begin_shape, grad_shape, jax.ShapeDtypeStruct((4, edge, block_size), jnp.float32)
+        ],
         scratch_shapes=[
             pltpu.VMEM((2, half - 2 * HALO, block_size), jnp.bfloat16),
             pltpu.SemaphoreType.DMA((1,)),
         ],
         input_output_aliases={7: 0},
     )(halves[0], misfit, checkpoint, trig, limit, pade_factors, inverse_t, adjoint_begin)
-    full_last = pl.BlockSpec((None, 2, rows, block_size), fixed_last)
+    tail = rows - half
     adjoint_begin, grad_second = pl.pallas_call(
         make_second_half_kernel(last),
         grid=(1,),
         in_specs=[
-            half_spec,
-            half_spec,
-            full_last,
-            full_last,
+            pl.BlockSpec((4, edge, block_size), lambda b: (0, 0, 0)),
+            pl.BlockSpec((None, 2, tail, block_size), lambda b: (0, 0, 0, 0)),
+            pl.BlockSpec((None, 2, tail, block_size), lambda b: (0, 0, 1, last)),
+            any_spec,
             trig_last,
-            limit_spec,
-            pade_spec,
+            any_spec,
+            any_spec,
             inverse_spec,
             any_spec,
         ],
         out_specs=[any_spec, grad_spec],
         out_shape=[begin_shape, grad_shape],
         scratch_shapes=[
-            pltpu.VMEM((2, half + HALO, block_size), jnp.bfloat16),
+            pltpu.VMEM(pade_factors.shape, jnp.bfloat16),
+            pltpu.VMEM((2, tail + HALO, block_size), jnp.bfloat16),
             pltpu.VMEM((2, HALO, block_size), jnp.bfloat16),
-            pltpu.SemaphoreType.DMA((2,)),
+            pltpu.VMEM((tail + HALO, 1), jnp.int32),
+            pltpu.VMEM((HALO, 1), jnp.int32),
+            pltpu.VMEM((2, tail + HALO, block_size), jnp.bfloat16),
+            pltpu.VMEM((2, HALO, block_size), jnp.bfloat16),
+            pltpu.SemaphoreType.DMA((7,)),
         ],
         input_output_aliases={8: 0},
     )(
-        halves[0], halves[1], misfit, checkpoint, trig, limit, pade_factors, inverse_t,
+        halo, halves[1], misfit, checkpoint, trig, limit, pade_factors, inverse_t,
         adjoint_begin,
     )
     grads.append(grad_first + grad_second)

time: 85 us -> 83.4 us (0.981)
  local copies, waits for them, and re-layouts: 7.02 us -> 4.46 us
  waiting for transfers between devices: 22.3 us -> 23.4 us
    unnamed x21 -> x17, local copies, waits for them, and re-layouts: 3.47 us -> 1.87 us
    ppermute x9, waiting for transfers between devices: 22.3 us -> 23.4 us  [passed_along(): return lax.ppermute(value, axis, pairs)]
    slice x1, local copies, waits for them, and re-layouts: 1.04 us -> 0.07 us  [fused_local(): second_half = passed_along(last_columns[:, :, half:], 'range', -1)]
  transfers between devices with their start and end apart: 9 -> 9, of which waited for: 5 -> 5; matrix products, arithmetic and copies ran while one was open for 6% -> 5% of each run, Pallas kernels for 33% -> 33%
where the time goes in v3:
time: 83.4 us; the launch traced here: 83 us
  Pallas kernels  34.2 us (41%)
  waiting for transfers between devices  23.4 us (28%)
  starting transfers between devices  18 us (22%)
  local copies, waits for them, and re-layouts  4.46 us (5%)
  other arithmetic  1.99 us (2%)
  between operations  0.89 us (1%)
    ppermute x9, waiting for transfers between devices, passed_along(): return lax.ppermute(value, axis, pairs)  23.4 us
    ppermute x9, starting transfers between devices, passed_along(): return lax.ppermute(value, axis, pairs)  18 us
    pallas_call x1, Pallas kernels, fused_local(): pl.pallas_call(forward_kernel, grid=(block_count,), in_specs=[field_spec,...  13.1 us
    pallas_call x1, Pallas kernels, fused_local(): pl.pallas_call(kernel, grid=(1,), in_specs=in_specs, out_specs=[block_spe...  8.61 us
    pallas_call x1, Pallas kernels, fused_local(): pl.pallas_call(make_second_half_kernel(last), grid=(1,), in_specs=[pl.Blo...  6.55 us
    pallas_call x1, Pallas kernels, fused_local(): pl.pallas_call(make_first_half_kernel(last), grid=(1,), in_specs=[half_sp...  5.97 us
    unnamed x17, local copies, waits for them, and re-layouts  1.87 us
  transfers between devices with their start and end apart: 9, of which 5 were waited for; matrix products, arithmetic and copies ran while one was open for 5% of the time, Pallas kernels for 33%

profile of v3, /device:TPU:0, one launch (start us, length us, event | category | flops | bytes accessed | tf_op | source)
XLA Modules:
  0.0 83.0 jit_solution(9627295839505116945)
XLA Ops:
  0.6 0.0 copy-start
  0.6 0.0 copy-start.4
  0.7 0.0 copy-start.1
  0.7 5.1 %collective-permute-start = (f32[1,512]{1,0:T(1,128)}, f32[1,512]{1,0:T(1,128)S(1)}, u32[]{:S(2)}, u32[]{:S(2)}) collective-permute-start(f32[1,512]{1,0:T(1,128)} %param.15), channel_id=1, source_target_pairs={{0,8},{8,16},{16,24},{1,9},{9,17},{17,25},{2,10},{10,18},{18,26},{... | collective-permute-start | bytes 6152 | tf_op jit(solution)/shard_map/ppermute | solution.py:16
  5.8 3.3 %collective-permute-start.2 = (f32[1,512]{1,0:T(1,128)}, f32[1,512]{1,0:T(1,128)S(1)}, u32[]{:S(2)}, u32[]{:S(2)}) collective-permute-start(f32[1,512]{1,0:T(1,128)} %param.15), channel_id=1, source_target_pairs={{0,24},{1,25},{2,26},{3,27},{4,28},{5,29},{6,30},{7,31}} | collective-permute-start | bytes 6152 | tf_op jit(solution)/shard_map/ppermute | solution.py:16
  9.1 1.8 %collective-permute-start.1 = (f32[1,512]{1,0:T(1,128)}, f32[1,512]{1,0:T(1,128)S(1)}, u32[]{:S(2)}, u32[]{:S(2)}) collective-permute-start(f32[1,512]{1,0:T(1,128)} %param.15), channel_id=1, source_target_pairs={{0,16},{8,24},{1,17},{9,25},{2,18},{10,26},{3,19},{11,27},{4,20},{... | collective-permute-start | bytes 6152 | tf_op jit(solution)/shard_map/ppermute | solution.py:16
  10.9 1.3 %slice.12 = bf16[1,2,1024,256]{3,2,1,0:T(8,128)(2,1)S(1)} slice(bf16[1,2,1024,512]{3,2,1,0:T(8,128)(2,1)} %param.9), slice={[0:1], [0:2], [0:1024], [0:256]} | slice | bytes 2097152 | tf_op jit(solution)/shard_map/slice | solution.py:440
  12.2 0.0 copy-start.5
  12.2 0.0 copy-start.3
  12.3 1.3 %collective-permute-start.3 = (bf16[1,2,1024,256]{3,2,1,0:T(8,128)(2,1)S(1)}, bf16[1,2,1024,256]{3,2,1,0:T(8,128)(2,1)S(1)}, u32[]{:S(2)}, u32[]{:S(2)}) collective-permute-start(bf16[1,2,1024,256]{3,2,1,0:T(8,128)(2,1)S(1)} %slice.12), channel_id=1, source_target_pairs={{8,0},{16,8},{24,16},{9,1},{17,9},{25,17},{10,2},{18,10},{26,18},{... | collective-permute-start | bytes 3145736 | tf_op jit(solution)/shard_map/ppermute | solution.py:16
  13.6 0.0 copy-done
  13.6 0.1 fusion.5
  13.6 1.3 %collective-permute-start.5 = (bf16[1,2,512,256]{3,2,1,0:T(8,128)(2,1)S(1)}, bf16[1,2,512,256]{3,2,1,0:T(8,128)(2,1)}, u32[]{:S(2)}, u32[]{:S(2)}) collective-permute-start(bf16[1,2,512,256]{3,2,1,0:T(8,128)(2,1)S(1)} %get-tuple-element.23), channel_id=1, source_target_pairs={{8,0},{16,8},{24,16},{9,1},{17,9},{25,17},{10,2},{18,10},{26,18},{... | collective-permute-start | bytes 1572872 | tf_op jit(solution)/shard_map/ppermute | solution.py:16
  15.0 0.0 copy-done.4
  15.0 0.1 pad.4.clone
  15.0 0.1 pad.5.clone
  15.1 0.0 copy-done.1
  15.1 0.8 %copy.15 = bf16[1,2,256,256]{2,3,1,0:T(8,128)(2,1)} copy(bf16[1,2,256,256]{3,2,1,0:T(8,128)(2,1)S(1)} %copy-done.1) | data formatting | bytes 524288 | tf_op args[4]
  16.0 1.0 %copy.16.limit_ref.limit_hbm = s32[1024,1]{1,0:T(8,128)} copy(s32[1024,1]{0,1:T(1,128)S(1)} %subtract_bitcast_fusion) | data formatting | bytes 8192 | tf_op jit(solution)/shard_map/sub | solution.py:454
  17.0 0.0 collective-permute-done
  17.0 1.3 %collective-permute-start.4 = (bf16[1,2,512,256]{3,2,1,0:T(8,128)(2,1)S(1)}, bf16[1,2,512,256]{3,2,1,0:T(8,128)(2,1)}, u32[]{:S(2)}, u32[]{:S(2)}) collective-permute-start(bf16[1,2,512,256]{3,2,1,0:T(8,128)(2,1)S(1)} %get-tuple-element.24), channel_id=1, source_target_pairs={{8,0},{16,8},{24,16},{9,1},{17,9},{25,17},{10,2},{18,10},{26,18},{... | collective-permute-start | bytes 1572872 | tf_op jit(solution)/shard_map/ppermute | solution.py:16
  18.3 0.0 collective-permute-done.2
  18.3 0.0 collective-permute-done.1
  18.3 0.0 copy-done.5
  18.3 0.0 copy-done.3
  18.5 0.7 maximum_maximum_fusion.trig_ref
  19.1 13.1 %shard_map.103 = bf16[1,2,1024,512]{3,2,1,0:T(8,128)(2,1)} custom-call(bf16[1,2,1024,512]{3,2,1,0:T(8,128)(2,1)} %source_hbm.1, f32[4,512]{1,0:T(4,128)} %maximum_maximum_fusion.trig_ref, s32[1024,1]{1,0:T(8,128)} %copy.16.limit_ref.limit_hbm, bf16[6,2,256,256]{3,2,1,0:T(8,128)(2,1)} %pade_hbm.1, bf16[2,256,256]{2,1,0:T(8,128)(2,1)} %bitcast.17), custom_call_target="tpu_custom_call" | custom-call | tf_op jit(solution)/shard_map/pallas_call | solution.py:462
  32.2 8.0 %collective-permute-done.3.arrival_ref = bf16[1,2,1024,256]{3,2,1,0:T(8,128)(2,1)S(1)} collective-permute-done((bf16[1,2,1024,256]{3,2,1,0:T(8,128)(2,1)S(1)}, bf16[1,2,1024,256]{3,2,1,0:T(8,128)(2,1)S(1)}, u32[]{:S(2)}, u32[]{:S(2)}) %collective-permute-start.3) | collective-permute-done | bytes 1048608 | tf_op jit(solution)/shard_map/ppermute | solution.py:16
  40.2 0.0 copy-start.2
  40.2 1.0 %copy-done.2 = bf16[1,2,1024,256]{3,2,1,0:T(8,128)(2,1)} copy-done((bf16[1,2,1024,256]{3,2,1,0:T(8,128)(2,1)}, bf16[1,2,1024,256]{3,2,1,0:T(8,128)(2,1)S(1)}, u32[]{:S(2)}) %copy-start.2) | copy-done | bytes 1048600
  41.2 8.6 %shard_map.104 = (bf16[1,2,1024,512]{3,2,1,0:T(8,128)(2,1)}, f32[1,256]{1,0:T(1,128)}) custom-call(bf16[1,2,1024,256]{3,2,1,0:T(8,128)(2,1)} %copy-done.2, bf16[1,2,1024,512]{3,2,1,0:T(8,128)(2,1)} %misfit_ref.5, bf16[1,2,1024,512]{3,2,1,0:T(8,128)(2,1)} %source_hbm.1, f32[4,512]{1,0:T(4,128)} %maximum_maximum_fusion.trig_ref, ...), custom_call_target="tpu_custom_call" | custom-call | tf_op jit(solution)/shard_map/pallas_call | solution.py:493
  49.8 11.3 %collective-permute-done.4.arrival_ref = bf16[1,2,512,256]{3,2,1,0:T(8,128)(2,1)} collective-permute-done((bf16[1,2,512,256]{3,2,1,0:T(8,128)(2,1)S(1)}, bf16[1,2,512,256]{3,2,1,0:T(8,128)(2,1)}, u32[]{:S(2)}, u32[]{:S(2)}) %collective-permute-start.4) | collective-permute-done | bytes 524320 | tf_op jit(solution)/shard_map/ppermute | solution.py:16
  61.1 6.0 %shard_map.105 = (bf16[1,2,1024,512]{3,2,1,0:T(8,128)(2,1)}, f32[1,256]{1,0:T(1,128)}, f32[4,16,256]{2,1,0:T(8,128)}) custom-call(bf16[1,2,512,256]{3,2,1,0:T(8,128)(2,1)} %collective-permute-done.4.arrival_ref, bf16[1,2,1024,512]{3,2,1,0:T(8,128)(2,1)} %misfit_ref.5, bf16[1,2,1024,512]{3,2,1,0:T(8,128)(2,1)} %source_hbm.1, ...), custom_call_target="tpu_custom_call", output_to_operand_aliasing={{0}: (7, {})} | custom-call | tf_op jit(solution)/shard_map/pallas_call | solution.py:516
  67.0 0.0 collective-permute-done.5.arrival_ref
  67.1 0.0 copy-start.6
  67.1 0.0 copy-start.7
  67.1 6.6 %shard_map.106 = (bf16[1,2,1024,512]{3,2,1,0:T(8,128)(2,1)}, f32[1,256]{1,0:T(1,128)}) custom-call(f32[4,16,256]{2,1,0:T(8,128)} %get-tuple-element.15.halo_ref, bf16[1,2,512,256]{3,2,1,0:T(8,128)(2,1)} %collective-permute-done.5.arrival_ref, bf16[1,2,1024,512]{3,2,1,0:T(8,128)(2,1)} %misfit_ref.5, ...), custom_call_target="tpu_custom_call", output_to_operand_aliasing={{0}: (8, {})} | custom-call | tf_op jit(solution)/shard_map/pallas_call | solution.py:540
  73.6 0.0 copy-done.6
  73.6 0.7 add.29
  74.3 0.0 copy-done.7
  74.3 1.3 %collective-permute-start.8 = (f32[1,512]{1,0:T(1,128)S(1)}, f32[1,512]{1,0:T(1,128)S(1)}, u32[]{:S(2)}, u32[]{:S(2)}) collective-permute-start(f32[1,512]{1,0:T(1,128)S(1)} %bitcast.20), channel_id=1, source_target_pairs={{24,0},{25,1},{26,2},{27,3},{28,4},{29,5},{30,6},{31,7}} | collective-permute-start | bytes 6152 | tf_op jit(solution)/shard_map/ppermute | solution.py:16
  75.6 1.3 %collective-permute-start.7 = (f32[1,512]{1,0:T(1,128)S(1)}, f32[1,512]{1,0:T(1,128)S(1)}, u32[]{:S(2)}, u32[]{:S(2)}) collective-permute-start(f32[1,512]{1,0:T(1,128)S(1)} %bitcast.21), channel_id=1, source_target_pairs={{16,0},{24,8},{17,1},{25,9},{18,2},{26,10},{19,3},{27,11},{20,4},{... | collective-permute-start | bytes 6152 | tf_op jit(solution)/shard_map/ppermute | solution.py:16
  76.9 1.3 %collective-permute-start.6 = (f32[1,512]{1,0:T(1,128)S(1)}, f32[1,512]{1,0:T(1,128)S(1)}, u32[]{:S(2)}, u32[]{:S(2)}) collective-permute-start(f32[1,512]{1,0:T(1,128)S(1)} %bitcast.22), channel_id=1, source_target_pairs={{8,0},{16,8},{24,16},{9,1},{17,9},{25,17},{10,2},{18,10},{26,18},{... | collective-permute-start | bytes 6152 | tf_op jit(solution)/shard_map/ppermute | solution.py:16
  78.2 3.4 %collective-permute-done.8 = f32[1,512]{1,0:T(1,128)S(1)} collective-permute-done((f32[1,512]{1,0:T(1,128)S(1)}, f32[1,512]{1,0:T(1,128)S(1)}, u32[]{:S(2)}, u32[]{:S(2)}) %collective-permute-start.8) | collective-permute-done | bytes 2080 | tf_op jit(solution)/shard_map/ppermute | solution.py:16
  81.6 0.4 collective-permute-done.7
  82.0 0.4 collective-permute-done.6
  82.4 0.6 add_add_fusion
  (5 shorter events, 0.1 us)
Async XLA Ops:
  0.6 12.9 %copy-start = (bf16[1,2,1024,512]{3,2,1,0:T(8,128)(2,1)S(1)}, bf16[1,2,1024,512]{3,2,1,0:T(8,128)(2,1)}, u32[]{:S(2)}) copy-start(bf16[1,2,1024,512]{3,2,1,0:T(8,128)(2,1)} %param.9) | copy-start | bytes 6291460
  0.6 14.3 %copy-start.4 = (s32[1,1024]{1,0:T(1,128)S(1)}, s32[1,1024]{1,0:T(1,128)}, u32[]{:S(2)}) copy-start(s32[1,1024]{1,0:T(1,128)} %param.13) | copy-start | bytes 12292
  0.7 14.5 %copy-start.1 = (bf16[1,2,256,256]{3,2,1,0:T(8,128)(2,1)S(1)}, bf16[1,2,256,256]{3,2,1,0:T(8,128)(2,1)}, u32[]{:S(2)}) copy-start(bf16[1,2,256,256]{3,2,1,0:T(8,128)(2,1)} %param.12) | copy-start | bytes 786436
  0.7 16.3 %collective-permute-start = (f32[1,512]{1,0:T(1,128)}, f32[1,512]{1,0:T(1,128)S(1)}, u32[]{:S(2)}, u32[]{:S(2)}) collective-permute-start(f32[1,512]{1,0:T(1,128)} %param.15), channel_id=1, source_target_pairs={{0,8},{8,16},{16,24},{1,9},{9,17},{17,25},{2,10},{10,18},{18,26},{... | collective-permute-start | bytes 6152 | tf_op jit(solution)/shard_map/ppermute | solution.py:16
  5.8 12.5 %collective-permute-start.2 = (f32[1,512]{1,0:T(1,128)}, f32[1,512]{1,0:T(1,128)S(1)}, u32[]{:S(2)}, u32[]{:S(2)}) collective-permute-start(f32[1,512]{1,0:T(1,128)} %param.15), channel_id=1, source_target_pairs={{0,24},{1,25},{2,26},{3,27},{4,28},{5,29},{6,30},{7,31}} | collective-permute-start | bytes 6152 | tf_op jit(solution)/shard_map/ppermute | solution.py:16
  9.1 9.2 %collective-permute-start.1 = (f32[1,512]{1,0:T(1,128)}, f32[1,512]{1,0:T(1,128)S(1)}, u32[]{:S(2)}, u32[]{:S(2)}) collective-permute-start(f32[1,512]{1,0:T(1,128)} %param.15), channel_id=1, source_target_pairs={{0,16},{8,24},{1,17},{9,25},{2,18},{10,26},{3,19},{11,27},{4,20},{... | collective-permute-start | bytes 6152 | tf_op jit(solution)/shard_map/ppermute | solution.py:16
  12.2 6.1 %copy-start.5 = (f32[1,512]{1,0:T(1,128)S(1)}, f32[1,512]{1,0:T(1,128)}, u32[]{:S(2)}) copy-start(f32[1,512]{1,0:T(1,128)} %param.15) | copy-start | bytes 6148
  12.2 6.1 %copy-start.3 = (f32[512]{0:T(512)S(1)}, f32[512]{0:T(512)}, u32[]{:S(2)}) copy-start(f32[512]{0:T(512)} %param.14) | copy-start | bytes 6148
  12.3 27.9 %collective-permute-start.3 = (bf16[1,2,1024,256]{3,2,1,0:T(8,128)(2,1)S(1)}, bf16[1,2,1024,256]{3,2,1,0:T(8,128)(2,1)S(1)}, u32[]{:S(2)}, u32[]{:S(2)}) collective-permute-start(bf16[1,2,1024,256]{3,2,1,0:T(8,128)(2,1)S(1)} %slice.12), channel_id=1, source_target_pairs={{8,0},{16,8},{24,16},{9,1},{17,9},{25,17},{10,2},{18,10},{26,18},{... | collective-permute-start | bytes 3145736 | tf_op jit(solution)/shard_map/ppermute | solution.py:16
  13.6 53.4 %collective-permute-start.5 = (bf16[1,2,512,256]{3,2,1,0:T(8,128)(2,1)S(1)}, bf16[1,2,512,256]{3,2,1,0:T(8,128)(2,1)}, u32[]{:S(2)}, u32[]{:S(2)}) collective-permute-start(bf16[1,2,512,256]{3,2,1,0:T(8,128)(2,1)S(1)} %get-tuple-element.23), channel_id=1, source_target_pairs={{8,0},{16,8},{24,16},{9,1},{17,9},{25,17},{10,2},{18,10},{26,18},{... | collective-permute-start | bytes 1572872 | tf_op jit(solution)/shard_map/ppermute | solution.py:16
  17.0 44.1 %collective-permute-start.4 = (bf16[1,2,512,256]{3,2,1,0:T(8,128)(2,1)S(1)}, bf16[1,2,512,256]{3,2,1,0:T(8,128)(2,1)}, u32[]{:S(2)}, u32[]{:S(2)}) collective-permute-start(bf16[1,2,512,256]{3,2,1,0:T(8,128)(2,1)S(1)} %get-tuple-element.24), channel_id=1, source_target_pairs={{8,0},{16,8},{24,16},{9,1},{17,9},{25,17},{10,2},{18,10},{26,18},{... | collective-permute-start | bytes 1572872 | tf_op jit(solution)/shard_map/ppermute | solution.py:16
  40.2 1.0 %copy-start.2 = (bf16[1,2,1024,256]{3,2,1,0:T(8,128)(2,1)}, bf16[1,2,1024,256]{3,2,1,0:T(8,128)(2,1)S(1)}, u32[]{:S(2)}) copy-start(bf16[1,2,1024,256]{3,2,1,0:T(8,128)(2,1)S(1)} %collective-permute-done.3.arrival_ref) | copy-start | bytes 3145732
  67.1 6.6 %copy-start.6 = (f32[1,256]{1,0:T(1,128)S(1)}, f32[1,256]{1,0:T(1,128)}, u32[]{:S(2)}) copy-start(f32[1,256]{1,0:T(1,128)} %get-tuple-element.19) | copy-start | bytes 3076
  67.1 7.3 %copy-start.7 = (f32[1,256]{1,0:T(1,128)S(1)}, f32[1,256]{1,0:T(1,128)}, u32[]{:S(2)}) copy-start(f32[1,256]{1,0:T(1,128)} %get-tuple-element.18) | copy-start | bytes 3076
  74.3 7.3 %collective-permute-start.8 = (f32[1,512]{1,0:T(1,128)S(1)}, f32[1,512]{1,0:T(1,128)S(1)}, u32[]{:S(2)}, u32[]{:S(2)}) collective-permute-start(f32[1,512]{1,0:T(1,128)S(1)} %bitcast.20), channel_id=1, source_target_pairs={{24,0},{25,1},{26,2},{27,3},{28,4},{29,5},{30,6},{31,7}} | collective-permute-start | bytes 6152 | tf_op jit(solution)/shard_map/ppermute | solution.py:16
  75.6 6.4 %collective-permute-start.7 = (f32[1,512]{1,0:T(1,128)S(1)}, f32[1,512]{1,0:T(1,128)S(1)}, u32[]{:S(2)}, u32[]{:S(2)}) collective-permute-start(f32[1,512]{1,0:T(1,128)S(1)} %bitcast.21), channel_id=1, source_target_pairs={{16,0},{24,8},{17,1},{25,9},{18,2},{26,10},{19,3},{27,11},{20,4},{... | collective-permute-start | bytes 6152 | tf_op jit(solution)/shard_map/ppermute | solution.py:16
  76.9 5.5 %collective-permute-start.6 = (f32[1,512]{1,0:T(1,128)S(1)}, f32[1,512]{1,0:T(1,128)S(1)}, u32[]{:S(2)}, u32[]{:S(2)}) collective-permute-start(f32[1,512]{1,0:T(1,128)S(1)} %bitcast.22), channel_id=1, source_target_pairs={{8,0},{16,8},{24,16},{9,1},{17,9},{25,17},{10,2},{18,10},{26,18},{... | collective-permute-start | bytes 6152 | tf_op jit(solution)/shard_map/ppermute | solution.py:16

commit v4 on v3

--- a/solution.py
+++ b/solution.py
@@ -347,8 +347,14 @@
         tail, width = arrival_ref.shape[1], arrival_ref.shape[2]
         half = source_hbm.shape[2] - tail
         columns = pl.ds(block_index * width, width)
+        factor_count = pade_ref.shape[0]
+        pade_loads = [
+            pltpu.make_async_copy(pade_hbm.at[factor], pade_ref.at[factor], copy_sem.at[7 + factor])
+            for factor in range(factor_count - 1, -1, -1)
+        ]
+        for load in pade_loads:
+            load.start()
         loads = [
-            pltpu.make_async_copy(pade_hbm, pade_ref, copy_sem.at[0]),
             pltpu.make_async_copy(
                 source_hbm.at[0, :, pl.ds(half - HALO, tail + HALO), columns],
                 source_main,
@@ -382,11 +388,19 @@
         span = tail + 2 * HALO
         num_r = numerator_rows(jnp.concatenate(pieces_r, axis=0))[HALO : HALO + span]
         num_i = numerator_rows(jnp.concatenate(pieces_i, axis=0))[HALO : HALO + span]
-        loads[0].wait()
-        cot_r, cot_i = depth_adjoint(
-            num_r.astype(jnp.bfloat16), num_i.astype(jnp.bfloat16), pade_ref
-        )
-        for load in loads[1:]:
+        cur_r = num_r.astype(jnp.bfloat16)
+        cur_i = num_i.astype(jnp.bfloat16)
+        for load, factor in zip(pade_loads, range(factor_count - 1, -1, -1)):
+            load.wait()
+            pade_r = pade_ref[factor, 0]
+            pade_i = pade_ref[factor, 1]
+            real_part = dot_nn(cur_r, pade_r) + dot_nn(cur_i, pade_i)
+            imag_part = dot_nn(cur_i, pade_r) - dot_nn(cur_r, pade_i)
+            cur_r = real_part.astype(jnp.bfloat16)
+            cur_i = imag_part.astype(jnp.bfloat16)
+        cot_r = cur_r.astype(jnp.float32)
+        cot_i = cur_i.astype(jnp.float32)
+        for load in loads:
             load.wait()
         source_r = jnp.concatenate(
             [source_main[0].astype(jnp.float32), source_wrap[0].astype(jnp.float32)], axis=0
@@ -561,7 +575,7 @@
             pltpu.VMEM((HALO, 1), jnp.int32),
             pltpu.VMEM((2, tail + HALO, block_size), jnp.bfloat16),
             pltpu.VMEM((2, HALO, block_size), jnp.bfloat16),
-            pltpu.SemaphoreType.DMA((7,)),
+            pltpu.SemaphoreType.DMA((7 + pade_factors.shape[0],)),
         ],
         input_output_aliases={8: 0},
     )(

time: 83.4 us -> 83.9 us (level)
  no operation moved by 1% of the time
where the time goes in v4:
time: 83.9 us; the launch traced here: 83.4 us
  Pallas kernels  34.7 us (41%)
  waiting for transfers between devices  23.4 us (28%)
  starting transfers between devices  18 us (21%)
  local copies, waits for them, and re-layouts  4.46 us (5%)
  other arithmetic  1.99 us (2%)
  between operations  0.89 us (1%)
    ppermute x9, waiting for transfers between devices, passed_along(): return lax.ppermute(value, axis, pairs)  23.4 us
    ppermute x9, starting transfers between devices, passed_along(): return lax.ppermute(value, axis, pairs)  18 us
    pallas_call x1, Pallas kernels, fused_local(): pl.pallas_call(forward_kernel, grid=(block_count,), in_specs=[field_spec,...  13.1 us
    pallas_call x1, Pallas kernels, fused_local(): pl.pallas_call(kernel, grid=(1,), in_specs=in_specs, out_specs=[block_spe...  8.61 us
    pallas_call x1, Pallas kernels, fused_local(): pl.pallas_call(make_second_half_kernel(last), grid=(1,), in_specs=[pl.Blo...  6.99 us
    pallas_call x1, Pallas kernels, fused_local(): pl.pallas_call(make_first_half_kernel(last), grid=(1,), in_specs=[half_sp...  5.97 us
    unnamed x17, local copies, waits for them, and re-layouts  1.87 us
  transfers between devices with their start and end apart: 9, of which 5 were waited for; matrix products, arithmetic and copies ran while one was open for 5% of the time, Pallas kernels for 33%

profile of v4, /device:TPU:0, one launch (start us, length us, event | category | flops | bytes accessed | tf_op | source)
XLA Modules:
  0.0 83.4 jit_solution(6288819441068579176)
XLA Ops:
  0.6 0.0 copy-start
  0.6 0.0 copy-start.4
  0.7 0.0 copy-start.1
  0.7 5.1 %collective-permute-start = (f32[1,512]{1,0:T(1,128)}, f32[1,512]{1,0:T(1,128)S(1)}, u32[]{:S(2)}, u32[]{:S(2)}) collective-permute-start(f32[1,512]{1,0:T(1,128)} %param.15), channel_id=1, source_target_pairs={{0,8},{8,16},{16,24},{1,9},{9,17},{17,25},{2,10},{10,18},{18,26},{... | collective-permute-start | bytes 6152 | tf_op jit(solution)/shard_map/ppermute | solution.py:16
  5.8 3.3 %collective-permute-start.2 = (f32[1,512]{1,0:T(1,128)}, f32[1,512]{1,0:T(1,128)S(1)}, u32[]{:S(2)}, u32[]{:S(2)}) collective-permute-start(f32[1,512]{1,0:T(1,128)} %param.15), channel_id=1, source_target_pairs={{0,24},{1,25},{2,26},{3,27},{4,28},{5,29},{6,30},{7,31}} | collective-permute-start | bytes 6152 | tf_op jit(solution)/shard_map/ppermute | solution.py:16
  9.1 1.8 %collective-permute-start.1 = (f32[1,512]{1,0:T(1,128)}, f32[1,512]{1,0:T(1,128)S(1)}, u32[]{:S(2)}, u32[]{:S(2)}) collective-permute-start(f32[1,512]{1,0:T(1,128)} %param.15), channel_id=1, source_target_pairs={{0,16},{8,24},{1,17},{9,25},{2,18},{10,26},{3,19},{11,27},{4,20},{... | collective-permute-start | bytes 6152 | tf_op jit(solution)/shard_map/ppermute | solution.py:16
  10.9 1.3 %slice.12 = bf16[1,2,1024,256]{3,2,1,0:T(8,128)(2,1)S(1)} slice(bf16[1,2,1024,512]{3,2,1,0:T(8,128)(2,1)} %param.9), slice={[0:1], [0:2], [0:1024], [0:256]} | slice | bytes 2097152 | tf_op jit(solution)/shard_map/slice | solution.py:454
  12.2 0.0 copy-start.5
  12.2 0.0 copy-start.3
  12.3 1.3 %collective-permute-start.3 = (bf16[1,2,1024,256]{3,2,1,0:T(8,128)(2,1)S(1)}, bf16[1,2,1024,256]{3,2,1,0:T(8,128)(2,1)S(1)}, u32[]{:S(2)}, u32[]{:S(2)}) collective-permute-start(bf16[1,2,1024,256]{3,2,1,0:T(8,128)(2,1)S(1)} %slice.12), channel_id=1, source_target_pairs={{8,0},{16,8},{24,16},{9,1},{17,9},{25,17},{10,2},{18,10},{26,18},{... | collective-permute-start | bytes 3145736 | tf_op jit(solution)/shard_map/ppermute | solution.py:16
  13.6 0.0 copy-done
  13.6 0.1 fusion.5
  13.6 1.3 %collective-permute-start.5 = (bf16[1,2,512,256]{3,2,1,0:T(8,128)(2,1)S(1)}, bf16[1,2,512,256]{3,2,1,0:T(8,128)(2,1)}, u32[]{:S(2)}, u32[]{:S(2)}) collective-permute-start(bf16[1,2,512,256]{3,2,1,0:T(8,128)(2,1)S(1)} %get-tuple-element.23), channel_id=1, source_target_pairs={{8,0},{16,8},{24,16},{9,1},{17,9},{25,17},{10,2},{18,10},{26,18},{... | collective-permute-start | bytes 1572872 | tf_op jit(solution)/shard_map/ppermute | solution.py:16
  15.0 0.0 copy-done.4
  15.0 0.1 pad.4.clone
  15.0 0.1 pad.5.clone
  15.1 0.0 copy-done.1
  15.1 0.8 %copy.15 = bf16[1,2,256,256]{2,3,1,0:T(8,128)(2,1)} copy(bf16[1,2,256,256]{3,2,1,0:T(8,128)(2,1)S(1)} %copy-done.1) | data formatting | bytes 524288 | tf_op args[4]
  16.0 1.0 %copy.16.limit_ref.limit_hbm = s32[1024,1]{1,0:T(8,128)} copy(s32[1024,1]{0,1:T(1,128)S(1)} %subtract_bitcast_fusion) | data formatting | bytes 8192 | tf_op jit(solution)/shard_map/sub | solution.py:468
  17.0 0.0 collective-permute-done
  17.0 1.3 %collective-permute-start.4 = (bf16[1,2,512,256]{3,2,1,0:T(8,128)(2,1)S(1)}, bf16[1,2,512,256]{3,2,1,0:T(8,128)(2,1)}, u32[]{:S(2)}, u32[]{:S(2)}) collective-permute-start(bf16[1,2,512,256]{3,2,1,0:T(8,128)(2,1)S(1)} %get-tuple-element.24), channel_id=1, source_target_pairs={{8,0},{16,8},{24,16},{9,1},{17,9},{25,17},{10,2},{18,10},{26,18},{... | collective-permute-start | bytes 1572872 | tf_op jit(solution)/shard_map/ppermute | solution.py:16
  18.3 0.0 collective-permute-done.2
  18.3 0.0 collective-permute-done.1
  18.3 0.0 copy-done.5
  18.3 0.0 copy-done.3
  18.5 0.7 maximum_maximum_fusion.trig_ref
  19.1 13.1 %shard_map.103 = bf16[1,2,1024,512]{3,2,1,0:T(8,128)(2,1)} custom-call(bf16[1,2,1024,512]{3,2,1,0:T(8,128)(2,1)} %source_hbm.1, f32[4,512]{1,0:T(4,128)} %maximum_maximum_fusion.trig_ref, s32[1024,1]{1,0:T(8,128)} %copy.16.limit_ref.limit_hbm, bf16[6,2,256,256]{3,2,1,0:T(8,128)(2,1)} %pade_hbm.1, bf16[2,256,256]{2,1,0:T(8,128)(2,1)} %bitcast.17), custom_call_target="tpu_custom_call" | custom-call | tf_op jit(solution)/shard_map/pallas_call | solution.py:476
  32.2 8.0 %collective-permute-done.3.arrival_ref = bf16[1,2,1024,256]{3,2,1,0:T(8,128)(2,1)S(1)} collective-permute-done((bf16[1,2,1024,256]{3,2,1,0:T(8,128)(2,1)S(1)}, bf16[1,2,1024,256]{3,2,1,0:T(8,128)(2,1)S(1)}, u32[]{:S(2)}, u32[]{:S(2)}) %collective-permute-start.3) | collective-permute-done | bytes 1048608 | tf_op jit(solution)/shard_map/ppermute | solution.py:16
  40.2 0.0 copy-start.2
  40.2 1.0 %copy-done.2 = bf16[1,2,1024,256]{3,2,1,0:T(8,128)(2,1)} copy-done((bf16[1,2,1024,256]{3,2,1,0:T(8,128)(2,1)}, bf16[1,2,1024,256]{3,2,1,0:T(8,128)(2,1)S(1)}, u32[]{:S(2)}) %copy-start.2) | copy-done | bytes 1048600
  41.2 8.6 %shard_map.104 = (bf16[1,2,1024,512]{3,2,1,0:T(8,128)(2,1)}, f32[1,256]{1,0:T(1,128)}) custom-call(bf16[1,2,1024,256]{3,2,1,0:T(8,128)(2,1)} %copy-done.2, bf16[1,2,1024,512]{3,2,1,0:T(8,128)(2,1)} %misfit_ref.5, bf16[1,2,1024,512]{3,2,1,0:T(8,128)(2,1)} %source_hbm.1, f32[4,512]{1,0:T(4,128)} %maximum_maximum_fusion.trig_ref, ...), custom_call_target="tpu_custom_call" | custom-call | tf_op jit(solution)/shard_map/pallas_call | solution.py:507
  49.8 11.3 %collective-permute-done.4.arrival_ref = bf16[1,2,512,256]{3,2,1,0:T(8,128)(2,1)} collective-permute-done((bf16[1,2,512,256]{3,2,1,0:T(8,128)(2,1)S(1)}, bf16[1,2,512,256]{3,2,1,0:T(8,128)(2,1)}, u32[]{:S(2)}, u32[]{:S(2)}) %collective-permute-start.4) | collective-permute-done | bytes 524320 | tf_op jit(solution)/shard_map/ppermute | solution.py:16
  61.1 6.0 %shard_map.105 = (bf16[1,2,1024,512]{3,2,1,0:T(8,128)(2,1)}, f32[1,256]{1,0:T(1,128)}, f32[4,16,256]{2,1,0:T(8,128)}) custom-call(bf16[1,2,512,256]{3,2,1,0:T(8,128)(2,1)} %collective-permute-done.4.arrival_ref, bf16[1,2,1024,512]{3,2,1,0:T(8,128)(2,1)} %misfit_ref.5, bf16[1,2,1024,512]{3,2,1,0:T(8,128)(2,1)} %source_hbm.1, ...), custom_call_target="tpu_custom_call", output_to_operand_aliasing={{0}: (7, {})} | custom-call | tf_op jit(solution)/shard_map/pallas_call | solution.py:530
  67.0 0.0 collective-permute-done.5.arrival_ref
  67.1 0.0 copy-start.6
  67.1 0.0 copy-start.7
  67.1 7.0 %shard_map.106 = (bf16[1,2,1024,512]{3,2,1,0:T(8,128)(2,1)}, f32[1,256]{1,0:T(1,128)}) custom-call(f32[4,16,256]{2,1,0:T(8,128)} %get-tuple-element.15.halo_ref, bf16[1,2,512,256]{3,2,1,0:T(8,128)(2,1)} %collective-permute-done.5.arrival_ref, bf16[1,2,1024,512]{3,2,1,0:T(8,128)(2,1)} %misfit_ref.5, ...), custom_call_target="tpu_custom_call", output_to_operand_aliasing={{0}: (8, {})} | custom-call | tf_op jit(solution)/shard_map/pallas_call | solution.py:554
  74.1 0.0 copy-done.6
  74.1 0.7 add.29
  74.8 0.0 copy-done.7
  74.8 1.3 %collective-permute-start.8 = (f32[1,512]{1,0:T(1,128)S(1)}, f32[1,512]{1,0:T(1,128)S(1)}, u32[]{:S(2)}, u32[]{:S(2)}) collective-permute-start(f32[1,512]{1,0:T(1,128)S(1)} %bitcast.20), channel_id=1, source_target_pairs={{24,0},{25,1},{26,2},{27,3},{28,4},{29,5},{30,6},{31,7}} | collective-permute-start | bytes 6152 | tf_op jit(solution)/shard_map/ppermute | solution.py:16
  76.1 1.3 %collective-permute-start.7 = (f32[1,512]{1,0:T(1,128)S(1)}, f32[1,512]{1,0:T(1,128)S(1)}, u32[]{:S(2)}, u32[]{:S(2)}) collective-permute-start(f32[1,512]{1,0:T(1,128)S(1)} %bitcast.21), channel_id=1, source_target_pairs={{16,0},{24,8},{17,1},{25,9},{18,2},{26,10},{19,3},{27,11},{20,4},{... | collective-permute-start | bytes 6152 | tf_op jit(solution)/shard_map/ppermute | solution.py:16
  77.4 1.3 %collective-permute-start.6 = (f32[1,512]{1,0:T(1,128)S(1)}, f32[1,512]{1,0:T(1,128)S(1)}, u32[]{:S(2)}, u32[]{:S(2)}) collective-permute-start(f32[1,512]{1,0:T(1,128)S(1)} %bitcast.22), channel_id=1, source_target_pairs={{8,0},{16,8},{24,16},{9,1},{17,9},{25,17},{10,2},{18,10},{26,18},{... | collective-permute-start | bytes 6152 | tf_op jit(solution)/shard_map/ppermute | solution.py:16
  78.7 3.4 %collective-permute-done.8 = f32[1,512]{1,0:T(1,128)S(1)} collective-permute-done((f32[1,512]{1,0:T(1,128)S(1)}, f32[1,512]{1,0:T(1,128)S(1)}, u32[]{:S(2)}, u32[]{:S(2)}) %collective-permute-start.8) | collective-permute-done | bytes 2080 | tf_op jit(solution)/shard_map/ppermute | solution.py:16
  82.0 0.4 collective-permute-done.7
  82.4 0.4 collective-permute-done.6
  82.8 0.6 add_add_fusion
  (5 shorter events, 0.1 us)
Async XLA Ops:
  0.6 12.9 %copy-start = (bf16[1,2,1024,512]{3,2,1,0:T(8,128)(2,1)S(1)}, bf16[1,2,1024,512]{3,2,1,0:T(8,128)(2,1)}, u32[]{:S(2)}) copy-start(bf16[1,2,1024,512]{3,2,1,0:T(8,128)(2,1)} %param.9) | copy-start | bytes 6291460
  0.6 14.3 %copy-start.4 = (s32[1,1024]{1,0:T(1,128)S(1)}, s32[1,1024]{1,0:T(1,128)}, u32[]{:S(2)}) copy-start(s32[1,1024]{1,0:T(1,128)} %param.13) | copy-start | bytes 12292
  0.7 14.5 %copy-start.1 = (bf16[1,2,256,256]{3,2,1,0:T(8,128)(2,1)S(1)}, bf16[1,2,256,256]{3,2,1,0:T(8,128)(2,1)}, u32[]{:S(2)}) copy-start(bf16[1,2,256,256]{3,2,1,0:T(8,128)(2,1)} %param.12) | copy-start | bytes 786436
  0.7 16.3 %collective-permute-start = (f32[1,512]{1,0:T(1,128)}, f32[1,512]{1,0:T(1,128)S(1)}, u32[]{:S(2)}, u32[]{:S(2)}) collective-permute-start(f32[1,512]{1,0:T(1,128)} %param.15), channel_id=1, source_target_pairs={{0,8},{8,16},{16,24},{1,9},{9,17},{17,25},{2,10},{10,18},{18,26},{... | collective-permute-start | bytes 6152 | tf_op jit(solution)/shard_map/ppermute | solution.py:16
  5.8 12.5 %collective-permute-start.2 = (f32[1,512]{1,0:T(1,128)}, f32[1,512]{1,0:T(1,128)S(1)}, u32[]{:S(2)}, u32[]{:S(2)}) collective-permute-start(f32[1,512]{1,0:T(1,128)} %param.15), channel_id=1, source_target_pairs={{0,24},{1,25},{2,26},{3,27},{4,28},{5,29},{6,30},{7,31}} | collective-permute-start | bytes 6152 | tf_op jit(solution)/shard_map/ppermute | solution.py:16
  9.1 9.2 %collective-permute-start.1 = (f32[1,512]{1,0:T(1,128)}, f32[1,512]{1,0:T(1,128)S(1)}, u32[]{:S(2)}, u32[]{:S(2)}) collective-permute-start(f32[1,512]{1,0:T(1,128)} %param.15), channel_id=1, source_target_pairs={{0,16},{8,24},{1,17},{9,25},{2,18},{10,26},{3,19},{11,27},{4,20},{... | collective-permute-start | bytes 6152 | tf_op jit(solution)/shard_map/ppermute | solution.py:16
  12.2 6.1 %copy-start.5 = (f32[1,512]{1,0:T(1,128)S(1)}, f32[1,512]{1,0:T(1,128)}, u32[]{:S(2)}) copy-start(f32[1,512]{1,0:T(1,128)} %param.15) | copy-start | bytes 6148
  12.2 6.1 %copy-start.3 = (f32[512]{0:T(512)S(1)}, f32[512]{0:T(512)}, u32[]{:S(2)}) copy-start(f32[512]{0:T(512)} %param.14) | copy-start | bytes 6148
  12.3 27.9 %collective-permute-start.3 = (bf16[1,2,1024,256]{3,2,1,0:T(8,128)(2,1)S(1)}, bf16[1,2,1024,256]{3,2,1,0:T(8,128)(2,1)S(1)}, u32[]{:S(2)}, u32[]{:S(2)}) collective-permute-start(bf16[1,2,1024,256]{3,2,1,0:T(8,128)(2,1)S(1)} %slice.12), channel_id=1, source_target_pairs={{8,0},{16,8},{24,16},{9,1},{17,9},{25,17},{10,2},{18,10},{26,18},{... | collective-permute-start | bytes 3145736 | tf_op jit(solution)/shard_map/ppermute | solution.py:16
  13.6 53.4 %collective-permute-start.5 = (bf16[1,2,512,256]{3,2,1,0:T(8,128)(2,1)S(1)}, bf16[1,2,512,256]{3,2,1,0:T(8,128)(2,1)}, u32[]{:S(2)}, u32[]{:S(2)}) collective-permute-start(bf16[1,2,512,256]{3,2,1,0:T(8,128)(2,1)S(1)} %get-tuple-element.23), channel_id=1, source_target_pairs={{8,0},{16,8},{24,16},{9,1},{17,9},{25,17},{10,2},{18,10},{26,18},{... | collective-permute-start | bytes 1572872 | tf_op jit(solution)/shard_map/ppermute | solution.py:16
  17.0 44.1 %collective-permute-start.4 = (bf16[1,2,512,256]{3,2,1,0:T(8,128)(2,1)S(1)}, bf16[1,2,512,256]{3,2,1,0:T(8,128)(2,1)}, u32[]{:S(2)}, u32[]{:S(2)}) collective-permute-start(bf16[1,2,512,256]{3,2,1,0:T(8,128)(2,1)S(1)} %get-tuple-element.24), channel_id=1, source_target_pairs={{8,0},{16,8},{24,16},{9,1},{17,9},{25,17},{10,2},{18,10},{26,18},{... | collective-permute-start | bytes 1572872 | tf_op jit(solution)/shard_map/ppermute | solution.py:16
  40.2 1.0 %copy-start.2 = (bf16[1,2,1024,256]{3,2,1,0:T(8,128)(2,1)}, bf16[1,2,1024,256]{3,2,1,0:T(8,128)(2,1)S(1)}, u32[]{:S(2)}) copy-start(bf16[1,2,1024,256]{3,2,1,0:T(8,128)(2,1)S(1)} %collective-permute-done.3.arrival_ref) | copy-start | bytes 3145732
  67.1 7.0 %copy-start.6 = (f32[1,256]{1,0:T(1,128)S(1)}, f32[1,256]{1,0:T(1,128)}, u32[]{:S(2)}) copy-start(f32[1,256]{1,0:T(1,128)} %get-tuple-element.19) | copy-start | bytes 3076
  67.1 7.7 %copy-start.7 = (f32[1,256]{1,0:T(1,128)S(1)}, f32[1,256]{1,0:T(1,128)}, u32[]{:S(2)}) copy-start(f32[1,256]{1,0:T(1,128)} %get-tuple-element.18) | copy-start | bytes 3076
  74.8 7.3 %collective-permute-start.8 = (f32[1,512]{1,0:T(1,128)S(1)}, f32[1,512]{1,0:T(1,128)S(1)}, u32[]{:S(2)}, u32[]{:S(2)}) collective-permute-start(f32[1,512]{1,0:T(1,128)S(1)} %bitcast.20), channel_id=1, source_target_pairs={{24,0},{25,1},{26,2},{27,3},{28,4},{29,5},{30,6},{31,7}} | collective-permute-start | bytes 6152 | tf_op jit(solution)/shard_map/ppermute | solution.py:16
  76.1 6.4 %collective-permute-start.7 = (f32[1,512]{1,0:T(1,128)S(1)}, f32[1,512]{1,0:T(1,128)S(1)}, u32[]{:S(2)}, u32[]{:S(2)}) collective-permute-start(f32[1,512]{1,0:T(1,128)S(1)} %bitcast.21), channel_id=1, source_target_pairs={{16,0},{24,8},{17,1},{25,9},{18,2},{26,10},{19,3},{27,11},{20,4},{... | collective-permute-start | bytes 6152 | tf_op jit(solution)/shard_map/ppermute | solution.py:16
  77.4 5.5 %collective-permute-start.6 = (f32[1,512]{1,0:T(1,128)S(1)}, f32[1,512]{1,0:T(1,128)S(1)}, u32[]{:S(2)}, u32[]{:S(2)}) collective-permute-start(f32[1,512]{1,0:T(1,128)S(1)} %bitcast.22), channel_id=1, source_target_pairs={{8,0},{16,8},{24,16},{9,1},{17,9},{25,17},{10,2},{18,10},{26,18},{... | collective-permute-start | bytes 6152 | tf_op jit(solution)/shard_map/ppermute | solution.py:16

commit v5 on v3

--- a/solution.py
+++ b/solution.py
@@ -199,18 +199,20 @@
 
 def make_backward_kernel(block_index):
     def backward_kernel(
-        arrival_ref, misfit_ref, source_ref, trig_ref, limit_ref, pade_ref, inverse_t_ref,
+        lead_ref, rest_ref, misfit_ref, source_ref, trig_ref, limit_ref, pade_ref, inverse_t_ref,
         out_ref, grad_ref,
     ):
         rows, width = source_ref.shape[1], source_ref.shape[2]
+        arrival_r = jnp.concatenate([lead_ref[0], rest_ref[0]], axis=0)
+        arrival_i = jnp.concatenate([lead_ref[1], rest_ref[1]], axis=0)
         lam_r = (
-            arrival_ref[0].astype(jnp.float32) + misfit_ref[0].astype(jnp.float32)
+            arrival_r.astype(jnp.float32) + misfit_ref[0].astype(jnp.float32)
         ).astype(jnp.bfloat16)
         lam_i = (
-            arrival_ref[1].astype(jnp.float32) + misfit_ref[1].astype(jnp.float32)
+            arrival_i.astype(jnp.float32) + misfit_ref[1].astype(jnp.float32)
         ).astype(jnp.bfloat16)
-        inv_r = inverse_t_ref[0]
-        inv_i = inverse_t_ref[1]
+        inv_r = inverse_t_ref[0].T
+        inv_i = inverse_t_ref[1].T
         block_width = inv_r.shape[0]
         pieces_r = []
         pieces_i = []
@@ -296,8 +298,8 @@
         half, width = arrival_ref.shape[1], arrival_ref.shape[2]
         lam_r = lam_rows(arrival_ref[0], misfit_ref[0])
         lam_i = lam_rows(arrival_ref[1], misfit_ref[1])
-        inv_r = inverse_t_ref[0]
-        inv_i = inverse_t_ref[1]
+        inv_r = inverse_t_ref[0].T
+        inv_i = inverse_t_ref[1].T
         block_width = inv_r.shape[0]
         pieces_r = []
         pieces_i = []
@@ -364,8 +366,8 @@
         ]
         for load in loads:
             load.start()
-        inv_r = inverse_t_ref[0]
-        inv_i = inverse_t_ref[1]
+        inv_r = inverse_t_ref[0].T
+        inv_i = inverse_t_ref[1].T
         block_width = inv_r.shape[0]
         lam_r = lam_rows(arrival_ref[0], misfit_ref[0])
         lam_i = lam_rows(arrival_ref[1], misfit_ref[1])
@@ -435,12 +437,14 @@
     depth_start = lax.axis_index("line") * depth_rows
     half = rows // 2
     last = block_count - 1
-    arrivals = [
-        passed_along(
-            adjoint_start[:, :, :, index * block_size : (index + 1) * block_size], "range", -1
-        )
-        for index in range(last)
-    ]
+    arrivals = []
+    for index in range(last):
+        lead_part = adjoint_start[:, :, :half, index * block_size : (index + 1) * block_size]
+        lead_part, adjoint_start = lax.optimization_barrier((lead_part, adjoint_start))
+        columns = adjoint_start[:, :, :, index * block_size : (index + 1) * block_size]
+        lead = passed_along(lead_part, "range", -1)
+        rest = passed_along(columns[:, :, half:], "range", -1)
+        arrivals.append((lead, rest))
     last_columns = adjoint_start[:, :, :, last * block_size :]
     first_half = passed_along(last_columns[:, :, :half], "range", -1)
     second_half = passed_along(last_columns[:, :, half:], "range", -1)
@@ -453,7 +457,7 @@
     )
     limit = (bottom[0] - depth_start)[:, None]
     inverse = azimuth_inverse[0]
-    inverse_t = jnp.swapaxes(inverse, 1, 2)
+    inverse_t = inverse
     field_spec = pl.BlockSpec((None, 2, rows, block_size), lambda b: (0, 0, 0, b))
     trig_spec = pl.BlockSpec((4, block_size), lambda b: (0, b))
     limit_spec = pl.BlockSpec((rows, 1), lambda b: (0, 0))
@@ -471,9 +475,10 @@
     grads = []
     for index in range(last):
         fixed = lambda b, index=index: (0, 0, 0, index)
-        chunk_spec = pl.BlockSpec((None, 2, rows, block_size), lambda b: (0, 0, 0, 0))
+        chunk_spec = pl.BlockSpec((None, 2, half, block_size), lambda b: (0, 0, 0, 0))
         block_spec = pl.BlockSpec((None, 2, rows, block_size), fixed)
         in_specs = [
+            chunk_spec,
             chunk_spec,
             block_spec,
             block_spec,
@@ -482,14 +487,14 @@
             pade_spec,
             inverse_spec,
         ]
-        operands = [arrivals[index], misfit, checkpoint, trig, limit, pade_factors, inverse_t]
+        operands = [*arrivals[index], misfit, checkpoint, trig, limit, pade_factors, inverse_t]
         aliases = {}
         kernel = make_backward_kernel(index)
         if adjoint_begin is not None:
             in_specs.append(pl.BlockSpec(memory_space=pl.ANY))
             operands.append(adjoint_begin)
             aliases = {len(operands) - 1: 0}
-            kernel = lambda *refs, kernel=kernel: kernel(*refs[:7], *refs[8:])
+            kernel = lambda *refs, kernel=kernel: kernel(*refs[:8], *refs[9:])
         adjoint_begin, grad_part = pl.pallas_call(
             kernel,
             grid=(1,),

time: 83.4 us -> 92.5 us (1.11)
  waiting for transfers between devices: 23.4 us -> 31 us
  starting transfers between devices: 18 us -> 19.2 us
    ppermute x9 -> x10, waiting for transfers between devices: 23.4 us -> 31 us  [passed_along(): return lax.ppermute(value, axis, pairs)]
    slice x1, local copies, waits for them, and re-layouts: 0.07 us -> 1.5 us  [fused_local(): second_half = passed_along(last_columns[:, :, half:], 'range', -1)]
    ppermute x9 -> x10, starting transfers between devices: 18 us -> 19.2 us  [passed_along(): return lax.ppermute(value, axis, pairs)]
    unnamed x17 -> x14, local copies, waits for them, and re-layouts: 1.87 us -> 0.82 us
  transfers between devices with their start and end apart: 9 -> 10, of which waited for: 5 -> 4; matrix products, arithmetic and copies ran while one was open for 5% -> 5% of each run, Pallas kernels for 33% -> 30%
where the time goes in v5:
time: 92.5 us; the launch traced here: 92 us
  Pallas kernels  34.3 us (37%)
  waiting for transfers between devices  31 us (34%)
  starting transfers between devices  19.2 us (21%)
  local copies, waits for them, and re-layouts  4.65 us (5%)
  other arithmetic  2.02 us (2%)
    ppermute x10, waiting for transfers between devices, passed_along(): return lax.ppermute(value, axis, pairs)  31 us
    ppermute x10, starting transfers between devices, passed_along(): return lax.ppermute(value, axis, pairs)  19.2 us
    pallas_call x1, Pallas kernels, fused_local(): pl.pallas_call(forward_kernel, grid=(block_count,), in_specs=[field_spec,...  13.1 us
    pallas_call x1, Pallas kernels, fused_local(): pl.pallas_call(kernel, grid=(1,), in_specs=in_specs, out_specs=[block_spe...  8.63 us
    pallas_call x1, Pallas kernels, fused_local(): pl.pallas_call(make_second_half_kernel(last), grid=(1,), in_specs=[pl.Blo...  6.57 us
    pallas_call x1, Pallas kernels, fused_local(): pl.pallas_call(make_first_half_kernel(last), grid=(1,), in_specs=[half_sp...  6.01 us
  transfers between devices with their start and end apart: 10, of which 4 were waited for; matrix products, arithmetic and copies ran while one was open for 5% of the time, Pallas kernels for 30%

profile of v5, /device:TPU:0, one launch (start us, length us, event | category | flops | bytes accessed | tf_op | source)
XLA Modules:
  0.0 92.0 jit_solution(6422559506083310906)
XLA Ops:
  0.6 0.0 copy-start.3
  0.6 5.0 %collective-permute-start = (f32[1,512]{1,0:T(1,128)}, f32[1,512]{1,0:T(1,128)S(1)}, u32[]{:S(2)}, u32[]{:S(2)}) collective-permute-start(f32[1,512]{1,0:T(1,128)} %param.15), channel_id=1, source_target_pairs={{0,8},{8,16},{16,24},{1,9},{9,17},{17,25},{2,10},{10,18},{18,26},{... | collective-permute-start | bytes 6152 | tf_op jit(solution)/shard_map/ppermute | solution.py:16
  5.6 3.3 %collective-permute-start.2 = (f32[1,512]{1,0:T(1,128)}, f32[1,512]{1,0:T(1,128)S(1)}, u32[]{:S(2)}, u32[]{:S(2)}) collective-permute-start(f32[1,512]{1,0:T(1,128)} %param.15), channel_id=1, source_target_pairs={{0,24},{1,25},{2,26},{3,27},{4,28},{5,29},{6,30},{7,31}} | collective-permute-start | bytes 6152 | tf_op jit(solution)/shard_map/ppermute | solution.py:16
  8.9 1.8 %collective-permute-start.1 = (f32[1,512]{1,0:T(1,128)}, f32[1,512]{1,0:T(1,128)S(1)}, u32[]{:S(2)}, u32[]{:S(2)}) collective-permute-start(f32[1,512]{1,0:T(1,128)} %param.15), channel_id=1, source_target_pairs={{0,16},{8,24},{1,17},{9,25},{2,18},{10,26},{3,19},{11,27},{4,20},{... | collective-permute-start | bytes 6152 | tf_op jit(solution)/shard_map/ppermute | solution.py:16
  10.8 1.1 %slice.17 = bf16[1,2,512,256]{3,2,1,0:T(8,128)(2,1)S(1)} slice(bf16[1,2,1024,512]{3,2,1,0:T(8,128)(2,1)} %param.9), slice={[0:1], [0:2], [0:512], [0:256]} | slice | bytes 1048576 | tf_op jit(solution)/shard_map/slice | solution.py:442
  11.9 0.0 copy-start.4
  11.9 0.0 copy-start.2
  11.9 1.3 %collective-permute-start.3 = (bf16[1,2,512,256]{3,2,1,0:T(8,128)(2,1)S(1)}, bf16[1,2,512,256]{3,2,1,0:T(8,128)(2,1)S(1)}, u32[]{:S(2)}, u32[]{:S(2)}) collective-permute-start(bf16[1,2,512,256]{3,2,1,0:T(8,128)(2,1)S(1)} %slice.17), channel_id=1, source_target_pairs={{8,0},{16,8},{24,16},{9,1},{17,9},{25,17},{10,2},{18,10},{26,18},{... | collective-permute-start | bytes 1572872 | tf_op jit(solution)/shard_map/ppermute | solution.py:16
  13.2 1.5 %fusion.5 = (bf16[1,2,512,256]{3,2,1,0:T(8,128)(2,1)S(1)}, bf16[1,2,512,256]{3,2,1,0:T(8,128)(2,1)S(1)}, bf16[1,2,512,256]{3,2,1,0:T(8,128)(2,1)S(1)}) fusion(bf16[1,2,1024,512]{3,2,1,0:T(8,128)(2,1)} %param.9), kind=kLoop, calls=%fused_computation.11 | loop fusion | bytes 3145728 | tf_op jit(solution)/shard_map/slice | solution.py:450
  14.7 1.3 %collective-permute-start.6 = (bf16[1,2,512,256]{3,2,1,0:T(8,128)(2,1)S(1)}, bf16[1,2,512,256]{3,2,1,0:T(8,128)(2,1)}, u32[]{:S(2)}, u32[]{:S(2)}) collective-permute-start(bf16[1,2,512,256]{3,2,1,0:T(8,128)(2,1)S(1)} %get-tuple-element.29), channel_id=1, source_target_pairs={{8,0},{16,8},{24,16},{9,1},{17,9},{25,17},{10,2},{18,10},{26,18},{... | collective-permute-start | bytes 1572872 | tf_op jit(solution)/shard_map/ppermute | solution.py:16
  16.0 0.0 copy-done.3
  16.0 0.1 pad.4.clone
  16.1 0.1 pad.5.clone
  16.2 1.0 %copy.13.limit_ref.limit_hbm = s32[1024,1]{1,0:T(8,128)} copy(s32[1024,1]{0,1:T(1,128)S(1)} %subtract_bitcast_fusion) | data formatting | bytes 8192 | tf_op jit(solution)/shard_map/sub | solution.py:458
  17.2 0.0 collective-permute-done
  17.2 1.3 %collective-permute-start.5 = (bf16[1,2,512,256]{3,2,1,0:T(8,128)(2,1)S(1)}, bf16[1,2,512,256]{3,2,1,0:T(8,128)(2,1)}, u32[]{:S(2)}, u32[]{:S(2)}) collective-permute-start(bf16[1,2,512,256]{3,2,1,0:T(8,128)(2,1)S(1)} %get-tuple-element.30), channel_id=1, source_target_pairs={{8,0},{16,8},{24,16},{9,1},{17,9},{25,17},{10,2},{18,10},{26,18},{... | collective-permute-start | bytes 1572872 | tf_op jit(solution)/shard_map/ppermute | solution.py:16
  18.5 0.0 collective-permute-done.2
  18.5 1.3 %collective-permute-start.4 = (bf16[1,2,512,256]{3,2,1,0:T(8,128)(2,1)S(1)}, bf16[1,2,512,256]{3,2,1,0:T(8,128)(2,1)S(1)}, u32[]{:S(2)}, u32[]{:S(2)}) collective-permute-start(bf16[1,2,512,256]{3,2,1,0:T(8,128)(2,1)S(1)} %get-tuple-element.31), channel_id=1, source_target_pairs={{8,0},{16,8},{24,16},{9,1},{17,9},{25,17},{10,2},{18,10},{26,18},{... | collective-permute-start | bytes 1572872 | tf_op jit(solution)/shard_map/ppermute | solution.py:16
  19.8 0.0 collective-permute-done.1
  19.8 0.0 copy-done.4
  19.9 0.0 copy-done.2
  20.0 0.7 maximum_maximum_fusion.trig_ref
  20.7 13.1 %shard_map.103 = bf16[1,2,1024,512]{3,2,1,0:T(8,128)(2,1)} custom-call(bf16[1,2,1024,512]{3,2,1,0:T(8,128)(2,1)} %source_hbm.1, f32[4,512]{1,0:T(4,128)} %maximum_maximum_fusion.trig_ref, s32[1024,1]{1,0:T(8,128)} %copy.13.limit_ref.limit_hbm, bf16[6,2,256,256]{3,2,1,0:T(8,128)(2,1)} %pade_hbm.1, bf16[2,256,256]{2,1,0:T(8,128)(2,1)} %bitcast.11), custom_call_target="tpu_custom_call" | custom-call | tf_op jit(solution)/shard_map/pallas_call | solution.py:466
  33.8 0.0 collective-permute-done.3.lead_ref
  33.8 0.0 copy-start
  33.8 26.8 %collective-permute-done.4.rest_ref = bf16[1,2,512,256]{3,2,1,0:T(8,128)(2,1)S(1)} collective-permute-done((bf16[1,2,512,256]{3,2,1,0:T(8,128)(2,1)S(1)}, bf16[1,2,512,256]{3,2,1,0:T(8,128)(2,1)S(1)}, u32[]{:S(2)}, u32[]{:S(2)}) %collective-permute-start.4) | collective-permute-done | bytes 524320 | tf_op jit(solution)/shard_map/ppermute | solution.py:16
  60.6 0.0 copy-done
  60.6 0.0 copy-start.1
  60.6 0.8 copy-done.1
  61.4 8.6 %shard_map.104 = (bf16[1,2,1024,512]{3,2,1,0:T(8,128)(2,1)}, f32[1,256]{1,0:T(1,128)}) custom-call(bf16[1,2,512,256]{3,2,1,0:T(8,128)(2,1)} %copy-done, bf16[1,2,512,256]{3,2,1,0:T(8,128)(2,1)} %copy-done.1, bf16[1,2,1024,512]{3,2,1,0:T(8,128)(2,1)} %misfit_ref.5, bf16[1,2,1024,512]{3,2,1,0:T(8,128)(2,1)} %source_hbm.1, ...), custom_call_target="tpu_custom_call" | custom-call | tf_op jit(solution)/shard_map/pallas_call | solution.py:498
  70.0 0.0 collective-permute-done.5.arrival_ref
  70.0 6.0 %shard_map.105 = (bf16[1,2,1024,512]{3,2,1,0:T(8,128)(2,1)}, f32[1,256]{1,0:T(1,128)}, f32[4,16,256]{2,1,0:T(8,128)}) custom-call(bf16[1,2,512,256]{3,2,1,0:T(8,128)(2,1)} %collective-permute-done.5.arrival_ref, bf16[1,2,1024,512]{3,2,1,0:T(8,128)(2,1)} %misfit_ref.5, bf16[1,2,1024,512]{3,2,1,0:T(8,128)(2,1)} %source_hbm.1, ...), custom_call_target="tpu_custom_call", output_to_operand_aliasing={{0}: (7, {})} | custom-call | tf_op jit(solution)/shard_map/pallas_call | solution.py:521
  76.1 0.0 collective-permute-done.6.arrival_ref
  76.1 0.0 copy-start.5
  76.1 0.0 copy-start.6
  76.1 6.6 %shard_map.106 = (bf16[1,2,1024,512]{3,2,1,0:T(8,128)(2,1)}, f32[1,256]{1,0:T(1,128)}) custom-call(f32[4,16,256]{2,1,0:T(8,128)} %get-tuple-element.21.halo_ref, bf16[1,2,512,256]{3,2,1,0:T(8,128)(2,1)} %collective-permute-done.6.arrival_ref, bf16[1,2,1024,512]{3,2,1,0:T(8,128)(2,1)} %misfit_ref.5, ...), custom_call_target="tpu_custom_call", output_to_operand_aliasing={{0}: (8, {})} | custom-call | tf_op jit(solution)/shard_map/pallas_call | solution.py:545
  82.7 0.0 copy-done.5
  82.7 0.7 add.29
  83.4 0.0 copy-done.6
  83.4 1.3 %collective-permute-start.9 = (f32[1,512]{1,0:T(1,128)S(1)}, f32[1,512]{1,0:T(1,128)S(1)}, u32[]{:S(2)}, u32[]{:S(2)}) collective-permute-start(f32[1,512]{1,0:T(1,128)S(1)} %bitcast.17), channel_id=1, source_target_pairs={{24,0},{25,1},{26,2},{27,3},{28,4},{29,5},{30,6},{31,7}} | collective-permute-start | bytes 6152 | tf_op jit(solution)/shard_map/ppermute | solution.py:16
  84.7 1.3 %collective-permute-start.8 = (f32[1,512]{1,0:T(1,128)S(1)}, f32[1,512]{1,0:T(1,128)S(1)}, u32[]{:S(2)}, u32[]{:S(2)}) collective-permute-start(f32[1,512]{1,0:T(1,128)S(1)} %bitcast.18), channel_id=1, source_target_pairs={{16,0},{24,8},{17,1},{25,9},{18,2},{26,10},{19,3},{27,11},{20,4},{... | collective-permute-start | bytes 6152 | tf_op jit(solution)/shard_map/ppermute | solution.py:16
  86.0 1.3 %collective-permute-start.7 = (f32[1,512]{1,0:T(1,128)S(1)}, f32[1,512]{1,0:T(1,128)S(1)}, u32[]{:S(2)}, u32[]{:S(2)}) collective-permute-start(f32[1,512]{1,0:T(1,128)S(1)} %bitcast.19), channel_id=1, source_target_pairs={{8,0},{16,8},{24,16},{9,1},{17,9},{25,17},{10,2},{18,10},{26,18},{... | collective-permute-start | bytes 6152 | tf_op jit(solution)/shard_map/ppermute | solution.py:16
  87.3 3.4 %collective-permute-done.9 = f32[1,512]{1,0:T(1,128)S(1)} collective-permute-done((f32[1,512]{1,0:T(1,128)S(1)}, f32[1,512]{1,0:T(1,128)S(1)}, u32[]{:S(2)}, u32[]{:S(2)}) %collective-permute-start.9) | collective-permute-done | bytes 2080 | tf_op jit(solution)/shard_map/ppermute | solution.py:16
  90.7 0.4 collective-permute-done.8
  91.1 0.4 collective-permute-done.7
  91.5 0.6 add_add_fusion
  (5 shorter events, 0.1 us)
Async XLA Ops:
  0.6 15.4 %copy-start.3 = (s32[1,1024]{1,0:T(1,128)S(1)}, s32[1,1024]{1,0:T(1,128)}, u32[]{:S(2)}) copy-start(s32[1,1024]{1,0:T(1,128)} %param.13) | copy-start | bytes 12292
  0.6 16.6 %collective-permute-start = (f32[1,512]{1,0:T(1,128)}, f32[1,512]{1,0:T(1,128)S(1)}, u32[]{:S(2)}, u32[]{:S(2)}) collective-permute-start(f32[1,512]{1,0:T(1,128)} %param.15), channel_id=1, source_target_pairs={{0,8},{8,16},{16,24},{1,9},{9,17},{17,25},{2,10},{10,18},{18,26},{... | collective-permute-start | bytes 6152 | tf_op jit(solution)/shard_map/ppermute | solution.py:16
  5.6 12.9 %collective-permute-start.2 = (f32[1,512]{1,0:T(1,128)}, f32[1,512]{1,0:T(1,128)S(1)}, u32[]{:S(2)}, u32[]{:S(2)}) collective-permute-start(f32[1,512]{1,0:T(1,128)} %param.15), channel_id=1, source_target_pairs={{0,24},{1,25},{2,26},{3,27},{4,28},{5,29},{6,30},{7,31}} | collective-permute-start | bytes 6152 | tf_op jit(solution)/shard_map/ppermute | solution.py:16
  8.9 10.9 %collective-permute-start.1 = (f32[1,512]{1,0:T(1,128)}, f32[1,512]{1,0:T(1,128)S(1)}, u32[]{:S(2)}, u32[]{:S(2)}) collective-permute-start(f32[1,512]{1,0:T(1,128)} %param.15), channel_id=1, source_target_pairs={{0,16},{8,24},{1,17},{9,25},{2,18},{10,26},{3,19},{11,27},{4,20},{... | collective-permute-start | bytes 6152 | tf_op jit(solution)/shard_map/ppermute | solution.py:16
  11.9 8.0 %copy-start.4 = (f32[1,512]{1,0:T(1,128)S(1)}, f32[1,512]{1,0:T(1,128)}, u32[]{:S(2)}) copy-start(f32[1,512]{1,0:T(1,128)} %param.15) | copy-start | bytes 6148
  11.9 8.0 %copy-start.2 = (f32[512]{0:T(512)S(1)}, f32[512]{0:T(512)}, u32[]{:S(2)}) copy-start(f32[512]{0:T(512)} %param.14) | copy-start | bytes 6148
  11.9 21.9 %collective-permute-start.3 = (bf16[1,2,512,256]{3,2,1,0:T(8,128)(2,1)S(1)}, bf16[1,2,512,256]{3,2,1,0:T(8,128)(2,1)S(1)}, u32[]{:S(2)}, u32[]{:S(2)}) collective-permute-start(bf16[1,2,512,256]{3,2,1,0:T(8,128)(2,1)S(1)} %slice.17), channel_id=1, source_target_pairs={{8,0},{16,8},{24,16},{9,1},{17,9},{25,17},{10,2},{18,10},{26,18},{... | collective-permute-start | bytes 1572872 | tf_op jit(solution)/shard_map/ppermute | solution.py:16
  14.7 61.3 %collective-permute-start.6 = (bf16[1,2,512,256]{3,2,1,0:T(8,128)(2,1)S(1)}, bf16[1,2,512,256]{3,2,1,0:T(8,128)(2,1)}, u32[]{:S(2)}, u32[]{:S(2)}) collective-permute-start(bf16[1,2,512,256]{3,2,1,0:T(8,128)(2,1)S(1)} %get-tuple-element.29), channel_id=1, source_target_pairs={{8,0},{16,8},{24,16},{9,1},{17,9},{25,17},{10,2},{18,10},{26,18},{... | collective-permute-start | bytes 1572872 | tf_op jit(solution)/shard_map/ppermute | solution.py:16
  17.2 52.8 %collective-permute-start.5 = (bf16[1,2,512,256]{3,2,1,0:T(8,128)(2,1)S(1)}, bf16[1,2,512,256]{3,2,1,0:T(8,128)(2,1)}, u32[]{:S(2)}, u32[]{:S(2)}) collective-permute-start(bf16[1,2,512,256]{3,2,1,0:T(8,128)(2,1)S(1)} %get-tuple-element.30), channel_id=1, source_target_pairs={{8,0},{16,8},{24,16},{9,1},{17,9},{25,17},{10,2},{18,10},{26,18},{... | collective-permute-start | bytes 1572872 | tf_op jit(solution)/shard_map/ppermute | solution.py:16
  18.5 42.1 %collective-permute-start.4 = (bf16[1,2,512,256]{3,2,1,0:T(8,128)(2,1)S(1)}, bf16[1,2,512,256]{3,2,1,0:T(8,128)(2,1)S(1)}, u32[]{:S(2)}, u32[]{:S(2)}) collective-permute-start(bf16[1,2,512,256]{3,2,1,0:T(8,128)(2,1)S(1)} %get-tuple-element.31), channel_id=1, source_target_pairs={{8,0},{16,8},{24,16},{9,1},{17,9},{25,17},{10,2},{18,10},{26,18},{... | collective-permute-start | bytes 1572872 | tf_op jit(solution)/shard_map/ppermute | solution.py:16
  33.8 26.8 %copy-start = (bf16[1,2,512,256]{3,2,1,0:T(8,128)(2,1)}, bf16[1,2,512,256]{3,2,1,0:T(8,128)(2,1)S(1)}, u32[]{:S(2)}) copy-start(bf16[1,2,512,256]{3,2,1,0:T(8,128)(2,1)S(1)} %collective-permute-done.3.lead_ref) | copy-start | bytes 1572868
  60.6 0.8 copy-start.1
  76.1 6.6 %copy-start.5 = (f32[1,256]{1,0:T(1,128)S(1)}, f32[1,256]{1,0:T(1,128)}, u32[]{:S(2)}) copy-start(f32[1,256]{1,0:T(1,128)} %get-tuple-element.25) | copy-start | bytes 3076
  76.1 7.3 %copy-start.6 = (f32[1,256]{1,0:T(1,128)S(1)}, f32[1,256]{1,0:T(1,128)}, u32[]{:S(2)}) copy-start(f32[1,256]{1,0:T(1,128)} %get-tuple-element.24) | copy-start | bytes 3076
  83.4 7.3 %collective-permute-start.9 = (f32[1,512]{1,0:T(1,128)S(1)}, f32[1,512]{1,0:T(1,128)S(1)}, u32[]{:S(2)}, u32[]{:S(2)}) collective-permute-start(f32[1,512]{1,0:T(1,128)S(1)} %bitcast.17), channel_id=1, source_target_pairs={{24,0},{25,1},{26,2},{27,3},{28,4},{29,5},{30,6},{31,7}} | collective-permute-start | bytes 6152 | tf_op jit(solution)/shard_map/ppermute | solution.py:16
  84.7 6.4 %collective-permute-start.8 = (f32[1,512]{1,0:T(1,128)S(1)}, f32[1,512]{1,0:T(1,128)S(1)}, u32[]{:S(2)}, u32[]{:S(2)}) collective-permute-start(f32[1,512]{1,0:T(1,128)S(1)} %bitcast.18), channel_id=1, source_target_pairs={{16,0},{24,8},{17,1},{25,9},{18,2},{26,10},{19,3},{27,11},{20,4},{... | collective-permute-start | bytes 6152 | tf_op jit(solution)/shard_map/ppermute | solution.py:16
  86.0 5.5 %collective-permute-start.7 = (f32[1,512]{1,0:T(1,128)S(1)}, f32[1,512]{1,0:T(1,128)S(1)}, u32[]{:S(2)}, u32[]{:S(2)}) collective-permute-start(f32[1,512]{1,0:T(1,128)S(1)} %bitcast.19), channel_id=1, source_target_pairs={{8,0},{16,8},{24,16},{9,1},{17,9},{25,17},{10,2},{18,10},{26,18},{... | collective-permute-start | bytes 6152 | tf_op jit(solution)/shard_map/ppermute | solution.py:16

commit v6 on v3

--- a/solution.py
+++ b/solution.py
@@ -341,7 +341,8 @@
 def make_second_half_kernel(block_index):
     def kernel(
         halo_ref, arrival_ref, misfit_ref, source_hbm, trig_ref, limit_hbm, pade_hbm,
-        inverse_t_ref, begin_in, begin_out, grad_ref, pade_ref, source_main, source_wrap,
+        inverse_t_ref, begin_in, whole_grad_ref, first_grad_ref, scale_ref,
+        begin_out, grad_ref, pade_ref, source_main, source_wrap,
         limit_main, limit_wrap, main_ref, wrap_ref, copy_sem,
     ):
         tail, width = arrival_ref.shape[1], arrival_ref.shape[2]
@@ -410,7 +411,10 @@
         )
         main_copy.start()
         wrap_copy.start()
-        grad_ref[...] = grad_row
+        scale = scale_ref[...]
+        lead = block_index * width
+        grad_ref[:, :lead] = whole_grad_ref[...] * scale[:, :lead] / (half + tail)
+        grad_ref[:, lead:] = (first_grad_ref[...] + grad_row) * scale[:, lead:] / (half + tail)
         main_copy.wait()
         wrap_copy.wait()
 
@@ -537,7 +541,9 @@
         input_output_aliases={7: 0},
     )(halves[0], misfit, checkpoint, trig, limit, pade_factors, inverse_t, adjoint_begin)
     tail = rows - half
-    adjoint_begin, grad_second = pl.pallas_call(
+    scale = (-8.0 / (profile * profile * profile))[None, :]
+    whole_row = pl.BlockSpec((1, depth_rows), lambda b: (0, 0))
+    adjoint_begin, grad_here = pl.pallas_call(
         make_second_half_kernel(last),
         grid=(1,),
         in_specs=[
@@ -550,9 +556,12 @@
             any_spec,
             inverse_spec,
             any_spec,
+            pl.BlockSpec((1, last * block_size), lambda b: (0, 0)),
+            grad_spec,
+            whole_row,
         ],
-        out_specs=[any_spec, grad_spec],
-        out_shape=[begin_shape, grad_shape],
+        out_specs=[any_spec, whole_row],
+        out_shape=[begin_shape, jax.ShapeDtypeStruct((1, depth_rows), jnp.float32)],
         scratch_shapes=[
             pltpu.VMEM(pade_factors.shape, jnp.bfloat16),
             pltpu.VMEM((2, tail + HALO, block_size), jnp.bfloat16),
@@ -566,11 +575,8 @@
         input_output_aliases={8: 0},
     )(
         halo, halves[1], misfit, checkpoint, trig, limit, pade_factors, inverse_t,
-        adjoint_begin,
-    )
-    grads.append(grad_first + grad_second)
-    grad_sum = jnp.concatenate(grads, axis=1)
-    grad_here = grad_sum * (-8.0 / (profile * profile * profile)) / rows
+        adjoint_begin, jnp.concatenate(grads, axis=1), grad_first, scale,
+    )
     grad_increment = range_scan(grad_here, -1)
     return (field_end, adjoint_begin, grad_increment)
 

time: 83.4 us -> 84.4 us (1.012)
  local copies, waits for them, and re-layouts: 4.46 us -> 6.09 us
  waiting for transfers between devices: 23.4 us -> 22.3 us
    ppermute x9, waiting for transfers between devices: 23.4 us -> 22.3 us  [passed_along(): return lax.ppermute(value, axis, pairs)]
    unnamed x17 -> x15, local copies, waits for them, and re-layouts: 1.87 us -> 2.67 us
  transfers between devices with their start and end apart: 9 -> 9, of which waited for: 5 -> 5; matrix products, arithmetic and copies ran while one was open for 5% -> 7% of each run, Pallas kernels for 33% -> 33%
where the time goes in v6:
time: 84.4 us; the launch traced here: 84 us
  Pallas kernels  34.3 us (41%)
  waiting for transfers between devices  22.3 us (26%)
  starting transfers between devices  18 us (21%)
  local copies, waits for them, and re-layouts  6.09 us (7%)
  other arithmetic  2.52 us (3%)
  between operations  0.85 us (1%)
    ppermute x9, waiting for transfers between devices, passed_along(): return lax.ppermute(value, axis, pairs)  22.3 us
    ppermute x9, starting transfers between devices, passed_along(): return lax.ppermute(value, axis, pairs)  18 us
    pallas_call x1, Pallas kernels, fused_local(): pl.pallas_call(forward_kernel, grid=(block_count,), in_specs=[field_spec,...  13.1 us
    pallas_call x1, Pallas kernels, fused_local(): pl.pallas_call(kernel, grid=(1,), in_specs=in_specs, out_specs=[block_spe...  8.62 us
    pallas_call x1, Pallas kernels, fused_local(): pl.pallas_call(make_second_half_kernel(last), grid=(1,), in_specs=[pl.Blo...  6.57 us
    pallas_call x1, Pallas kernels, fused_local(): pl.pallas_call(make_first_half_kernel(last), grid=(1,), in_specs=[half_sp...  5.97 us
    unnamed x15, local copies, waits for them, and re-layouts  2.67 us
  transfers between devices with their start and end apart: 9, of which 5 were waited for; matrix products, arithmetic and copies ran while one was open for 7% of the time, Pallas kernels for 33%

profile of v6, /device:TPU:0, one launch (start us, length us, event | category | flops | bytes accessed | tf_op | source)
XLA Modules:
  0.0 84.0 jit_solution(850405628642472739)
XLA Ops:
  0.6 0.0 copy-start
  0.6 0.0 copy-start.4
  0.7 0.0 copy-start.1
  0.7 5.1 %collective-permute-start = (f32[1,512]{1,0:T(1,128)}, f32[1,512]{1,0:T(1,128)S(1)}, u32[]{:S(2)}, u32[]{:S(2)}) collective-permute-start(f32[1,512]{1,0:T(1,128)} %param.15), channel_id=1, source_target_pairs={{0,8},{8,16},{16,24},{1,9},{9,17},{17,25},{2,10},{10,18},{18,26},{... | collective-permute-start | bytes 6152 | tf_op jit(solution)/shard_map/ppermute | solution.py:16
  5.8 3.3 %collective-permute-start.2 = (f32[1,512]{1,0:T(1,128)}, f32[1,512]{1,0:T(1,128)S(1)}, u32[]{:S(2)}, u32[]{:S(2)}) collective-permute-start(f32[1,512]{1,0:T(1,128)} %param.15), channel_id=1, source_target_pairs={{0,24},{1,25},{2,26},{3,27},{4,28},{5,29},{6,30},{7,31}} | collective-permute-start | bytes 6152 | tf_op jit(solution)/shard_map/ppermute | solution.py:16
  9.1 1.8 %collective-permute-start.1 = (f32[1,512]{1,0:T(1,128)}, f32[1,512]{1,0:T(1,128)S(1)}, u32[]{:S(2)}, u32[]{:S(2)}) collective-permute-start(f32[1,512]{1,0:T(1,128)} %param.15), channel_id=1, source_target_pairs={{0,16},{8,24},{1,17},{9,25},{2,18},{10,26},{3,19},{11,27},{4,20},{... | collective-permute-start | bytes 6152 | tf_op jit(solution)/shard_map/ppermute | solution.py:16
  10.9 1.3 %slice.12 = bf16[1,2,1024,256]{3,2,1,0:T(8,128)(2,1)S(1)} slice(bf16[1,2,1024,512]{3,2,1,0:T(8,128)(2,1)} %param.9), slice={[0:1], [0:2], [0:1024], [0:256]} | slice | bytes 2097152 | tf_op jit(solution)/shard_map/slice | solution.py:444
  12.2 0.0 copy-start.5
  12.2 0.0 copy-start.6
  12.3 1.3 %collective-permute-start.3 = (bf16[1,2,1024,256]{3,2,1,0:T(8,128)(2,1)S(1)}, bf16[1,2,1024,256]{3,2,1,0:T(8,128)(2,1)S(1)}, u32[]{:S(2)}, u32[]{:S(2)}) collective-permute-start(bf16[1,2,1024,256]{3,2,1,0:T(8,128)(2,1)S(1)} %slice.12), channel_id=1, source_target_pairs={{8,0},{16,8},{24,16},{9,1},{17,9},{25,17},{10,2},{18,10},{26,18},{... | collective-permute-start | bytes 3145736 | tf_op jit(solution)/shard_map/ppermute | solution.py:16
  13.6 0.0 copy-done
  13.6 0.9 %fusion.5 = (bf16[1,2,512,256]{3,2,1,0:T(8,128)(2,1)S(1)}, bf16[1,2,512,256]{3,2,1,0:T(8,128)(2,1)}) fusion(bf16[1,2,1024,512]{3,2,1,0:T(8,128)(2,1)S(1)} %copy-done), kind=kLoop, calls=%fused_computation.10 | loop fusion | bytes 2097152 | tf_op jit(solution)/shard_map/slice | solution.py:450
  14.5 1.3 %collective-permute-start.5 = (bf16[1,2,512,256]{3,2,1,0:T(8,128)(2,1)S(1)}, bf16[1,2,512,256]{3,2,1,0:T(8,128)(2,1)S(1)}, u32[]{:S(2)}, u32[]{:S(2)}) collective-permute-start(bf16[1,2,512,256]{3,2,1,0:T(8,128)(2,1)S(1)} %get-tuple-element.23), channel_id=1, source_target_pairs={{8,0},{16,8},{24,16},{9,1},{17,9},{25,17},{10,2},{18,10},{26,18},{... | collective-permute-start | bytes 1572872 | tf_op jit(solution)/shard_map/ppermute | solution.py:16
  15.8 0.0 copy-done.4
  15.8 0.1 pad.2.clone
  15.9 0.1 pad.3.clone
  15.9 0.0 copy-done.1
  15.9 0.9 %copy.15 = bf16[1,2,256,256]{2,3,1,0:T(8,128)(2,1)} copy(bf16[1,2,256,256]{3,2,1,0:T(8,128)(2,1)S(1)} %copy-done.1) | data formatting | bytes 524288 | tf_op args[4]
  16.8 1.0 %copy.16.limit_ref.limit_hbm = s32[1024,1]{1,0:T(8,128)} copy(s32[1024,1]{0,1:T(1,128)S(1)} %subtract_bitcast_fusion) | data formatting | bytes 8192 | tf_op jit(solution)/shard_map/sub | solution.py:458
  17.8 0.0 collective-permute-done
  17.8 1.3 %collective-permute-start.4 = (bf16[1,2,512,256]{3,2,1,0:T(8,128)(2,1)}, bf16[1,2,512,256]{3,2,1,0:T(8,128)(2,1)}, u32[]{:S(2)}, u32[]{:S(2)}) collective-permute-start(bf16[1,2,512,256]{3,2,1,0:T(8,128)(2,1)} %get-tuple-element.24), channel_id=1, source_target_pairs={{8,0},{16,8},{24,16},{9,1},{17,9},{25,17},{10,2},{18,10},{26,18},{... | collective-permute-start | bytes 1572872 | tf_op jit(solution)/shard_map/ppermute | solution.py:16
  19.1 0.0 collective-permute-done.2
  19.1 0.0 collective-permute-done.1
  19.2 0.0 copy-done.5
  19.2 0.0 copy-done.6
  19.2 0.6 fusion.3
  19.8 0.7 maximum_maximum_fusion.trig_ref
  20.5 13.1 %shard_map.103 = bf16[1,2,1024,512]{3,2,1,0:T(8,128)(2,1)} custom-call(bf16[1,2,1024,512]{3,2,1,0:T(8,128)(2,1)} %source_hbm.1, f32[4,512]{1,0:T(4,128)} %maximum_maximum_fusion.trig_ref, s32[1024,1]{1,0:T(8,128)} %copy.16.limit_ref.limit_hbm, bf16[6,2,256,256]{3,2,1,0:T(8,128)(2,1)} %pade_hbm.1, bf16[2,256,256]{2,1,0:T(8,128)(2,1)} %bitcast.15), custom_call_target="tpu_custom_call" | custom-call | tf_op jit(solution)/shard_map/pallas_call | solution.py:466
  33.6 6.6 %collective-permute-done.3.arrival_ref = bf16[1,2,1024,256]{3,2,1,0:T(8,128)(2,1)S(1)} collective-permute-done((bf16[1,2,1024,256]{3,2,1,0:T(8,128)(2,1)S(1)}, bf16[1,2,1024,256]{3,2,1,0:T(8,128)(2,1)S(1)}, u32[]{:S(2)}, u32[]{:S(2)}) %collective-permute-start.3) | collective-permute-done | bytes 1048608 | tf_op jit(solution)/shard_map/ppermute | solution.py:16
  40.2 0.0 copy-start.2
  40.2 1.0 %copy-done.2 = bf16[1,2,1024,256]{3,2,1,0:T(8,128)(2,1)} copy-done((bf16[1,2,1024,256]{3,2,1,0:T(8,128)(2,1)}, bf16[1,2,1024,256]{3,2,1,0:T(8,128)(2,1)S(1)}, u32[]{:S(2)}) %copy-start.2) | copy-done | bytes 1048600
  41.2 8.6 %shard_map.104 = (bf16[1,2,1024,512]{3,2,1,0:T(8,128)(2,1)}, f32[1,256]{1,0:T(1,128)}) custom-call(bf16[1,2,1024,256]{3,2,1,0:T(8,128)(2,1)} %copy-done.2, bf16[1,2,1024,512]{3,2,1,0:T(8,128)(2,1)} %misfit_ref.5, bf16[1,2,1024,512]{3,2,1,0:T(8,128)(2,1)} %source_hbm.1, f32[4,512]{1,0:T(4,128)} %maximum_maximum_fusion.trig_ref, ...), custom_call_target="tpu_custom_call" | custom-call | tf_op jit(solution)/shard_map/pallas_call | solution.py:497
  49.8 11.3 %collective-permute-done.4.arrival_ref = bf16[1,2,512,256]{3,2,1,0:T(8,128)(2,1)} collective-permute-done((bf16[1,2,512,256]{3,2,1,0:T(8,128)(2,1)}, bf16[1,2,512,256]{3,2,1,0:T(8,128)(2,1)}, u32[]{:S(2)}, u32[]{:S(2)}) %collective-permute-start.4) | collective-permute-done | bytes 524320 | tf_op jit(solution)/shard_map/ppermute | solution.py:16
  61.1 6.0 %shard_map.105 = (bf16[1,2,1024,512]{3,2,1,0:T(8,128)(2,1)}, f32[1,256]{1,0:T(1,128)}, f32[4,16,256]{2,1,0:T(8,128)}) custom-call(bf16[1,2,512,256]{3,2,1,0:T(8,128)(2,1)} %collective-permute-done.4.arrival_ref, bf16[1,2,1024,512]{3,2,1,0:T(8,128)(2,1)} %misfit_ref.5, bf16[1,2,1024,512]{3,2,1,0:T(8,128)(2,1)} %source_hbm.1, ...), custom_call_target="tpu_custom_call", output_to_operand_aliasing={{0}: (7, {})} | custom-call | tf_op jit(solution)/shard_map/pallas_call | solution.py:520
  67.0 0.0 collective-permute-done.5.arrival_ref
  67.1 0.0 copy-start.3
  67.1 0.8 copy-done.3
  67.8 6.6 %shard_map.106 = (bf16[1,2,1024,512]{3,2,1,0:T(8,128)(2,1)}, f32[1,512]{1,0:T(1,128)}) custom-call(f32[4,16,256]{2,1,0:T(8,128)} %get-tuple-element.15.halo_ref, bf16[1,2,512,256]{3,2,1,0:T(8,128)(2,1)} %copy-done.3, bf16[1,2,1024,512]{3,2,1,0:T(8,128)(2,1)} %misfit_ref.5, bf16[1,2,1024,512]{3,2,1,0:T(8,128)(2,1)} %source_hbm.1, ...), custom_call_target="tpu_custom_call", output_to_operand_aliasing={{0}: (8, {})} | custom-call | tf_op jit(solution)/shard_map/pallas_call | solution.py:546
  74.4 1.3 %collective-permute-start.8 = (f32[1,512]{1,0:T(1,128)}, f32[1,512]{1,0:T(1,128)S(1)}, u32[]{:S(2)}, u32[]{:S(2)}) collective-permute-start(f32[1,512]{1,0:T(1,128)} %get-tuple-element.20), channel_id=1, source_target_pairs={{24,0},{25,1},{26,2},{27,3},{28,4},{29,5},{30,6},{31,7}} | collective-permute-start | bytes 6152 | tf_op jit(solution)/shard_map/ppermute | solution.py:16
  75.7 1.3 %collective-permute-start.7 = (f32[1,512]{1,0:T(1,128)}, f32[1,512]{1,0:T(1,128)S(1)}, u32[]{:S(2)}, u32[]{:S(2)}) collective-permute-start(f32[1,512]{1,0:T(1,128)} %get-tuple-element.20), channel_id=1, source_target_pairs={{16,0},{24,8},{17,1},{25,9},{18,2},{26,10},{19,3},{27,11},{20,4},{... | collective-permute-start | bytes 6152 | tf_op jit(solution)/shard_map/ppermute | solution.py:16
  77.0 1.3 %collective-permute-start.6 = (f32[1,512]{1,0:T(1,128)}, f32[1,512]{1,0:T(1,128)S(1)}, u32[]{:S(2)}, u32[]{:S(2)}) collective-permute-start(f32[1,512]{1,0:T(1,128)} %get-tuple-element.20), channel_id=1, source_target_pairs={{8,0},{16,8},{24,16},{9,1},{17,9},{25,17},{10,2},{18,10},{26,18},{... | collective-permute-start | bytes 6152 | tf_op jit(solution)/shard_map/ppermute | solution.py:16
  78.3 3.6 %collective-permute-done.8 = f32[1,512]{1,0:T(1,128)S(1)} collective-permute-done((f32[1,512]{1,0:T(1,128)}, f32[1,512]{1,0:T(1,128)S(1)}, u32[]{:S(2)}, u32[]{:S(2)}) %collective-permute-start.8) | collective-permute-done | bytes 2080 | tf_op jit(solution)/shard_map/ppermute | solution.py:16
  81.9 0.4 collective-permute-done.7
  82.3 0.4 collective-permute-done.6
  82.7 1.3 %add_add_fusion = f32[1,512]{1,0:T(1,128)} fusion(f32[1,512]{1,0:T(1,128)S(1)} %collective-permute-done.8, f32[1,512]{1,0:T(1,128)S(1)} %collective-permute-done.7, f32[1,512]{1,0:T(1,128)} %get-tuple-element.20, f32[1,512]{1,0:T(1,128)S(1)} %collective-permute-done.6), kind=kLoop, calls=%fused_computation.7 | loop fusion | flops 1536 | bytes 10240 | tf_op jit(solution)/shard_map/add | solution.py:428
  (3 shorter events, 0.1 us)
Async XLA Ops:
  0.6 12.9 %copy-start = (bf16[1,2,1024,512]{3,2,1,0:T(8,128)(2,1)S(1)}, bf16[1,2,1024,512]{3,2,1,0:T(8,128)(2,1)}, u32[]{:S(2)}) copy-start(bf16[1,2,1024,512]{3,2,1,0:T(8,128)(2,1)} %param.9) | copy-start | bytes 6291460
  0.6 15.1 %copy-start.4 = (s32[1,1024]{1,0:T(1,128)S(1)}, s32[1,1024]{1,0:T(1,128)}, u32[]{:S(2)}) copy-start(s32[1,1024]{1,0:T(1,128)} %param.13) | copy-start | bytes 12292
  0.7 15.3 %copy-start.1 = (bf16[1,2,256,256]{3,2,1,0:T(8,128)(2,1)S(1)}, bf16[1,2,256,256]{3,2,1,0:T(8,128)(2,1)}, u32[]{:S(2)}) copy-start(bf16[1,2,256,256]{3,2,1,0:T(8,128)(2,1)} %param.12) | copy-start | bytes 786436
  0.7 17.2 %collective-permute-start = (f32[1,512]{1,0:T(1,128)}, f32[1,512]{1,0:T(1,128)S(1)}, u32[]{:S(2)}, u32[]{:S(2)}) collective-permute-start(f32[1,512]{1,0:T(1,128)} %param.15), channel_id=1, source_target_pairs={{0,8},{8,16},{16,24},{1,9},{9,17},{17,25},{2,10},{10,18},{18,26},{... | collective-permute-start | bytes 6152 | tf_op jit(solution)/shard_map/ppermute | solution.py:16
  5.8 13.4 %collective-permute-start.2 = (f32[1,512]{1,0:T(1,128)}, f32[1,512]{1,0:T(1,128)S(1)}, u32[]{:S(2)}, u32[]{:S(2)}) collective-permute-start(f32[1,512]{1,0:T(1,128)} %param.15), channel_id=1, source_target_pairs={{0,24},{1,25},{2,26},{3,27},{4,28},{5,29},{6,30},{7,31}} | collective-permute-start | bytes 6152 | tf_op jit(solution)/shard_map/ppermute | solution.py:16
  9.1 10.1 %collective-permute-start.1 = (f32[1,512]{1,0:T(1,128)}, f32[1,512]{1,0:T(1,128)S(1)}, u32[]{:S(2)}, u32[]{:S(2)}) collective-permute-start(f32[1,512]{1,0:T(1,128)} %param.15), channel_id=1, source_target_pairs={{0,16},{8,24},{1,17},{9,25},{2,18},{10,26},{3,19},{11,27},{4,20},{... | collective-permute-start | bytes 6152 | tf_op jit(solution)/shard_map/ppermute | solution.py:16
  12.2 6.9 %copy-start.5 = (f32[1,512]{1,0:T(1,128)S(1)}, f32[1,512]{1,0:T(1,128)}, u32[]{:S(2)}) copy-start(f32[1,512]{1,0:T(1,128)} %param.15) | copy-start | bytes 6148
  12.2 6.9 %copy-start.6 = (f32[512]{0:T(512)S(1)}, f32[512]{0:T(512)}, u32[]{:S(2)}) copy-start(f32[512]{0:T(512)} %param.14) | copy-start | bytes 6148
  12.3 27.9 %collective-permute-start.3 = (bf16[1,2,1024,256]{3,2,1,0:T(8,128)(2,1)S(1)}, bf16[1,2,1024,256]{3,2,1,0:T(8,128)(2,1)S(1)}, u32[]{:S(2)}, u32[]{:S(2)}) collective-permute-start(bf16[1,2,1024,256]{3,2,1,0:T(8,128)(2,1)S(1)} %slice.12), channel_id=1, source_target_pairs={{8,0},{16,8},{24,16},{9,1},{17,9},{25,17},{10,2},{18,10},{26,18},{... | collective-permute-start | bytes 3145736 | tf_op jit(solution)/shard_map/ppermute | solution.py:16
  14.5 52.6 %collective-permute-start.5 = (bf16[1,2,512,256]{3,2,1,0:T(8,128)(2,1)S(1)}, bf16[1,2,512,256]{3,2,1,0:T(8,128)(2,1)S(1)}, u32[]{:S(2)}, u32[]{:S(2)}) collective-permute-start(bf16[1,2,512,256]{3,2,1,0:T(8,128)(2,1)S(1)} %get-tuple-element.23), channel_id=1, source_target_pairs={{8,0},{16,8},{24,16},{9,1},{17,9},{25,17},{10,2},{18,10},{26,18},{... | collective-permute-start | bytes 1572872 | tf_op jit(solution)/shard_map/ppermute | solution.py:16
  17.8 43.2 %collective-permute-start.4 = (bf16[1,2,512,256]{3,2,1,0:T(8,128)(2,1)}, bf16[1,2,512,256]{3,2,1,0:T(8,128)(2,1)}, u32[]{:S(2)}, u32[]{:S(2)}) collective-permute-start(bf16[1,2,512,256]{3,2,1,0:T(8,128)(2,1)} %get-tuple-element.24), channel_id=1, source_target_pairs={{8,0},{16,8},{24,16},{9,1},{17,9},{25,17},{10,2},{18,10},{26,18},{... | collective-permute-start | bytes 1572872 | tf_op jit(solution)/shard_map/ppermute | solution.py:16
  40.2 1.0 %copy-start.2 = (bf16[1,2,1024,256]{3,2,1,0:T(8,128)(2,1)}, bf16[1,2,1024,256]{3,2,1,0:T(8,128)(2,1)S(1)}, u32[]{:S(2)}) copy-start(bf16[1,2,1024,256]{3,2,1,0:T(8,128)(2,1)S(1)} %collective-permute-done.3.arrival_ref) | copy-start | bytes 3145732
  67.1 0.8 copy-start.3
  74.4 7.5 %collective-permute-start.8 = (f32[1,512]{1,0:T(1,128)}, f32[1,512]{1,0:T(1,128)S(1)}, u32[]{:S(2)}, u32[]{:S(2)}) collective-permute-start(f32[1,512]{1,0:T(1,128)} %get-tuple-element.20), channel_id=1, source_target_pairs={{24,0},{25,1},{26,2},{27,3},{28,4},{29,5},{30,6},{31,7}} | collective-permute-start | bytes 6152 | tf_op jit(solution)/shard_map/ppermute | solution.py:16
  75.7 6.6 %collective-permute-start.7 = (f32[1,512]{1,0:T(1,128)}, f32[1,512]{1,0:T(1,128)S(1)}, u32[]{:S(2)}, u32[]{:S(2)}) collective-permute-start(f32[1,512]{1,0:T(1,128)} %get-tuple-element.20), channel_id=1, source_target_pairs={{16,0},{24,8},{17,1},{25,9},{18,2},{26,10},{19,3},{27,11},{20,4},{... | collective-permute-start | bytes 6152 | tf_op jit(solution)/shard_map/ppermute | solution.py:16
  77.0 5.7 %collective-permute-start.6 = (f32[1,512]{1,0:T(1,128)}, f32[1,512]{1,0:T(1,128)S(1)}, u32[]{:S(2)}, u32[]{:S(2)}) collective-permute-start(f32[1,512]{1,0:T(1,128)} %get-tuple-element.20), channel_id=1, source_target_pairs={{8,0},{16,8},{24,16},{9,1},{17,9},{25,17},{10,2},{18,10},{26,18},{... | collective-permute-start | bytes 6152 | tf_op jit(solution)/shard_map/ppermute | solution.py:16

commit v7 on v3

--- a/solution.py
+++ b/solution.py
@@ -341,8 +341,8 @@
 def make_second_half_kernel(block_index):
     def kernel(
         halo_ref, arrival_ref, misfit_ref, source_hbm, trig_ref, limit_hbm, pade_hbm,
-        inverse_t_ref, begin_in, begin_out, grad_ref, pade_ref, source_main, source_wrap,
-        limit_main, limit_wrap, main_ref, wrap_ref, copy_sem,
+        inverse_hbm, begin_in, begin_out, grad_ref, pade_ref, source_main, source_wrap,
+        limit_main, limit_wrap, main_ref, wrap_ref, inverse_t_ref, copy_sem,
     ):
         tail, width = arrival_ref.shape[1], arrival_ref.shape[2]
         half = source_hbm.shape[2] - tail
@@ -362,13 +362,16 @@
             ),
             pltpu.make_async_copy(limit_hbm.at[pl.ds(0, HALO)], limit_wrap, copy_sem.at[4]),
         ]
+        inverse_load = pltpu.make_async_copy(inverse_hbm, inverse_t_ref, copy_sem.at[7])
+        inverse_load.start()
         for load in loads:
             load.start()
+        lam_r = lam_rows(arrival_ref[0], misfit_ref[0])
+        lam_i = lam_rows(arrival_ref[1], misfit_ref[1])
+        inverse_load.wait()
         inv_r = inverse_t_ref[0]
         inv_i = inverse_t_ref[1]
         block_width = inv_r.shape[0]
-        lam_r = lam_rows(arrival_ref[0], misfit_ref[0])
-        lam_i = lam_rows(arrival_ref[1], misfit_ref[1])
         pieces_r = [halo_ref[0]]
         pieces_i = [halo_ref[1]]
         for start in range(0, tail, block_width):
@@ -548,7 +551,7 @@
             trig_last,
             any_spec,
             any_spec,
-            inverse_spec,
+            any_spec,
             any_spec,
         ],
         out_specs=[any_spec, grad_spec],
@@ -561,7 +564,8 @@
             pltpu.VMEM((HALO, 1), jnp.int32),
             pltpu.VMEM((2, tail + HALO, block_size), jnp.bfloat16),
             pltpu.VMEM((2, HALO, block_size), jnp.bfloat16),
-            pltpu.SemaphoreType.DMA((7,)),
+            pltpu.VMEM(inverse_t.shape, jnp.bfloat16),
+            pltpu.SemaphoreType.DMA((8,)),
         ],
         input_output_aliases={8: 0},
     )(

time: 83.4 us -> 83.5 us (level)
  no operation moved by 1% of the time
where the time goes in v7:
time: 83.5 us; the launch traced here: 83.1 us
  Pallas kernels  34.3 us (41%)
  waiting for transfers between devices  23.4 us (28%)
  starting transfers between devices  18 us (22%)
  local copies, waits for them, and re-layouts  4.46 us (5%)
  other arithmetic  1.99 us (2%)
  between operations  0.89 us (1%)
    ppermute x9, waiting for transfers between devices, passed_along(): return lax.ppermute(value, axis, pairs)  23.4 us
    ppermute x9, starting transfers between devices, passed_along(): return lax.ppermute(value, axis, pairs)  18 us
    pallas_call x1, Pallas kernels, fused_local(): pl.pallas_call(forward_kernel, grid=(block_count,), in_specs=[field_spec,...  13.1 us
    pallas_call x1, Pallas kernels, fused_local(): pl.pallas_call(kernel, grid=(1,), in_specs=in_specs, out_specs=[block_spe...  8.61 us
    pallas_call x1, Pallas kernels, fused_local(): pl.pallas_call(make_second_half_kernel(last), grid=(1,), in_specs=[pl.Blo...  6.63 us
    pallas_call x1, Pallas kernels, fused_local(): pl.pallas_call(make_first_half_kernel(last), grid=(1,), in_specs=[half_sp...  5.97 us
    unnamed x17, local copies, waits for them, and re-layouts  1.87 us
  transfers between devices with their start and end apart: 9, of which 5 were waited for; matrix products, arithmetic and copies ran while one was open for 5% of the time, Pallas kernels for 33%

profile of v7, /device:TPU:0, one launch (start us, length us, event | category | flops | bytes accessed | tf_op | source)
XLA Modules:
  0.0 83.1 jit_solution(13538800877187215978)
XLA Ops:
  0.6 0.0 copy-start
  0.6 0.0 copy-start.4
  0.7 0.0 copy-start.1
  0.7 5.1 %collective-permute-start = (f32[1,512]{1,0:T(1,128)}, f32[1,512]{1,0:T(1,128)S(1)}, u32[]{:S(2)}, u32[]{:S(2)}) collective-permute-start(f32[1,512]{1,0:T(1,128)} %param.15), channel_id=1, source_target_pairs={{0,8},{8,16},{16,24},{1,9},{9,17},{17,25},{2,10},{10,18},{18,26},{... | collective-permute-start | bytes 6152 | tf_op jit(solution)/shard_map/ppermute | solution.py:16
  5.8 3.3 %collective-permute-start.2 = (f32[1,512]{1,0:T(1,128)}, f32[1,512]{1,0:T(1,128)S(1)}, u32[]{:S(2)}, u32[]{:S(2)}) collective-permute-start(f32[1,512]{1,0:T(1,128)} %param.15), channel_id=1, source_target_pairs={{0,24},{1,25},{2,26},{3,27},{4,28},{5,29},{6,30},{7,31}} | collective-permute-start | bytes 6152 | tf_op jit(solution)/shard_map/ppermute | solution.py:16
  9.1 1.8 %collective-permute-start.1 = (f32[1,512]{1,0:T(1,128)}, f32[1,512]{1,0:T(1,128)S(1)}, u32[]{:S(2)}, u32[]{:S(2)}) collective-permute-start(f32[1,512]{1,0:T(1,128)} %param.15), channel_id=1, source_target_pairs={{0,16},{8,24},{1,17},{9,25},{2,18},{10,26},{3,19},{11,27},{4,20},{... | collective-permute-start | bytes 6152 | tf_op jit(solution)/shard_map/ppermute | solution.py:16
  10.9 1.3 %slice.12 = bf16[1,2,1024,256]{3,2,1,0:T(8,128)(2,1)S(1)} slice(bf16[1,2,1024,512]{3,2,1,0:T(8,128)(2,1)} %param.9), slice={[0:1], [0:2], [0:1024], [0:256]} | slice | bytes 2097152 | tf_op jit(solution)/shard_map/slice | solution.py:443
  12.2 0.0 copy-start.5
  12.2 0.0 copy-start.3
  12.3 1.3 %collective-permute-start.3 = (bf16[1,2,1024,256]{3,2,1,0:T(8,128)(2,1)S(1)}, bf16[1,2,1024,256]{3,2,1,0:T(8,128)(2,1)S(1)}, u32[]{:S(2)}, u32[]{:S(2)}) collective-permute-start(bf16[1,2,1024,256]{3,2,1,0:T(8,128)(2,1)S(1)} %slice.12), channel_id=1, source_target_pairs={{8,0},{16,8},{24,16},{9,1},{17,9},{25,17},{10,2},{18,10},{26,18},{... | collective-permute-start | bytes 3145736 | tf_op jit(solution)/shard_map/ppermute | solution.py:16
  13.6 0.0 copy-done
  13.6 0.1 fusion.5
  13.6 1.3 %collective-permute-start.5 = (bf16[1,2,512,256]{3,2,1,0:T(8,128)(2,1)S(1)}, bf16[1,2,512,256]{3,2,1,0:T(8,128)(2,1)}, u32[]{:S(2)}, u32[]{:S(2)}) collective-permute-start(bf16[1,2,512,256]{3,2,1,0:T(8,128)(2,1)S(1)} %get-tuple-element.23), channel_id=1, source_target_pairs={{8,0},{16,8},{24,16},{9,1},{17,9},{25,17},{10,2},{18,10},{26,18},{... | collective-permute-start | bytes 1572872 | tf_op jit(solution)/shard_map/ppermute | solution.py:16
  15.0 0.0 copy-done.4
  15.0 0.1 pad.4.clone
  15.0 0.1 pad.5.clone
  15.1 0.0 copy-done.1
  15.1 0.8 %copy.15 = bf16[1,2,256,256]{2,3,1,0:T(8,128)(2,1)} copy(bf16[1,2,256,256]{3,2,1,0:T(8,128)(2,1)S(1)} %copy-done.1) | data formatting | bytes 524288 | tf_op args[4]
  16.0 1.0 %copy.16.limit_ref.limit_hbm = s32[1024,1]{1,0:T(8,128)} copy(s32[1024,1]{0,1:T(1,128)S(1)} %subtract_bitcast_fusion) | data formatting | bytes 8192 | tf_op jit(solution)/shard_map/sub | solution.py:457
  17.0 0.0 collective-permute-done
  17.0 1.3 %collective-permute-start.4 = (bf16[1,2,512,256]{3,2,1,0:T(8,128)(2,1)S(1)}, bf16[1,2,512,256]{3,2,1,0:T(8,128)(2,1)}, u32[]{:S(2)}, u32[]{:S(2)}) collective-permute-start(bf16[1,2,512,256]{3,2,1,0:T(8,128)(2,1)S(1)} %get-tuple-element.24), channel_id=1, source_target_pairs={{8,0},{16,8},{24,16},{9,1},{17,9},{25,17},{10,2},{18,10},{26,18},{... | collective-permute-start | bytes 1572872 | tf_op jit(solution)/shard_map/ppermute | solution.py:16
  18.3 0.0 collective-permute-done.2
  18.3 0.0 collective-permute-done.1
  18.3 0.0 copy-done.5
  18.3 0.0 copy-done.3
  18.5 0.7 maximum_maximum_fusion.trig_ref
  19.1 13.1 %shard_map.103 = bf16[1,2,1024,512]{3,2,1,0:T(8,128)(2,1)} custom-call(bf16[1,2,1024,512]{3,2,1,0:T(8,128)(2,1)} %source_hbm.1, f32[4,512]{1,0:T(4,128)} %maximum_maximum_fusion.trig_ref, s32[1024,1]{1,0:T(8,128)} %copy.16.limit_ref.limit_hbm, bf16[6,2,256,256]{3,2,1,0:T(8,128)(2,1)} %pade_hbm.1, bf16[2,256,256]{2,1,0:T(8,128)(2,1)} %bitcast.17), custom_call_target="tpu_custom_call" | custom-call | tf_op jit(solution)/shard_map/pallas_call | solution.py:465
  32.2 8.0 %collective-permute-done.3.arrival_ref = bf16[1,2,1024,256]{3,2,1,0:T(8,128)(2,1)S(1)} collective-permute-done((bf16[1,2,1024,256]{3,2,1,0:T(8,128)(2,1)S(1)}, bf16[1,2,1024,256]{3,2,1,0:T(8,128)(2,1)S(1)}, u32[]{:S(2)}, u32[]{:S(2)}) %collective-permute-start.3) | collective-permute-done | bytes 1048608 | tf_op jit(solution)/shard_map/ppermute | solution.py:16
  40.2 0.0 copy-start.2
  40.2 1.0 %copy-done.2 = bf16[1,2,1024,256]{3,2,1,0:T(8,128)(2,1)} copy-done((bf16[1,2,1024,256]{3,2,1,0:T(8,128)(2,1)}, bf16[1,2,1024,256]{3,2,1,0:T(8,128)(2,1)S(1)}, u32[]{:S(2)}) %copy-start.2) | copy-done | bytes 1048600
  41.2 8.6 %shard_map.104 = (bf16[1,2,1024,512]{3,2,1,0:T(8,128)(2,1)}, f32[1,256]{1,0:T(1,128)}) custom-call(bf16[1,2,1024,256]{3,2,1,0:T(8,128)(2,1)} %copy-done.2, bf16[1,2,1024,512]{3,2,1,0:T(8,128)(2,1)} %misfit_ref.5, bf16[1,2,1024,512]{3,2,1,0:T(8,128)(2,1)} %source_hbm.1, f32[4,512]{1,0:T(4,128)} %maximum_maximum_fusion.trig_ref, ...), custom_call_target="tpu_custom_call" | custom-call | tf_op jit(solution)/shard_map/pallas_call | solution.py:496
  49.8 11.3 %collective-permute-done.4.arrival_ref = bf16[1,2,512,256]{3,2,1,0:T(8,128)(2,1)} collective-permute-done((bf16[1,2,512,256]{3,2,1,0:T(8,128)(2,1)S(1)}, bf16[1,2,512,256]{3,2,1,0:T(8,128)(2,1)}, u32[]{:S(2)}, u32[]{:S(2)}) %collective-permute-start.4) | collective-permute-done | bytes 524320 | tf_op jit(solution)/shard_map/ppermute | solution.py:16
  61.1 6.0 %shard_map.105 = (bf16[1,2,1024,512]{3,2,1,0:T(8,128)(2,1)}, f32[1,256]{1,0:T(1,128)}, f32[4,16,256]{2,1,0:T(8,128)}) custom-call(bf16[1,2,512,256]{3,2,1,0:T(8,128)(2,1)} %collective-permute-done.4.arrival_ref, bf16[1,2,1024,512]{3,2,1,0:T(8,128)(2,1)} %misfit_ref.5, bf16[1,2,1024,512]{3,2,1,0:T(8,128)(2,1)} %source_hbm.1, ...), custom_call_target="tpu_custom_call", output_to_operand_aliasing={{0}: (7, {})} | custom-call | tf_op jit(solution)/shard_map/pallas_call | solution.py:519
  67.0 0.0 collective-permute-done.5.arrival_ref
  67.1 0.0 copy-start.6
  67.1 0.0 copy-start.7
  67.1 6.6 %shard_map.106 = (bf16[1,2,1024,512]{3,2,1,0:T(8,128)(2,1)}, f32[1,256]{1,0:T(1,128)}) custom-call(f32[4,16,256]{2,1,0:T(8,128)} %get-tuple-element.15.halo_ref, bf16[1,2,512,256]{3,2,1,0:T(8,128)(2,1)} %collective-permute-done.5.arrival_ref, bf16[1,2,1024,512]{3,2,1,0:T(8,128)(2,1)} %misfit_ref.5, ...), custom_call_target="tpu_custom_call", output_to_operand_aliasing={{0}: (8, {})} | custom-call | tf_op jit(solution)/shard_map/pallas_call | solution.py:543
  73.7 0.0 copy-done.6
  73.7 0.7 add.29
  74.4 0.0 copy-done.7
  74.4 1.3 %collective-permute-start.8 = (f32[1,512]{1,0:T(1,128)S(1)}, f32[1,512]{1,0:T(1,128)S(1)}, u32[]{:S(2)}, u32[]{:S(2)}) collective-permute-start(f32[1,512]{1,0:T(1,128)S(1)} %bitcast.20), channel_id=1, source_target_pairs={{24,0},{25,1},{26,2},{27,3},{28,4},{29,5},{30,6},{31,7}} | collective-permute-start | bytes 6152 | tf_op jit(solution)/shard_map/ppermute | solution.py:16
  75.7 1.3 %collective-permute-start.7 = (f32[1,512]{1,0:T(1,128)S(1)}, f32[1,512]{1,0:T(1,128)S(1)}, u32[]{:S(2)}, u32[]{:S(2)}) collective-permute-start(f32[1,512]{1,0:T(1,128)S(1)} %bitcast.21), channel_id=1, source_target_pairs={{16,0},{24,8},{17,1},{25,9},{18,2},{26,10},{19,3},{27,11},{20,4},{... | collective-permute-start | bytes 6152 | tf_op jit(solution)/shard_map/ppermute | solution.py:16
  77.0 1.3 %collective-permute-start.6 = (f32[1,512]{1,0:T(1,128)S(1)}, f32[1,512]{1,0:T(1,128)S(1)}, u32[]{:S(2)}, u32[]{:S(2)}) collective-permute-start(f32[1,512]{1,0:T(1,128)S(1)} %bitcast.22), channel_id=1, source_target_pairs={{8,0},{16,8},{24,16},{9,1},{17,9},{25,17},{10,2},{18,10},{26,18},{... | collective-permute-start | bytes 6152 | tf_op jit(solution)/shard_map/ppermute | solution.py:16
  78.3 3.4 %collective-permute-done.8 = f32[1,512]{1,0:T(1,128)S(1)} collective-permute-done((f32[1,512]{1,0:T(1,128)S(1)}, f32[1,512]{1,0:T(1,128)S(1)}, u32[]{:S(2)}, u32[]{:S(2)}) %collective-permute-start.8) | collective-permute-done | bytes 2080 | tf_op jit(solution)/shard_map/ppermute | solution.py:16
  81.7 0.4 collective-permute-done.7
  82.1 0.4 collective-permute-done.6
  82.5 0.6 add_add_fusion
  (5 shorter events, 0.1 us)
Async XLA Ops:
  0.6 12.9 %copy-start = (bf16[1,2,1024,512]{3,2,1,0:T(8,128)(2,1)S(1)}, bf16[1,2,1024,512]{3,2,1,0:T(8,128)(2,1)}, u32[]{:S(2)}) copy-start(bf16[1,2,1024,512]{3,2,1,0:T(8,128)(2,1)} %param.9) | copy-start | bytes 6291460
  0.6 14.3 %copy-start.4 = (s32[1,1024]{1,0:T(1,128)S(1)}, s32[1,1024]{1,0:T(1,128)}, u32[]{:S(2)}) copy-start(s32[1,1024]{1,0:T(1,128)} %param.13) | copy-start | bytes 12292
  0.7 14.5 %copy-start.1 = (bf16[1,2,256,256]{3,2,1,0:T(8,128)(2,1)S(1)}, bf16[1,2,256,256]{3,2,1,0:T(8,128)(2,1)}, u32[]{:S(2)}) copy-start(bf16[1,2,256,256]{3,2,1,0:T(8,128)(2,1)} %param.12) | copy-start | bytes 786436
  0.7 16.3 %collective-permute-start = (f32[1,512]{1,0:T(1,128)}, f32[1,512]{1,0:T(1,128)S(1)}, u32[]{:S(2)}, u32[]{:S(2)}) collective-permute-start(f32[1,512]{1,0:T(1,128)} %param.15), channel_id=1, source_target_pairs={{0,8},{8,16},{16,24},{1,9},{9,17},{17,25},{2,10},{10,18},{18,26},{... | collective-permute-start | bytes 6152 | tf_op jit(solution)/shard_map/ppermute | solution.py:16
  5.8 12.5 %collective-permute-start.2 = (f32[1,512]{1,0:T(1,128)}, f32[1,512]{1,0:T(1,128)S(1)}, u32[]{:S(2)}, u32[]{:S(2)}) collective-permute-start(f32[1,512]{1,0:T(1,128)} %param.15), channel_id=1, source_target_pairs={{0,24},{1,25},{2,26},{3,27},{4,28},{5,29},{6,30},{7,31}} | collective-permute-start | bytes 6152 | tf_op jit(solution)/shard_map/ppermute | solution.py:16
  9.1 9.2 %collective-permute-start.1 = (f32[1,512]{1,0:T(1,128)}, f32[1,512]{1,0:T(1,128)S(1)}, u32[]{:S(2)}, u32[]{:S(2)}) collective-permute-start(f32[1,512]{1,0:T(1,128)} %param.15), channel_id=1, source_target_pairs={{0,16},{8,24},{1,17},{9,25},{2,18},{10,26},{3,19},{11,27},{4,20},{... | collective-permute-start | bytes 6152 | tf_op jit(solution)/shard_map/ppermute | solution.py:16
  12.2 6.1 %copy-start.5 = (f32[1,512]{1,0:T(1,128)S(1)}, f32[1,512]{1,0:T(1,128)}, u32[]{:S(2)}) copy-start(f32[1,512]{1,0:T(1,128)} %param.15) | copy-start | bytes 6148
  12.2 6.1 %copy-start.3 = (f32[512]{0:T(512)S(1)}, f32[512]{0:T(512)}, u32[]{:S(2)}) copy-start(f32[512]{0:T(512)} %param.14) | copy-start | bytes 6148
  12.3 27.9 %collective-permute-start.3 = (bf16[1,2,1024,256]{3,2,1,0:T(8,128)(2,1)S(1)}, bf16[1,2,1024,256]{3,2,1,0:T(8,128)(2,1)S(1)}, u32[]{:S(2)}, u32[]{:S(2)}) collective-permute-start(bf16[1,2,1024,256]{3,2,1,0:T(8,128)(2,1)S(1)} %slice.12), channel_id=1, source_target_pairs={{8,0},{16,8},{24,16},{9,1},{17,9},{25,17},{10,2},{18,10},{26,18},{... | collective-permute-start | bytes 3145736 | tf_op jit(solution)/shard_map/ppermute | solution.py:16
  13.6 53.4 %collective-permute-start.5 = (bf16[1,2,512,256]{3,2,1,0:T(8,128)(2,1)S(1)}, bf16[1,2,512,256]{3,2,1,0:T(8,128)(2,1)}, u32[]{:S(2)}, u32[]{:S(2)}) collective-permute-start(bf16[1,2,512,256]{3,2,1,0:T(8,128)(2,1)S(1)} %get-tuple-element.23), channel_id=1, source_target_pairs={{8,0},{16,8},{24,16},{9,1},{17,9},{25,17},{10,2},{18,10},{26,18},{... | collective-permute-start | bytes 1572872 | tf_op jit(solution)/shard_map/ppermute | solution.py:16
  17.0 44.1 %collective-permute-start.4 = (bf16[1,2,512,256]{3,2,1,0:T(8,128)(2,1)S(1)}, bf16[1,2,512,256]{3,2,1,0:T(8,128)(2,1)}, u32[]{:S(2)}, u32[]{:S(2)}) collective-permute-start(bf16[1,2,512,256]{3,2,1,0:T(8,128)(2,1)S(1)} %get-tuple-element.24), channel_id=1, source_target_pairs={{8,0},{16,8},{24,16},{9,1},{17,9},{25,17},{10,2},{18,10},{26,18},{... | collective-permute-start | bytes 1572872 | tf_op jit(solution)/shard_map/ppermute | solution.py:16
  40.2 1.0 %copy-start.2 = (bf16[1,2,1024,256]{3,2,1,0:T(8,128)(2,1)}, bf16[1,2,1024,256]{3,2,1,0:T(8,128)(2,1)S(1)}, u32[]{:S(2)}) copy-start(bf16[1,2,1024,256]{3,2,1,0:T(8,128)(2,1)S(1)} %collective-permute-done.3.arrival_ref) | copy-start | bytes 3145732
  67.1 6.7 %copy-start.6 = (f32[1,256]{1,0:T(1,128)S(1)}, f32[1,256]{1,0:T(1,128)}, u32[]{:S(2)}) copy-start(f32[1,256]{1,0:T(1,128)} %get-tuple-element.19) | copy-start | bytes 3076
  67.1 7.3 %copy-start.7 = (f32[1,256]{1,0:T(1,128)S(1)}, f32[1,256]{1,0:T(1,128)}, u32[]{:S(2)}) copy-start(f32[1,256]{1,0:T(1,128)} %get-tuple-element.18) | copy-start | bytes 3076
  74.4 7.3 %collective-permute-start.8 = (f32[1,512]{1,0:T(1,128)S(1)}, f32[1,512]{1,0:T(1,128)S(1)}, u32[]{:S(2)}, u32[]{:S(2)}) collective-permute-start(f32[1,512]{1,0:T(1,128)S(1)} %bitcast.20), channel_id=1, source_target_pairs={{24,0},{25,1},{26,2},{27,3},{28,4},{29,5},{30,6},{31,7}} | collective-permute-start | bytes 6152 | tf_op jit(solution)/shard_map/ppermute | solution.py:16
  75.7 6.4 %collective-permute-start.7 = (f32[1,512]{1,0:T(1,128)S(1)}, f32[1,512]{1,0:T(1,128)S(1)}, u32[]{:S(2)}, u32[]{:S(2)}) collective-permute-start(f32[1,512]{1,0:T(1,128)S(1)} %bitcast.21), channel_id=1, source_target_pairs={{16,0},{24,8},{17,1},{25,9},{18,2},{26,10},{19,3},{27,11},{20,4},{... | collective-permute-start | bytes 6152 | tf_op jit(solution)/shard_map/ppermute | solution.py:16
  77.0 5.5 %collective-permute-start.6 = (f32[1,512]{1,0:T(1,128)S(1)}, f32[1,512]{1,0:T(1,128)S(1)}, u32[]{:S(2)}, u32[]{:S(2)}) collective-permute-start(f32[1,512]{1,0:T(1,128)S(1)} %bitcast.22), channel_id=1, source_target_pairs={{8,0},{16,8},{24,16},{9,1},{17,9},{25,17},{10,2},{18,10},{26,18},{... | collective-permute-start | bytes 6152 | tf_op jit(solution)/shard_map/ppermute | solution.py:16
